TPU v7x, 32 devices: a whole 2x2x4 slice. The times are simulated.
32 devices in a mesh: seq: 4 (over y, x), dp: 8 (over z, core).
Axes of the slice: x: 2, y: 2, z: 4, core: 2. Of those that a mesh axis runs over, the one named last changes fastest.
Arguments:
- queries: bfloat16 [8, 512, 4096], P('dp', 'seq'), may hold values from -6 to 6
- keys: bfloat16 [8, 512, 4096], P('dp', 'seq'), may hold values from -6 to 6
- values: bfloat16 [8, 512, 4096], P('dp', 'seq'), may hold values from -6 to 6
- cotangent: bfloat16 [8, 512, 4096], P('dp', 'seq'), may hold values from -6 to 6
- taps: float32 [3, 7, 4096], replicated, may hold values from -2 to 2
- residue: float32 [16, 4096], replicated, may hold values from -0.12 to 0.12
- skip: float32 [4096], replicated, may hold values from 0.5 to 1.5
- decay: float32 [16, 4096], replicated, may hold values from 0.0001953125 to 0.06
Outputs:
- mixed: bfloat16 [8, 512, 4096], P('dp', 'seq')
- grad_queries: bfloat16 [8, 512, 4096], P('dp', 'seq')
- grad_keys: bfloat16 [8, 512, 4096], P('dp', 'seq')
- grad_values: bfloat16 [8, 512, 4096], P('dp', 'seq')
- grad_taps: float32 [3, 7, 4096], replicated
- grad_residue: float32 [16, 4096], replicated
- grad_skip: float32 [4096], replicated
All inputs are finite; a program needn't handle non-finite values.
Results may differ from a plain program's by a relative error of at most 0.001.
Values may be sent and summed in bfloat16 or wider, within the bound.
No kernel may reach another device: no remote copies, remote signals or barrier semaphores. Data moves between devices by JAX's collectives and lax.ppermute only.
A program may use at most 256 MiB of HBM per device.

v0:
```python
import jax
import jax.numpy as jnp
from jax import lax
from jax.sharding import PartitionSpec as P

BLOCK = 16


def passed_along(x, axis, by):
    count = lax.axis_size(axis)
    pairs = [(i, i + by) for i in range(count) if 0 <= i + by < count]
    return lax.ppermute(x, axis, pairs)


def carried_in(value, axis, join, neutral, backward):
    count, mine = (lax.axis_size(axis), lax.axis_index(axis))
    pieces = jax.tree.map(lambda part: lax.all_gather(part, axis), value)
    if backward:
        pieces = jax.tree.map(lambda part: part[::-1], pieces)
        mine = count - 1 - mine
    total = jax.tree.map(
        lambda part, zero: jnp.full_like(part, 0) + jnp.asarray(zero, part.dtype), value, neutral
    )

    def lap(position, total):
        longer = join(total, jax.tree.map(lambda part: part[position], pieces))
        return jax.tree.map(lambda new, old: jnp.where(position < mine, new, old), longer, total)

    return lax.fori_loop(0, count - 1, lap, total)


def make_tables(decay, residue, width):
    steps = jnp.arange(width).astype(decay.dtype)
    power = jnp.exp(-decay[None] * steps[:, None, None])
    lag_filter = jnp.sum(power * residue[None], 1)
    ahead = jnp.arange(width)[:, None] - jnp.arange(width)[None, :]
    onehot = (ahead[:, :, None] == jnp.arange(width)[None, None, :]).astype(decay.dtype)
    toeplitz = jnp.sum(onehot[:, :, :, None] * lag_filter[None, None], 2)
    tail = power[::-1]
    decayed = power * jnp.exp(-decay)[None]
    head = decayed * residue[None]
    jump = jnp.exp(-decay * width)
    return (power, onehot, toeplitz, tail, decayed, head, jump)


def block_ends(stacked, tail):
    return jnp.sum(stacked[:, :, None, :] * tail[None], 1)


def chain(ends, start, jump):

    def advance(state, end):
        return (jump * state + end, state)

    final, starts = lax.scan(advance, start, ends)
    return (starts, final)


def convolve(stacked, starts, toeplitz, head):
    inner = jnp.sum(stacked[:, None] * toeplitz[None], 2)
    return inner + jnp.sum(starts[:, None] * head[None], 2)


def featurize(padded, weights):
    margin = weights.shape[0] - 1
    count = padded.shape[0] - margin
    total = jnp.zeros_like(padded[:count])
    for lag in range(weights.shape[0]):
        total = total + weights[lag] * padded[margin - lag : margin - lag + count]
    return total


def transpose_taps(padded, weights):
    margin = weights.shape[0] - 1
    count = padded.shape[0] - margin
    total = jnp.zeros_like(padded[:count])
    for lag in range(weights.shape[0]):
        total = total + weights[lag] * padded[lag : lag + count]
    return total


def tap_terms(adjoint, padded, count_taps):
    margin = count_taps - 1
    rows = adjoint.shape[0]
    windows = jnp.stack(
        [padded[margin - lag : margin - lag + rows] for lag in range(count_taps)], 0
    )
    return jnp.sum(adjoint[None] * windows, 1)


def compose(earlier, later):
    return (earlier[0] * later[0], later[0] * earlier[1] + later[1])


def per_device(queries, keys, values, cotangent, taps, residue, skip, decay):
    rows = queries.shape[1]
    width = queries.shape[2]
    count_taps = taps.shape[1]
    margin = count_taps - 1
    blocks = rows // BLOCK
    own = (queries[0], keys[0], values[0])
    rim = passed_along(
        (own[0][rows - margin :], own[1][rows - margin :], own[2][rows - margin :]), "seq", 1
    )
    padded = [jnp.concatenate([rim[idx], own[idx]], 0).astype(jnp.float32) for idx in range(3)]
    feats = [featurize(padded[idx], taps[idx]) for idx in range(3)]
    product = feats[1] * feats[2]
    power, onehot, toeplitz, tail, decayed, head, jump = make_tables(decay, residue, BLOCK)
    whole_jump = jnp.exp(-decay * rows)
    block_steps = (jnp.arange(blocks) * BLOCK).astype(decay.dtype)
    offsets = jnp.exp(-decay[None] * block_steps[:, None, None])
    identity = (jnp.ones_like(jump), jnp.zeros_like(jump))
    stacked = product.reshape(blocks, BLOCK, width)
    ends = block_ends(stacked, tail)
    local_starts, local_final = chain(ends, jnp.zeros_like(jump), jump)
    incoming = carried_in((whole_jump, local_final), "seq", compose, identity, False)[1]
    starts = local_starts + offsets * incoming[None]
    conv_out = convolve(stacked, starts, toeplitz, head).reshape(rows, width) + skip * product
    mixed = (feats[0] * conv_out).astype(jnp.bfloat16)
    grad = cotangent[0].astype(jnp.float32)
    adj_q = grad * conv_out
    adj_z = grad * feats[0]
    flipped = adj_z[::-1].reshape(blocks, BLOCK, width)
    back_ends = block_ends(flipped, tail)
    local_back, back_final = chain(back_ends, jnp.zeros_like(jump), jump)
    back_in = carried_in((whole_jump, back_final), "seq", compose, identity, True)[1]
    back_starts = local_back + offsets * back_in[None]
    adj_u = convolve(flipped, back_starts, toeplitz, head).reshape(rows, width)[::-1] + skip * adj_z
    adj_k = adj_u * feats[2]
    adj_v = adj_u * feats[1]
    adjoints = (adj_q, adj_k, adj_v)
    after = passed_along((adj_q[:margin], adj_k[:margin], adj_v[:margin]), "seq", -1)
    grad_streams = [
        transpose_taps(jnp.concatenate([adjoints[idx], after[idx]], 0), taps[idx]).astype(
            jnp.bfloat16
        )[None]
        for idx in range(3)
    ]
    tap_grad = jnp.stack([tap_terms(adjoints[idx], padded[idx], count_taps) for idx in range(3)], 0)
    adj_blocks = adj_z.reshape(blocks, BLOCK, width)
    state_part = jnp.sum(jnp.sum(adj_blocks[:, :, None, :] * decayed[None], 1) * starts, 0)
    pairs = jnp.sum(adj_blocks[:, :, None, :] * stacked[:, None], 0)
    lag_sums = jnp.sum(pairs[:, :, None, :] * onehot[:, :, :, None], (0, 1))
    local_part = jnp.sum(lag_sums[:, None, :] * power, 0)
    residue_grad = state_part + local_part
    skip_grad = jnp.sum(adj_z * product, 0)
    shares = (
        lax.psum_scatter(tap_grad, "seq", scatter_dimension=2, tiled=True),
        lax.psum_scatter(residue_grad, "seq", scatter_dimension=1, tiled=True),
        lax.psum_scatter(skip_grad, "seq", scatter_dimension=0, tiled=True),
    )
    totals = lax.psum((shares[0], shares[1], shares[2]), "dp")
    summed = (
        lax.all_gather(totals[0], "seq", axis=2, tiled=True),
        lax.all_gather(totals[1], "seq", axis=1, tiled=True),
        lax.all_gather(totals[2], "seq", axis=0, tiled=True),
    )
    return (
        mixed[None],
        grad_streams[0],
        grad_streams[1],
        grad_streams[2],
        summed[0],
        summed[1],
        summed[2],
    )


def solution(mesh):
    return jax.shard_map(
        per_device,
        mesh=mesh,
        in_specs=(
            P("dp", "seq", None),
            P("dp", "seq", None),
            P("dp", "seq", None),
            P("dp", "seq", None),
            P(),
            P(),
            P(),
            P(),
        ),
        out_specs=(
            P("dp", "seq", None),
            P("dp", "seq", None),
            P("dp", "seq", None),
            P("dp", "seq", None),
            P(),
            P(),
            P(),
        ),
        check_vma=False,
    )
```

profile of v0, /device:TPU:0, one launch (start us, length us, event | category | flops | bytes accessed | tf_op | source)
XLA Modules:
  0.0 475.7 jit_solution(10176977647038046650)
XLA Ops:
  8.2 4.9 %collective-permute-start.2 = (bf16[6,4096]{1,0:T(8,128)(2,1)S(1)}, bf16[6,4096]{1,0:T(8,128)(2,1)S(1)}, u32[]{:S(2)}, u32[]{:S(2)}) collective-permute-start(bf16[6,4096]{1,0:T(8,128)(2,1)S(1)} %slice_bitcast_fusion), channel_id=1, source_target_pairs={{0,8},{8,16},{16,24},{1,9},{9,17},{17,25},{2,10},{10,18},{18,26},{... | collective-permute-start | bytes 147464 | tf_op jit(solution)/shard_map/ppermute | solution.py:12
  26.1 6.1 %broadcast_multiply_fusion = (f32[16,16,4096]{2,1,0:T(8,128)}, f32[16,16,4096]{2,1,0:T(8,128)}, f32[16,4096]{1,0:T(8,128)S(1)}, f32[16,16,4096]{2,1,0:T(8,128)}) fusion(f32[16,4096]{1,0:T(8,128)S(1)} %copy-done.24, f32[16,4096]{1,0:T(8,128)S(1)} %get-tuple-element.421, f32[16]{0:T(128)S(1)} %iota_convert_fusion, f32[16,4096]{1,0:T(8,128)S(1)} %get-tuple-element.422), kind=kLoop, calls=%fused_computation.139 | loop fusion | flops 5177344 | bytes 13631552 | tf_op jit(solution)/shard_map/mul | solution.py:41
  32.2 30.0 %multiply_reduce_fusion.1 = f32[16,16,4096]{2,1,0:T(8,128)} fusion(f32[16,4096]{1,0:T(8,128)S(1)} %get-tuple-element.395, f32[16,16,16]{2,1,0:T(8,128)S(1)} %fusion.63), kind=kLoop, calls=%fused_computation.11 | loop fusion | flops 32505856 | bytes 4472832 | tf_op jit(solution)/shard_map/reduce_sum | solution.py:38
  76.9 17.4 %multiply_reduce_fusion.15 = (f32[4096]{0:T(1024)}, f32[128,4096]{1,0:T(8,128)}, f32[128,4096]{1,0:T(8,128)}, f32[128,4096]{1,0:T(8,128)}, f32[128,4096]{1,0:T(8,128)}, /*index=5*/f32[128,4096]{1,0:T(8,128)}) fusion(bf16[1,128,4096]{2,1,0:T(8,128)(2,1)} %param.19, f32[134,4096]{1,0:T(8,128)} %copy-done.2, f32[4096]{0:T(1024)} %bitcast.196, ...), kind=kLoop, calls=%fused_computation.132 | loop fusion | flops 23064576 | bytes 55934976 | tf_op jit(solution)/shard_map/reduce_sum | solution.py:146
  94.3 16.8 %rev.16 = f32[128,4096]{1,0:T(8,128)} reverse(f32[128,4096]{1,0:T(8,128)} %get-tuple-element.382), dimensions={0} | reverse | bytes 4194304 | tf_op jit(solution)/shard_map/rev | solution.py:123
  111.1 33.7 %multiply_reduce_fusion.6 = (f32[8,16,4096]{2,1,0:T(8,128)}, f32[8,16,4096]{2,1,0:T(8,128)}, f32[8,16,4096]{2,1,0:T(8,128)}, f32[8,16,4096]{2,1,0:T(8,128)}, f32[16,16,4096]{2,1,0:T(8,128)}, /*index=5*/f32[8,16,4096]{2,1,0:T(8,128)}) fusion(f32[8,16,4096]{2,1,0:T(8,128)} %bitcast.144, f32[16,16,4096]{2,1,0:T(8,128)} %multiply_reduce_fusion.1, ...), kind=kLoop, calls=%fused_computation.16 | loop fusion | flops 96993280 | bytes 33554432 | tf_op jit(solution)/shard_map/reduce_sum | solution.py:60
  146.3 14.8 %while.54 = (s32[]{:T(128)}, f32[16,4096]{1,0:T(8,128)S(1)}, f32[8,16,4096]{2,1,0:T(8,128)}, f32[16,4096]{1,0:T(8,128)S(1)}, f32[8,16,4096]{2,1,0:T(8,128)}, /*index=5*/s32[]{:T(128)}, s32[]{:T(128)}) while((s32[]{:T(128)}, f32[16,4096]{1,0:T(8,128)S(1)}, f32[8,16,4096]{2,1,0:T(8,128)}, f32[16,4096]{1,0:T(8,128)S(1)}, ...), condition=%wide.region_5.6_spmd.clone, body=%wide.region_4.5_spmd.clone.sunk | while | flops 262147 | bytes 1572968 | solution.py:55
  162.7 15.1 %while.56 = (s32[]{:T(128)}, f32[16,4096]{1,0:T(8,128)S(1)}, f32[8,16,4096]{2,1,0:T(8,128)}, f32[16,4096]{1,0:T(8,128)S(1)}, f32[8,16,4096]{2,1,0:T(8,128)}, /*index=5*/s32[]{:T(128)}, s32[]{:T(128)}) while((s32[]{:T(128)}, f32[16,4096]{1,0:T(8,128)S(1)}, f32[8,16,4096]{2,1,0:T(8,128)}, f32[16,4096]{1,0:T(8,128)S(1)}, ...), condition=%wide.region_12.13_spmd.clone, body=%wide.region_11.12_spmd.clone.sunk | while | flops 262147 | bytes 1572968 | solution.py:55
  205.9 6.6 %multiply_reduce_fusion = f32[16,4096]{1,0:T(8,128)S(1)} fusion(f32[16,16,4096]{2,1,0:T(8,128)S(1)} %copy-done.9, f32[16,16,16]{2,1,0:T(8,128)S(1)} %copy-done.21), kind=kLoop, calls=%fused_computation.10 | loop fusion | flops 33488896 | bytes 4472832 | tf_op jit(solution)/shard_map/reduce_sum | solution.py:143
  214.2 13.9 %all-reduce = f32[4096]{0:T(1024)S(1)} all-reduce(f32[4096]{0:T(1024)S(1)} %copy-done.45), channel_id=7, replica_groups=mesh['seq'=4,'dp'=8] {'seq'}, use_global_device_ids=true, to_apply=%region_29.30.clone | all-reduce | flops 4096 | bytes 32768
  228.1 13.6 %psum.23 = f32[1024]{0:T(1024)S(1)} all-reduce(f32[1024]{0:T(1024)S(1)} %dynamic-slice.1), channel_id=1, replica_groups=mesh['seq'=4,'dp'=8] {'dp'}, use_global_device_ids=true, to_apply=%region_30.31 | all-reduce | flops 1024 | bytes 8192 | tf_op jit(solution)/shard_map/psum | solution.py:152
  241.7 8.6 %all_gather.37 = f32[4096]{0:T(1024)} all-gather(f32[1024]{0:T(1024)S(1)} %psum.23), channel_id=1, replica_groups=mesh['seq'=4,'dp'=8] {'seq'}, dimensions={0}, use_global_device_ids=true | all-gather | bytes 20480 | tf_op jit(solution)/shard_map/all_gather | solution.py:156
  261.8 15.5 %all-gather.9.cloned.1.call-done = f32[64,4096]{1,0:T(8,128)} async-done(((f32[16,4096]{1,0:T(8,128)}), f32[64,4096]{1,0:T(8,128)}) %all-gather.9.cloned.1.call-update) | async-done | bytes 1048592 | tf_op jit(solution)/shard_map/all_gather | solution.py:17
  285.0 19.6 %multiply_reduce_fusion.4 = (f32[8,16,4096]{2,1,0:T(8,128)S(1)}, f32[8,16,4096]{2,1,0:T(8,128)}) fusion(f32[8,16,4096]{2,1,0:T(8,128)S(1)} %get-tuple-element.417, f32[16,16,4096]{2,1,0:T(8,128)S(1)} %copy-done.10, f32[8,16,4096]{2,1,0:T(8,128)S(1)} %get-tuple-element.388), kind=kLoop, calls=%fused_computation.14 | loop fusion | flops 32505856 | bytes 12582912 | tf_op jit(solution)/shard_map/reduce_sum | solution.py:61
  306.2 16.9 %rev.19 = f32[128,4096]{1,0:T(8,128)} reverse(f32[128,4096]{1,0:T(8,128)} %bitcast.145), dimensions={0} | reverse | bytes 4194304 | tf_op jit(solution)/shard_map/rev | solution.py:128
  326.6 7.5 %fusion.61 = (f32[128,4096]{1,0:T(8,128)S(1)}, f32[128,4096]{1,0:T(8,128)S(1)}, bf16[1,128,4096]{2,1,0:T(8,128)(2,1)}, f32[128,4096]{1,0:T(8,128)}) fusion(f32[128,4096]{1,0:T(8,128)} %get-tuple-element.385, f32[128,4096]{1,0:T(8,128)} %rev.19, f32[128,4096]{1,0:T(8,128)S(1)} %copy-done.4, f32[4096]{0:T(1024)S(1)} %copy-done.48, ...), kind=kLoop, calls=%fused_computation.150 | loop fusion | flops 5242880 | bytes 23085056 | tf_op jit(solution)/shard_map/mul | solution.py:130
  342.0 11.8 %multiply_reduce_fusion.10 = (f32[7,4096]{1,0:T(8,128)S(1)}, f32[7,4096]{1,0:T(8,128)S(1)}) fusion(f32[7,128,4096]{2,1,0:T(8,128)} %bitcast_dynamic-update-slice_fusion.2, f32[128,4096]{1,0:T(8,128)} %copy-done.8, f32[7,128,4096]{2,1,0:T(8,128)} %bitcast_dynamic-update-slice_fusion.9, f32[128,4096]{1,0:T(8,128)S(1)} %get-tuple-element.390), kind=kLoop, calls=%fused_computation.20 | loop fusion | flops 14622720 | bytes 33783808 | tf_op jit(solution)/shard_map/reduce_sum | solution.py:88
  353.9 8.0 %multiply_reduce_fusion.12 = f32[7,4096]{1,0:T(8,128)S(1)} fusion(f32[7,128,4096]{2,1,0:T(8,128)} %bitcast_dynamic-update-slice_fusion.16, f32[128,4096]{1,0:T(8,128)} %get-tuple-element.424), kind=kLoop, calls=%fused_computation.22 | loop fusion | flops 7311360 | bytes 16891904 | tf_op jit(solution)/shard_map/reduce_sum | solution.py:88
  362.9 8.3 %fusion.60 = bf16[1,128,4096]{2,1,0:T(8,128)(2,1)} fusion(f32[6,4096]{1,0:T(8,128)S(1)} %collective-permute-done.5, f32[128,4096]{1,0:T(8,128)} %copy-done.8, f32[4096]{0:T(1024)S(1)} %bitcast.197, f32[4096]{0:T(1024)S(1)} %bitcast.195, f32[4096]{0:T(1024)S(1)} %bitcast.185, f32[4096]{0:T(1024)S(1)} %bitcast.187, f32[4096]{0:T(1024)S(1)} %bitcast.189, ...), kind=kLoop, calls=%fused_computation.149 | loop fusion | flops 10485760 | bytes 3358720 | tf_op jit(solution)/shard_map/broadcast_in_dim | solution.py:134
  374.3 18.7 %reduce-scatter.3.cloned.1.call-done = f32[3,7,1024]{2,1,0:T(8,128)} async-done(((f32[3,7,4096]{2,1,0:T(8,128)}), f32[3,7,1024]{2,1,0:T(8,128)}) %reduce-scatter.3.cloned.1.call-update) | async-done | bytes 86032 | tf_op jit(solution)/shard_map/reduce_scatter | solution.py:148
  393.1 8.6 %fusion.58 = bf16[1,128,4096]{2,1,0:T(8,128)(2,1)} fusion(f32[6,4096]{1,0:T(8,128)S(1)} %collective-permute-done.3, f32[128,4096]{1,0:T(8,128)} %get-tuple-element.424, f32[4096]{0:T(1024)S(1)} %bitcast.159, f32[4096]{0:T(1024)S(1)} %bitcast.161, f32[4096]{0:T(1024)S(1)} %bitcast.163, f32[4096]{0:T(1024)S(1)} %bitcast.165, f32[4096]{0:T(1024)S(1)} %bitcast.167, ...), kind=kLoop, calls=%fused_computation.147 | loop fusion | flops 10485760 | bytes 3358720 | tf_op jit(solution)/shard_map/broadcast_in_dim | solution.py:134
  401.7 46.3 %all-reduce.4.cloned.1.call-done = (f32[3,7,1024]{2,1,0:T(8,128)}, f32[16,1024]{1,0:T(8,128)}) async-done(((f32[3,7,1024]{2,1,0:T(8,128)}, f32[16,1024]{1,0:T(8,128)}), (f32[3,7,1024]{2,1,0:T(8,128)}, f32[16,1024]{1,0:T(8,128)})) %all-reduce.4.cloned.1.call-update) | async-done | bytes 151568 | tf_op jit(solution)/shard_map/psum | solution.py:152
  448.1 9.2 %all_gather.36 = f32[16,4096]{1,0:T(8,128)S(1)} all-gather(f32[16,1024]{1,0:T(8,128)} %get-tuple-element.380), channel_id=1, replica_groups=mesh['seq'=4,'dp'=8] {'seq'}, dimensions={1}, use_global_device_ids=true | all-gather | bytes 327680 | tf_op jit(solution)/shard_map/all_gather | solution.py:155
  457.2 9.6 %all_gather.35 = f32[3,7,4096]{2,1,0:T(8,128)S(1)} all-gather(f32[3,7,1024]{2,1,0:T(8,128)} %get-tuple-element.379), channel_id=1, replica_groups=mesh['seq'=4,'dp'=8] {'seq'}, dimensions={2}, use_global_device_ids=true | all-gather | bytes 430080 | tf_op jit(solution)/shard_map/all_gather | solution.py:154
  (230 shorter events, 135.9 us)
Async XLA Ops:
  7.2 18.9 %copy-start.24 = (f32[16,4096]{1,0:T(8,128)S(1)}, f32[16,4096]{1,0:T(8,128)}, u32[]{:S(2)}) copy-start(f32[16,4096]{1,0:T(8,128)} %param.21) | copy-start | bytes 786436
  7.2 246.1 %all-gather.7.cloned.1.call-start = ((), (), s32[]{:S(2)}) async-start(), calls=%async_computation.4 | async-start | bytes 1310720 | tf_op jit(solution)/shard_map/all_gather | solution.py:17
  8.2 60.7 %collective-permute-start.2 = (bf16[6,4096]{1,0:T(8,128)(2,1)S(1)}, bf16[6,4096]{1,0:T(8,128)(2,1)S(1)}, u32[]{:S(2)}, u32[]{:S(2)}) collective-permute-start(bf16[6,4096]{1,0:T(8,128)(2,1)S(1)} %slice_bitcast_fusion), channel_id=1, source_target_pairs={{0,8},{8,16},{16,24},{1,9},{9,17},{17,25},{2,10},{10,18},{18,26},{... | collective-permute-start | bytes 147464 | tf_op jit(solution)/shard_map/ppermute | solution.py:12
  13.9 57.4 %collective-permute-start.1 = (bf16[6,4096]{1,0:T(8,128)(2,1)S(1)}, bf16[6,4096]{1,0:T(8,128)(2,1)S(1)}, u32[]{:S(2)}, u32[]{:S(2)}) collective-permute-start(bf16[6,4096]{1,0:T(8,128)(2,1)S(1)} %slice_bitcast_fusion.1), channel_id=1, source_target_pairs={{0,8},{8,16},{16,24},{1,9},{9,17},{17,25},{2,10},{10,18},{18,26},{... | collective-permute-start | bytes 147464 | tf_op jit(solution)/shard_map/ppermute | solution.py:12
  18.2 55.5 %collective-permute-start = (bf16[6,4096]{1,0:T(8,128)(2,1)S(1)}, bf16[6,4096]{1,0:T(8,128)(2,1)S(1)}, u32[]{:S(2)}, u32[]{:S(2)}) collective-permute-start(bf16[6,4096]{1,0:T(8,128)(2,1)S(1)} %slice_bitcast_fusion.2), channel_id=1, source_target_pairs={{0,8},{8,16},{16,24},{1,9},{9,17},{17,25},{2,10},{10,18},{18,26},{... | collective-permute-start | bytes 147464 | tf_op jit(solution)/shard_map/ppermute | solution.py:12
  23.4 232.2 %all-gather.11.cloned.1.call-start = ((), (), s32[]{:S(2)}) async-start(), calls=%async_computation.6 | async-start | bytes 1310720 | tf_op jit(solution)/shard_map/all_gather | solution.py:17
  212.6 37.7 %copy-start.16 = (f32[16,4096]{1,0:T(8,128)S(1)}, f32[16,4096]{1,0:T(8,128)}, u32[]{:S(2)}) copy-start(f32[16,4096]{1,0:T(8,128)} %copy-done.15) | copy-start | bytes 786436
  212.6 37.7 %copy-start.51 = (f32[16]{0:T(128)S(1)}, f32[16]{0:T(128)}, u32[]{:S(2)}) copy-start(f32[16]{0:T(128)} %copy-done.50) | copy-start | bytes 196
  212.6 64.7 %all-gather.9.cloned.1.call-start = ((), (), s32[]{:S(2)}) async-start(), calls=%async_computation.5 | async-start | bytes 1310720 | tf_op jit(solution)/shard_map/all_gather | solution.py:17
  253.2 121.1 %reduce-scatter.5.cloned.1.call-start = ((), (), s32[]{:S(2)}) async-start(), calls=%async_computation.3 | async-start | bytes 327680 | tf_op jit(solution)/shard_map/reduce_scatter | solution.py:149
  257.8 23.3 %copy-start.13 = (f32[8,16,4096]{2,1,0:T(8,128)S(1)}, f32[8,16,4096]{2,1,0:T(8,128)}, u32[]{:S(2)}) copy-start(f32[8,16,4096]{2,1,0:T(8,128)} %get-tuple-element.338) | copy-start | bytes 6291460
  285.0 19.6 %copy-start.12 = (f32[8,16,4096]{2,1,0:T(8,128)S(1)}, f32[8,16,4096]{2,1,0:T(8,128)}, u32[]{:S(2)}) copy-start(f32[8,16,4096]{2,1,0:T(8,128)} %get-tuple-element.333) | copy-start | bytes 6291460
  338.0 55.0 %reduce-scatter.3.cloned.1.call-start = ((), (), s32[]{:S(2)}) async-start(), calls=%async_computation.2 | async-start | bytes 491520 | tf_op jit(solution)/shard_map/reduce_scatter | solution.py:148
  338.1 55.0 %collective-permute-start.3 = (f32[6,4096]{1,0:T(8,128)S(1)}, f32[6,4096]{1,0:T(8,128)S(1)}, u32[]{:S(2)}, u32[]{:S(2)}) collective-permute-start(f32[6,4096]{1,0:T(8,128)S(1)} %slice.387), channel_id=1, source_target_pairs={{8,0},{16,8},{24,16},{9,1},{17,9},{25,17},{10,2},{18,10},{26,18},{... | collective-permute-start | bytes 294920 | tf_op jit(solution)/shard_map/ppermute | solution.py:12
  339.4 31.9 %collective-permute-start.4 = (f32[6,4096]{1,0:T(8,128)S(1)}, f32[6,4096]{1,0:T(8,128)S(1)}, u32[]{:S(2)}, u32[]{:S(2)}) collective-permute-start(f32[6,4096]{1,0:T(8,128)S(1)} %slice.398), channel_id=1, source_target_pairs={{8,0},{16,8},{24,16},{9,1},{17,9},{25,17},{10,2},{18,10},{26,18},{... | collective-permute-start | bytes 294920 | tf_op jit(solution)/shard_map/ppermute | solution.py:12
  340.7 22.1 %collective-permute-start.5 = (f32[6,4096]{1,0:T(8,128)S(1)}, f32[6,4096]{1,0:T(8,128)S(1)}, u32[]{:S(2)}, u32[]{:S(2)}) collective-permute-start(f32[6,4096]{1,0:T(8,128)S(1)} %slice.409), channel_id=1, source_target_pairs={{8,0},{16,8},{24,16},{9,1},{17,9},{25,17},{10,2},{18,10},{26,18},{... | collective-permute-start | bytes 294920 | tf_op jit(solution)/shard_map/ppermute | solution.py:12
  362.8 85.3 %all-reduce.4.cloned.1.call-start = ((), (), s32[]{:S(2)}) async-start(), calls=%async_computation.7 | async-start | bytes 327680 | tf_op jit(solution)/shard_map/psum | solution.py:152
  371.2 21.9 %copy-start.25 = (f32[1,1,4096]{2,1,0:T(1,128)S(1)}, f32[1,1,4096]{2,1,0:T(1,128)}, u32[]{:S(2)}) copy-start(f32[1,1,4096]{2,1,0:T(1,128)} %get-tuple-element.409) | copy-start | bytes 49156
  371.2 21.9 %copy-start.26 = (f32[1,1,4096]{2,1,0:T(1,128)S(1)}, f32[1,1,4096]{2,1,0:T(1,128)}, u32[]{:S(2)}) copy-start(f32[1,1,4096]{2,1,0:T(1,128)} %get-tuple-element.410) | copy-start | bytes 49156
  371.2 21.9 %copy-start.27 = (f32[1,1,4096]{2,1,0:T(1,128)S(1)}, f32[1,1,4096]{2,1,0:T(1,128)}, u32[]{:S(2)}) copy-start(f32[1,1,4096]{2,1,0:T(1,128)} %get-tuple-element.411) | copy-start | bytes 49156
  371.2 21.9 %copy-start.28 = (f32[1,1,4096]{2,1,0:T(1,128)S(1)}, f32[1,1,4096]{2,1,0:T(1,128)}, u32[]{:S(2)}) copy-start(f32[1,1,4096]{2,1,0:T(1,128)} %get-tuple-element.412) | copy-start | bytes 49156
  371.2 21.9 %copy-start.29 = (f32[1,1,4096]{2,1,0:T(1,128)S(1)}, f32[1,1,4096]{2,1,0:T(1,128)}, u32[]{:S(2)}) copy-start(f32[1,1,4096]{2,1,0:T(1,128)} %get-tuple-element.413) | copy-start | bytes 49156
  371.2 21.9 %copy-start.30 = (f32[1,1,4096]{2,1,0:T(1,128)S(1)}, f32[1,1,4096]{2,1,0:T(1,128)}, u32[]{:S(2)}) copy-start(f32[1,1,4096]{2,1,0:T(1,128)} %get-tuple-element.414) | copy-start | bytes 49156
  393.1 75.2 %copy-start.47 = (f32[4096]{0:T(1024)S(1)}, f32[4096]{0:T(1024)}, u32[]{:S(2)}) copy-start(f32[4096]{0:T(1024)} %all_gather.37) | copy-start | bytes 49156
  (41 other events, 258.3 us)
Sparse Core Ops, SparseCore 0:
  23.5 25.8 all-gather.6
  212.7 25.9 all-gather.10
  253.3 23.9 all-gather.8
  338.1 25.6 reduce-scatter.4
  367.0 25.9 reduce-scatter.2
  395.3 52.7 all-reduce.3
where the time goes:
time: 479 us; the launch traced here: 476 us
  other arithmetic  214 us (45%)
  local copies, waits for them, and re-layouts  93.9 us (20%)
  waiting for transfers between devices  80.7 us (17%)
  blocking collectives  54.9 us (11%)
  starting transfers between devices  15.8 us (3%)
  between operations  15.5 us (3%)
    psum x1, waiting for transfers between devices, per_device(): totals = lax.psum((shares[0], shares[1], shares[2]), 'dp')  46.3 us
    unnamed x129, local copies, waits for them, and re-layouts  37.3 us
    reduce_sum x1, other arithmetic, convolve(): inner = jnp.sum(stacked[:, None] * toeplitz[None], 2)  33.7 us
    reduce_sum x1, other arithmetic, make_tables(): toeplitz = jnp.sum(onehot[:, :, :, None] * lag_filter[None, None], 2)  30 us
    broadcast_in_dim x3, other arithmetic, per_device(): transpose_taps(jnp.concatenate([adjoints[idx], after[idx]], 0), taps[idx])  19.9 us
    reduce_sum x2, other arithmetic, tap_terms(): return jnp.sum(adjoint[None] * windows, 1)  19.8 us
    reduce_sum x1, other arithmetic, convolve(): return inner + jnp.sum(starts[:, None] * head[None], 2)  19.6 us
    reduce_scatter x1, waiting for transfers between devices, per_device(): lax.psum_scatter(tap_grad, 'seq', scatter_dimension=2, tiled=True)  18.7 us
  transfers between devices with their start and end apart: 12, of which 3 were waited for; matrix products, arithmetic and copies ran while one was open for 51% of the time, Pallas kernels for 0%

commit v1 on v0

v1 whole, which is shorter than its diff:
```python
import functools

import jax
import jax.numpy as jnp
from jax import lax
from jax.experimental import pallas as pl
from jax.experimental.pallas import tpu as pltpu
from jax.sharding import PartitionSpec as P

LANES = 512
RIM = 8
TAIL = 16
F32 = jnp.float32


def passed_along(x, axis, by):
    count = lax.axis_size(axis)
    pairs = [(i, i + by) for i in range(count) if 0 <= i + by < count]
    return lax.ppermute(x, axis, pairs)


def load_padded(x_ref, rim_ref, pad_ref, s):
    rows = x_ref.shape[0]
    pad_ref[s, 0:RIM, :] = rim_ref[s].astype(F32)
    pad_ref[s, RIM : RIM + rows, :] = x_ref[...].astype(F32)


def featurize(pad_ref, taps_ref, s, rows):
    count = taps_ref.shape[1]
    total = taps_ref[s, 0:1, :] * pad_ref[s, RIM : RIM + rows, :]
    for lag in range(1, count):
        total = total + taps_ref[s, lag : lag + 1, :] * pad_ref[s, RIM - lag : RIM - lag + rows, :]
    return total


def states_kernel(q_ref, k_ref, v_ref, c_ref, rim_ref, taps_ref, a_ref, f_ref, b_ref, pad_ref, p_ref, z_ref):
    rows = q_ref.shape[0]
    for s, x_ref in enumerate((q_ref, k_ref, v_ref)):
        load_padded(x_ref, rim_ref, pad_ref, s)
    fq = featurize(pad_ref, taps_ref, 0, rows)
    fk = featurize(pad_ref, taps_ref, 1, rows)
    fv = featurize(pad_ref, taps_ref, 2, rows)
    p_ref[...] = fk * fv
    z_ref[...] = c_ref[...].astype(F32) * fq
    a = a_ref[...]

    def step(i, carry):
        h, g = carry
        h = a * h + p_ref[pl.ds(i, 1), :]
        g = a * g + z_ref[pl.ds(rows - 1 - i, 1), :]
        return (h, g)

    zero = jnp.zeros_like(a)
    h, g = lax.fori_loop(0, rows, step, (zero, zero), unroll=8)
    f_ref[...] = h
    b_ref[...] = g


def main_kernel(
    q_ref, k_ref, v_ref, c_ref, rim_ref, taps_ref, a_ref, r_ref, skip_ref, s_ref, g_ref,
    mixed_ref, gq_ref, gk_ref, gv_ref, tail_ref, head_ref, grads_ref,
    pad_ref, p_ref, z_ref, y_ref, u_ref, adj_ref,
):
    rows = q_ref.shape[0]
    count = taps_ref.shape[1]
    poles = a_ref.shape[0]
    for s, x_ref in enumerate((q_ref, k_ref, v_ref)):
        load_padded(x_ref, rim_ref, pad_ref, s)
    fq = featurize(pad_ref, taps_ref, 0, rows)
    fk = featurize(pad_ref, taps_ref, 1, rows)
    fv = featurize(pad_ref, taps_ref, 2, rows)
    cot = c_ref[...].astype(F32)
    p_ref[...] = fk * fv
    z_ref[...] = cot * fq
    a = a_ref[...]
    r = r_ref[...]

    def step(i, carry):
        h, g, acc = carry
        h = a * h + p_ref[pl.ds(i, 1), :]
        acc = acc + z_ref[pl.ds(i, 1), :] * h
        y_ref[pl.ds(i, 1), :] = jnp.sum(r * h, axis=0, keepdims=True)
        back = rows - 1 - i
        g = a * g + z_ref[pl.ds(back, 1), :]
        u_ref[pl.ds(back, 1), :] = jnp.sum(r * g, axis=0, keepdims=True)
        return (h, g, acc)

    h, g, acc = lax.fori_loop(
        0, rows, step, (s_ref[...], g_ref[...], jnp.zeros_like(a)), unroll=8
    )
    skip = skip_ref[...]
    p = p_ref[...]
    z = z_ref[...]
    conv = y_ref[...] + skip * p
    mixed_ref[...] = (fq * conv).astype(mixed_ref.dtype)
    adj_u = u_ref[...] + skip * z
    adjoints = (cot * conv, adj_u * fv, adj_u * fk)
    zeros_rim = jnp.zeros((RIM, adj_ref.shape[2]), F32)
    outs = (gq_ref, gk_ref, gv_ref)
    for s in range(3):
        adj_ref[s, 0:rows, :] = adjoints[s]
        adj_ref[s, rows : rows + RIM, :] = zeros_rim
        head_ref[s] = adjoints[s][0:RIM]
        total = taps_ref[s, 0:1, :] * adjoints[s]
        for lag in range(1, count):
            total = total + taps_ref[s, lag : lag + 1, :] * adj_ref[s, lag : lag + rows, :]
        outs[s][...] = total.astype(outs[s].dtype)
        tail_ref[s] = total[rows - TAIL : rows]
        for lag in range(count):
            window = pad_ref[s, RIM - lag : RIM - lag + rows, :]
            row = s * count + lag
            grads_ref[row : row + 1, :] = jnp.sum(adjoints[s] * window, axis=0, keepdims=True)
    base = 3 * count
    grads_ref[base : base + poles, :] = acc
    grads_ref[base + poles : base + poles + 1, :] = jnp.sum(z * p, axis=0, keepdims=True)


def tile(shape, lanes):
    nd = len(shape)
    return pl.BlockSpec(tuple(shape[:-1]) + (lanes,), lambda i: (0,) * (nd - 1) + (i,))


def run_states(q, k, v, c, rim, taps, a):
    rows, width = q.shape
    poles = a.shape[0]
    lanes = min(LANES, width)
    ins = (q, k, v, c, rim, taps, a)
    return pl.pallas_call(
        states_kernel,
        grid=(width // lanes,),
        in_specs=[tile(x.shape, lanes) for x in ins],
        out_specs=[tile((poles, width), lanes), tile((poles, width), lanes)],
        out_shape=[jax.ShapeDtypeStruct((poles, width), F32)] * 2,
        scratch_shapes=[
            pltpu.VMEM((3, rows + RIM, lanes), F32),
            pltpu.VMEM((rows, lanes), F32),
            pltpu.VMEM((rows, lanes), F32),
        ],
    )(*ins)


def run_main(q, k, v, c, rim, taps, a, r, skip, s_in, g_in):
    rows, width = q.shape
    poles = a.shape[0]
    count = taps.shape[1]
    lanes = min(LANES, width)
    ins = (q, k, v, c, rim, taps, a, r, skip, s_in, g_in)
    out_shapes = [
        jax.ShapeDtypeStruct((rows, width), jnp.bfloat16),
        jax.ShapeDtypeStruct((rows, width), jnp.bfloat16),
        jax.ShapeDtypeStruct((rows, width), jnp.bfloat16),
        jax.ShapeDtypeStruct((rows, width), jnp.bfloat16),
        jax.ShapeDtypeStruct((3, TAIL, width), F32),
        jax.ShapeDtypeStruct((3, RIM, width), F32),
        jax.ShapeDtypeStruct((3 * count + poles + 1, width), F32),
    ]
    return pl.pallas_call(
        main_kernel,
        grid=(width // lanes,),
        in_specs=[tile(x.shape, lanes) for x in ins],
        out_specs=[tile(o.shape, lanes) for o in out_shapes],
        out_shape=out_shapes,
        scratch_shapes=[
            pltpu.VMEM((3, rows + RIM, lanes), F32),
            pltpu.VMEM((rows, lanes), F32),
            pltpu.VMEM((rows, lanes), F32),
            pltpu.VMEM((rows, lanes), F32),
            pltpu.VMEM((rows, lanes), F32),
            pltpu.VMEM((3, rows + RIM, lanes), F32),
        ],
    )(*ins)


def carried(final, decay, rows, axis, by):
    count = lax.axis_size(axis)
    window = final
    incoming = jnp.zeros_like(final)
    span = 1
    covered = 0
    while span < count:
        got = passed_along(window, axis, by * span)
        incoming = incoming + jnp.exp(-decay * (rows * covered)) * got
        window = window + jnp.exp(-decay * (rows * span)) * got
        covered += span
        span *= 2
    return incoming


def per_device(queries, keys, values, cotangent, taps, residue, skip, decay):
    rows = queries.shape[1]
    width = queries.shape[2]
    count = taps.shape[1]
    poles = decay.shape[0]
    q, k, v, c = queries[0], keys[0], values[0], cotangent[0]
    rim = passed_along(jnp.stack([q[rows - RIM :], k[rows - RIM :], v[rows - RIM :]], 0), "seq", 1)
    a = jnp.exp(-decay)
    f_local, b_local = run_states(q, k, v, c, rim, taps, a)
    with jax.named_scope("modal_state_scan"):
        s_in = carried(f_local, decay, rows, "seq", 1)
        g_in = carried(b_local, decay, rows, "seq", -1)
    mixed, gq, gk, gv, tails, heads, grads = run_main(
        q, k, v, c, rim, taps, a, residue, skip.reshape(1, width), s_in, g_in
    )
    after = passed_along(heads, "seq", -1)
    ext = jnp.concatenate(
        [jnp.zeros((3, TAIL, width), F32), after[:, : count - 1], jnp.zeros((3, 1, width), F32)], 1
    )
    corr = sum(taps[:, lag, None, :] * ext[:, lag : lag + TAIL] for lag in range(count))
    fixed = (tails + corr).astype(jnp.bfloat16)
    streams = [
        lax.dynamic_update_slice(g, fixed[idx], (rows - TAIL, 0)) for idx, g in enumerate((gq, gk, gv))
    ]
    totals = lax.psum(grads, ("seq", "dp"))
    grad_taps = totals[: 3 * count].reshape(3, count, width)
    grad_residue = totals[3 * count : 3 * count + poles]
    grad_skip = totals[3 * count + poles]
    return (
        mixed[None],
        streams[0][None],
        streams[1][None],
        streams[2][None],
        grad_taps,
        grad_residue,
        grad_skip,
    )


def solution(mesh):
    return jax.shard_map(
        per_device,
        mesh=mesh,
        in_specs=(
            P("dp", "seq", None),
            P("dp", "seq", None),
            P("dp", "seq", None),
            P("dp", "seq", None),
            P(),
            P(),
            P(),
            P(),
        ),
        out_specs=(
            P("dp", "seq", None),
            P("dp", "seq", None),
            P("dp", "seq", None),
            P("dp", "seq", None),
            P(),
            P(),
            P(),
        ),
        check_vma=False,
    )
```

time: 479 us -> 255 us (0.53)
  other arithmetic: 214 us -> 5.89 us
  local copies, waits for them, and re-layouts: 93.9 us -> 7.39 us
  waiting for transfers between devices: 80.7 us -> 151 us
  Pallas kernels: 0 us -> 61.6 us
  blocking collectives: 54.9 us -> 0 us
    reduce_sum x9 -> x0, other arithmetic: 133 us -> none  [the longest x1 33.7 us: convolve(): inner = jnp.sum(stacked[:, None] * toeplitz[None], 2)]
    psum x1, waiting for transfers between devices: 46.3 us -> 131 us  [per_device(): totals = lax.psum(grads, ('seq', 'dp'))]
    pallas_call x0 -> x2, Pallas kernels: none -> 61.6 us  [the longest x1 46.5 us: run_main(): pl.pallas_call(main_kernel, grid=(width // lanes,), in_specs=[tile(x.shap...]
    rev x5 -> x0, local copies, waits for them, and re-layouts: 43 us -> none  [the longest x1 16.9 us: per_device(): convolve(flipped, back_starts, toeplitz, head).reshape(rows, width)[::-1]]
    unnamed x129 -> x12, local copies, waits for them, and re-layouts: 37.3 us -> 0.95 us
    all_gather x3 -> x0, blocking collectives: 27.4 us -> none  [the longest x1 9.56 us: per_device(): lax.all_gather(totals[0], 'seq', axis=2, tiled=True)]
    add x19 -> x2, other arithmetic: 24.2 us -> 2.01 us  [the longest x1 1.1 us: carried(): window = window + jnp.exp(-decay * (rows * span)) * got]
    broadcast_in_dim x3 -> x0, other arithmetic: 19.9 us -> none  [per_device(): transpose_taps(jnp.concatenate([adjoints[idx], after[idx]], 0), taps[idx])]
  transfers between devices with their start and end apart: 12 -> 7, of which waited for: 3 -> 6; matrix products, arithmetic and copies ran while one was open for 51% -> 2% of each run, Pallas kernels for 0% -> 0%
where the time goes in v1:
time: 255 us
  waiting for transfers between devices  151 us (59%)
  Pallas kernels  61.6 us (24%)
  starting transfers between devices  14.5 us (6%)
  between operations  14.2 us (6%)
  local copies, waits for them, and re-layouts  7.39 us (3%)
  other arithmetic  5.89 us (2%)
    psum x1, waiting for transfers between devices, per_device(): totals = lax.psum(grads, ('seq', 'dp'))  131 us
    pallas_call x1, Pallas kernels, run_main(): pl.pallas_call(main_kernel, grid=(width // lanes,), in_specs=[tile(x.shap...  46.5 us
    ppermute x6, waiting for transfers between devices, passed_along(): return lax.ppermute(x, axis, pairs)  19.6 us
    pallas_call x1, Pallas kernels, run_states(): pl.pallas_call(states_kernel, grid=(width // lanes,), in_specs=[tile(x.sh...  15.1 us
    ppermute x6, starting transfers between devices, passed_along(): return lax.ppermute(x, axis, pairs)  14.5 us
  transfers between devices with their start and end apart: 7, of which 6 were waited for; matrix products, arithmetic and copies ran while one was open for 2% of the time, Pallas kernels for 0%

profile of v1, /device:TPU:0, one launch (start us, length us, event | category | flops | bytes accessed | tf_op | source)
XLA Modules:
  0.0 254.6 jit_solution(9800308843102032400)
XLA Ops:
  7.2 0.9 slice.78
  8.1 0.8 slice.79
  8.9 0.8 slice.80
  9.8 4.9 %collective-permute-start = (bf16[3,8,4096]{2,1,0:T(8,128)(2,1)S(1)}, bf16[3,8,4096]{2,1,0:T(8,128)(2,1)S(1)}, u32[]{:S(2)}, u32[]{:S(2)}) collective-permute-start(bf16[3,8,4096]{2,1,0:T(8,128)(2,1)S(1)} %pad_maximum_fusion), channel_id=1, source_target_pairs={{0,8},{8,16},{16,24},{1,9},{9,17},{17,25},{2,10},{10,18},{18,26},{... | collective-permute-start | bytes 589832 | tf_op jit(solution)/shard_map/ppermute | solution.py:19
  14.7 2.6 %slice_multiply_fusion = (f32[3,1,4096]{2,1,0:T(1,128)S(1)}, f32[3,1,4096]{2,1,0:T(1,128)S(1)}, f32[3,1,4096]{2,1,0:T(1,128)S(1)}, f32[3,1,4096]{2,1,0:T(1,128)S...) fusion(f32[3,7,4096]{2,1,0:T(8,128)} %taps_ref.3), kind=kLoop, calls=%fused_computation.38 | loop fusion | flops 12288 | bytes 688128 | tf_op jit(solution)/shard_map/mul | solution.py:208
  17.3 0.7 negate_exponential_fusion.a_ref
  18.1 0.8 collective-permute-done.rim_ref
  19.5 15.1 %shard_map.135 = (f32[16,4096]{1,0:T(8,128)}, f32[16,4096]{1,0:T(8,128)}) custom-call(bf16[128,4096]{1,0:T(8,128)(2,1)} %bitcast.26, bf16[128,4096]{1,0:T(8,128)(2,1)} %bitcast.28, bf16[128,4096]{1,0:T(8,128)(2,1)} %bitcast.30, bf16[128,4096]{1,0:T(8,128)(2,1)} %bitcast.32, bf16[3,8,4096]{2,1,0:T(8,128)(2,1)} %copy-done.2, f32[3,7,4096]{2,1,0:T(8,128)} %taps_ref.3, ...), custom_call_target="tpu_custom_call" | custom-call | tf_op jit(solution)/shard_map/pallas_call | solution.py:128
  34.6 4.4 %collective-permute-start.1 = (f32[16,4096]{1,0:T(8,128)}, f32[16,4096]{1,0:T(8,128)S(1)}, u32[]{:S(2)}, u32[]{:S(2)}) collective-permute-start(f32[16,4096]{1,0:T(8,128)} %get-tuple-element.16), channel_id=1, source_target_pairs={{0,8},{8,16},{16,24},{1,9},{9,17},{17,25},{2,10},{10,18},{18,26},{... | collective-permute-start | bytes 786440 | tf_op jit(solution)/shard_map/modal_state_scan/ppermute | solution.py:19
  39.0 1.3 collective-permute-start.3
  40.4 3.6 %collective-permute-done.1 = f32[16,4096]{1,0:T(8,128)S(1)} collective-permute-done((f32[16,4096]{1,0:T(8,128)}, f32[16,4096]{1,0:T(8,128)S(1)}, u32[]{:S(2)}, u32[]{:S(2)}) %collective-permute-start.1) | collective-permute-done | bytes 262176 | tf_op jit(solution)/shard_map/modal_state_scan/ppermute | solution.py:19
  44.0 8.4 %collective-permute-done.3 = f32[16,4096]{1,0:T(8,128)S(1)} collective-permute-done((f32[16,4096]{1,0:T(8,128)}, f32[16,4096]{1,0:T(8,128)S(1)}, u32[]{:S(2)}, u32[]{:S(2)}) %collective-permute-start.3) | collective-permute-done | bytes 262176 | tf_op jit(solution)/shard_map/modal_state_scan/ppermute | solution.py:19
  52.4 1.1 multiply_add_fusion.1
  53.5 1.3 collective-permute-start.2
  54.8 1.3 collective-permute-start.4
  56.2 2.7 %collective-permute-done.2 = f32[16,4096]{1,0:T(8,128)S(1)} collective-permute-done((f32[16,4096]{1,0:T(8,128)S(1)}, f32[16,4096]{1,0:T(8,128)S(1)}, u32[]{:S(2)}, u32[]{:S(2)}) %collective-permute-start.2) | collective-permute-done | bytes 262176 | tf_op jit(solution)/shard_map/modal_state_scan/ppermute | solution.py:19
  58.9 4.2 %collective-permute-done.4 = f32[16,4096]{1,0:T(8,128)S(1)} collective-permute-done((f32[16,4096]{1,0:T(8,128)S(1)}, f32[16,4096]{1,0:T(8,128)S(1)}, u32[]{:S(2)}, u32[]{:S(2)}) %collective-permute-start.4) | collective-permute-done | bytes 262176 | tf_op jit(solution)/shard_map/modal_state_scan/ppermute | solution.py:19
  63.1 0.9 multiply_add_fusion
  64.0 46.5 %shard_map.136 = (bf16[128,4096]{1,0:T(8,128)(2,1)}, bf16[128,4096]{1,0:T(8,128)(2,1)}, bf16[128,4096]{1,0:T(8,128)(2,1)}, bf16[128,4096]{1,0:T(8,128)(2,1)}, f3...) custom-call(bf16[128,4096]{1,0:T(8,128)(2,1)} %bitcast.27, bf16[128,4096]{1,0:T(8,128)(2,1)} %bitcast.29, ...), custom_call_target="tpu_custom_call" | custom-call | tf_op jit(solution)/shard_map/pallas_call | solution.py:157
  110.4 1.3 collective-permute-start.5
  111.9 131.5 %all-reduce.3.cloned.1.call-done = f32[38,4096]{1,0:T(8,128)} async-done(((f32[38,4096]{1,0:T(8,128)}), f32[38,4096]{1,0:T(8,128)}) %all-reduce.3.cloned.1.call-update) | async-done | bytes 622608 | tf_op jit(solution)/shard_map/psum | solution.py:213
  243.3 1.0 slice-done
  244.3 0.8 reshape.38
  247.0 0.8 slice_dynamic-update-slice_fusion
  (20 shorter events, 2.9 us)
Async XLA Ops:
  7.2 10.1 %copy-start = (f32[16,4096]{1,0:T(8,128)S(1)}, f32[16,4096]{1,0:T(8,128)}, u32[]{:S(2)}) copy-start(f32[16,4096]{1,0:T(8,128)} %param.15) | copy-start | bytes 786436
  7.2 236.2 %all-reduce.3.cloned.1.call-start = ((), (), s32[]{:S(2)}) async-start(), calls=%async_computation | async-start | bytes 1310720 | tf_op jit(solution)/shard_map/psum | solution.py:213
  9.8 9.0 %collective-permute-start = (bf16[3,8,4096]{2,1,0:T(8,128)(2,1)S(1)}, bf16[3,8,4096]{2,1,0:T(8,128)(2,1)S(1)}, u32[]{:S(2)}, u32[]{:S(2)}) collective-permute-start(bf16[3,8,4096]{2,1,0:T(8,128)(2,1)S(1)} %pad_maximum_fusion), channel_id=1, source_target_pairs={{0,8},{8,16},{16,24},{1,9},{9,17},{17,25},{2,10},{10,18},{18,26},{... | collective-permute-start | bytes 589832 | tf_op jit(solution)/shard_map/ppermute | solution.py:19
  18.8 0.7 copy-start.2
  34.6 9.4 %collective-permute-start.1 = (f32[16,4096]{1,0:T(8,128)}, f32[16,4096]{1,0:T(8,128)S(1)}, u32[]{:S(2)}, u32[]{:S(2)}) collective-permute-start(f32[16,4096]{1,0:T(8,128)} %get-tuple-element.16), channel_id=1, source_target_pairs={{0,8},{8,16},{16,24},{1,9},{9,17},{17,25},{2,10},{10,18},{18,26},{... | collective-permute-start | bytes 786440 | tf_op jit(solution)/shard_map/modal_state_scan/ppermute | solution.py:19
  39.0 13.3 %collective-permute-start.3 = (f32[16,4096]{1,0:T(8,128)}, f32[16,4096]{1,0:T(8,128)S(1)}, u32[]{:S(2)}, u32[]{:S(2)}) collective-permute-start(f32[16,4096]{1,0:T(8,128)} %get-tuple-element.17), channel_id=1, source_target_pairs={{8,0},{16,8},{24,16},{9,1},{17,9},{25,17},{10,2},{18,10},{26,18},{... | collective-permute-start | bytes 786440 | tf_op jit(solution)/shard_map/modal_state_scan/ppermute | solution.py:19
  53.5 5.4 %collective-permute-start.2 = (f32[16,4096]{1,0:T(8,128)S(1)}, f32[16,4096]{1,0:T(8,128)S(1)}, u32[]{:S(2)}, u32[]{:S(2)}) collective-permute-start(f32[16,4096]{1,0:T(8,128)S(1)} %get-tuple-element.38), channel_id=1, source_target_pairs={{0,16},{8,24},{1,17},{9,25},{2,18},{10,26},{3,19},{11,27},{4,20},{... | collective-permute-start | bytes 786440 | tf_op jit(solution)/shard_map/modal_state_scan/ppermute | solution.py:19
  54.8 8.3 %collective-permute-start.4 = (f32[16,4096]{1,0:T(8,128)S(1)}, f32[16,4096]{1,0:T(8,128)S(1)}, u32[]{:S(2)}, u32[]{:S(2)}) collective-permute-start(f32[16,4096]{1,0:T(8,128)S(1)} %get-tuple-element.37), channel_id=1, source_target_pairs={{16,0},{24,8},{17,1},{25,9},{18,2},{26,10},{19,3},{27,11},{20,4},{... | collective-permute-start | bytes 786440 | tf_op jit(solution)/shard_map/modal_state_scan/ppermute | solution.py:19
  110.4 136.0 %collective-permute-start.5 = (f32[3,8,4096]{2,1,0:T(8,128)}, f32[3,8,4096]{2,1,0:T(8,128)S(1)}, u32[]{:S(2)}, u32[]{:S(2)}) collective-permute-start(f32[3,8,4096]{2,1,0:T(8,128)} %get-tuple-element.21), channel_id=1, source_target_pairs={{8,0},{16,8},{24,16},{9,1},{17,9},{25,17},{10,2},{18,10},{26,18},{... | collective-permute-start | bytes 1179656 | tf_op jit(solution)/shard_map/ppermute | solution.py:19
  243.3 1.0 slice-start
  243.3 1.8 copy-start.1
  243.3 3.1 %copy-start.3 = (f32[3,16,4096]{2,1,0:T(8,128)S(1)}, f32[3,16,4096]{2,1,0:T(8,128)}, u32[]{:S(2)}) copy-start(f32[3,16,4096]{2,1,0:T(8,128)} %get-tuple-element.20) | copy-start | bytes 2359300
Sparse Core Ops, SparseCore 0:
  111.9 131.4 all-reduce.2

commit v2 on v1

--- a/solution.py
+++ b/solution.py
@@ -171,19 +171,75 @@
     )(*ins)
 
 
-def carried(final, decay, rows, axis, by):
+def exchange(x, axis, size):
     count = lax.axis_size(axis)
-    window = final
-    incoming = jnp.zeros_like(final)
-    span = 1
-    covered = 0
-    while span < count:
-        got = passed_along(window, axis, by * span)
-        incoming = incoming + jnp.exp(-decay * (rows * covered)) * got
-        window = window + jnp.exp(-decay * (rows * span)) * got
-        covered += span
-        span *= 2
-    return incoming
+    return lax.ppermute(x, axis, [(i, i ^ size) for i in range(count)])
+
+
+def decayed(decay, rows, steps):
+    return jnp.exp(-decay * (rows * steps).astype(F32))
+
+
+def scan_states(final_f, final_b, decay, rows, axis):
+    count = lax.axis_size(axis)
+    mine = lax.axis_index(axis)
+    block_f, block_b = (final_f, final_b)
+    incoming_f = jnp.zeros_like(final_f)
+    incoming_b = jnp.zeros_like(final_b)
+    levels = count.bit_length() - 1
+    for level in range(levels):
+        size = 1 << level
+        upper = (mine // size) % 2 == 1
+        pos = mine % size
+        if level == levels - 1:
+            got = exchange(jnp.where(upper, block_b, block_f), axis, size)
+            got_f, got_b = (got, got)
+        else:
+            got = exchange(jnp.stack([block_f, block_b]), axis, size)
+            got_f, got_b = (got[0], got[1])
+        incoming_f = incoming_f + jnp.where(upper, decayed(decay, rows, pos) * got_f, 0.0)
+        incoming_b = incoming_b + jnp.where(upper, 0.0, decayed(decay, rows, size - 1 - pos) * got_b)
+        if level < levels - 1:
+            jump = jnp.exp(-decay * float(rows * size))
+            block_f = jnp.where(upper, block_f + jump * got_f, got_f + jump * block_f)
+            block_b = jnp.where(upper, got_b + jump * block_b, block_b + jump * got_b)
+    return (incoming_f, incoming_b)
+
+
+def butterfly_sum(x, steps):
+    shape = x.shape
+    flat = x.reshape(-1)
+    pieces = 1 << len(steps)
+    unit = pieces * 128
+    padded = -(-flat.shape[0] // unit) * unit
+    flat = jnp.pad(flat, (0, padded - flat.shape[0])).reshape(-1, 128)
+    sides = []
+    for axis, size in steps:
+        upper = (lax.axis_index(axis) // size) % 2 == 1
+        sides.append(upper)
+        half = flat.shape[0] // 2
+        low, high = (flat[:half], flat[half:])
+        keep = jnp.where(upper, high, low)
+        send = jnp.where(upper, low, high)
+        flat = keep + exchange(send, axis, size)
+    for (axis, size), upper in reversed(list(zip(steps, sides))):
+        got = exchange(flat, axis, size)
+        flat = jnp.where(upper, jnp.concatenate([got, flat]), jnp.concatenate([flat, got]))
+    return flat.reshape(-1)[: x.size].reshape(shape)
+
+
+def sum_steps():
+    steps = []
+    dp_count = lax.axis_size("dp")
+    seq_count = lax.axis_size("seq")
+    if dp_count & (dp_count - 1) or seq_count & (seq_count - 1):
+        return None
+    dp_bits = [1 << b for b in range(dp_count.bit_length() - 1)]
+    seq_bits = [1 << b for b in range(seq_count.bit_length() - 1)]
+    steps = [("dp", size) for size in dp_bits[:1]]
+    steps += [("seq", size) for size in seq_bits]
+    steps += [("dp", size) for size in dp_bits[1:]]
+    return steps
 
 
 def per_device(queries, keys, values, cotangent, taps, residue, skip, decay):
@@ -196,8 +252,7 @@
     a = jnp.exp(-decay)
     f_local, b_local = run_states(q, k, v, c, rim, taps, a)
     with jax.named_scope("modal_state_scan"):
-        s_in = carried(f_local, decay, rows, "seq", 1)
-        g_in = carried(b_local, decay, rows, "seq", -1)
+        s_in, g_in = scan_states(f_local, b_local, decay, rows, "seq")
     mixed, gq, gk, gv, tails, heads, grads = run_main(
         q, k, v, c, rim, taps, a, residue, skip.reshape(1, width), s_in, g_in
     )
@@ -210,7 +265,12 @@
     streams = [
         lax.dynamic_update_slice(g, fixed[idx], (rows - TAIL, 0)) for idx, g in enumerate((gq, gk, gv))
     ]
-    totals = lax.psum(grads, ("seq", "dp"))
+    steps = sum_steps()
+    if steps is None:
+        totals = lax.psum(grads, ("seq", "dp"))
+    else:
+        with jax.named_scope("filter_grad_sum"):
+            totals = butterfly_sum(grads, steps)
     grad_taps = totals[: 3 * count].reshape(3, count, width)
     grad_residue = totals[3 * count : 3 * count + poles]
     grad_skip = totals[3 * count + poles]

time: 255 us -> 144 us (0.56)
  waiting for transfers between devices: 151 us -> 40 us
  starting transfers between devices: 14.5 us -> 28.5 us
  between operations: 14.2 us -> 0.87 us
    psum x1 -> x0, waiting for transfers between devices: 131 us -> none  [per_device(): totals = lax.psum(grads, ('seq', 'dp'))]
    ppermute x0 -> x12, waiting for transfers between devices: none -> 35.9 us  [exchange(): return lax.ppermute(x, axis, [(i, i ^ size) for i in range(count)])]
    ppermute x0 -> x12, starting transfers between devices: none -> 22.4 us  [exchange(): return lax.ppermute(x, axis, [(i, i ^ size) for i in range(count)])]
    ppermute x6 -> x2, waiting for transfers between devices: 19.6 us -> 4.1 us  [passed_along(): return lax.ppermute(x, axis, pairs)]
    ppermute x6 -> x2, starting transfers between devices: 14.5 us -> 6.17 us  [passed_along(): return lax.ppermute(x, axis, pairs)]
  transfers between devices with their start and end apart: 7 -> 14, of which waited for: 6 -> 14; matrix products, arithmetic and copies ran while one was open for 2% -> 3% of each run, Pallas kernels for 0% -> 0%
where the time goes in v2:
time: 144 us
  Pallas kernels  61.6 us (43%)
  waiting for transfers between devices  40 us (28%)
  starting transfers between devices  28.5 us (20%)
  local copies, waits for them, and re-layouts  6.57 us (5%)
  other arithmetic  6.28 us (4%)
    pallas_call x1, Pallas kernels, run_main(): pl.pallas_call(main_kernel, grid=(width // lanes,), in_specs=[tile(x.shap...  46.5 us
    ppermute x12, waiting for transfers between devices, exchange(): return lax.ppermute(x, axis, [(i, i ^ size) for i in range(count)])  35.9 us
    ppermute x12, starting transfers between devices, exchange(): return lax.ppermute(x, axis, [(i, i ^ size) for i in range(count)])  22.4 us
    pallas_call x1, Pallas kernels, run_states(): pl.pallas_call(states_kernel, grid=(width // lanes,), in_specs=[tile(x.sh...  15.1 us
    ppermute x2, starting transfers between devices, passed_along(): return lax.ppermute(x, axis, pairs)  6.17 us
    ppermute x2, waiting for transfers between devices, passed_along(): return lax.ppermute(x, axis, pairs)  4.1 us
  transfers between devices with their start and end apart: 14, of which 14 were waited for; matrix products, arithmetic and copies ran while one was open for 3% of the time, Pallas kernels for 0%

profile of v2, /device:TPU:0, one launch (start us, length us, event | category | flops | bytes accessed | tf_op | source)
XLA Modules:
  0.0 143.8 jit_solution(2394358636376432993)
XLA Ops:
  3.2 4.9 %collective-permute-start = (bf16[3,8,4096]{2,1,0:T(8,128)(2,1)S(1)}, bf16[3,8,4096]{2,1,0:T(8,128)(2,1)S(1)}, u32[]{:S(2)}, u32[]{:S(2)}) collective-permute-start(bf16[3,8,4096]{2,1,0:T(8,128)(2,1)S(1)} %pad_maximum_fusion.1), channel_id=1, source_target_pairs={{0,8},{8,16},{16,24},{1,9},{9,17},{17,25},{2,10},{10,18},{18,26},{... | collective-permute-start | bytes 589832 | tf_op jit(solution)/shard_map/ppermute | solution.py:19
  8.1 1.7 %negate_exponential_fusion.a_ref = f32[16,4096]{1,0:T(8,128)} fusion(f32[16,4096]{1,0:T(8,128)} %param.15), kind=kLoop, calls=%fused_computation.31 | loop fusion | flops 65536 | bytes 524288 | tf_op jit(solution)/shard_map/exp | solution.py:252
  9.8 2.4 %collective-permute-done.rim_ref = bf16[3,8,4096]{2,1,0:T(8,128)(2,1)S(1)} collective-permute-done((bf16[3,8,4096]{2,1,0:T(8,128)(2,1)S(1)}, bf16[3,8,4096]{2,1,0:T(8,128)(2,1)S(1)}, u32[]{:S(2)}, u32[]{:S(2)}) %collective-permute-start) | collective-permute-done | bytes 196640 | tf_op jit(solution)/shard_map/ppermute | solution.py:19
  12.9 15.1 %shard_map.135 = (f32[16,4096]{1,0:T(8,128)}, f32[16,4096]{1,0:T(8,128)}) custom-call(bf16[128,4096]{1,0:T(8,128)(2,1)} %bitcast.41, bf16[128,4096]{1,0:T(8,128)(2,1)} %bitcast.43, bf16[128,4096]{1,0:T(8,128)(2,1)} %bitcast.45, bf16[128,4096]{1,0:T(8,128)(2,1)} %bitcast.47, bf16[3,8,4096]{2,1,0:T(8,128)(2,1)} %copy-done.4, f32[3,7,4096]{2,1,0:T(8,128)} %taps_ref.3, ...), custom_call_target="tpu_custom_call" | custom-call | tf_op jit(solution)/shard_map/pallas_call | solution.py:128
  29.2 2.5 %collective-permute-start.1 = (f32[2,16,4096]{2,1,0:T(8,128)S(1)}, f32[2,16,4096]{2,1,0:T(8,128)S(1)}, u32[]{:S(2)}, u32[]{:S(2)}) collective-permute-start(f32[2,16,4096]{2,1,0:T(8,128)S(1)} %pad_maximum_fusion), channel_id=1, source_target_pairs={{0,8},{8,0},{16,24},{24,16},{1,9},{9,1},{17,25},{25,17},{2,10},{10... | collective-permute-start | bytes 1572872 | tf_op jit(solution)/shard_map/modal_state_scan/ppermute | solution.py:176
  31.7 11.1 %collective-permute-done.1 = f32[2,16,4096]{2,1,0:T(8,128)S(1)} collective-permute-done((f32[2,16,4096]{2,1,0:T(8,128)S(1)}, f32[2,16,4096]{2,1,0:T(8,128)S(1)}, u32[]{:S(2)}, u32[]{:S(2)}) %collective-permute-start.1) | collective-permute-done | bytes 524320 | tf_op jit(solution)/shard_map/modal_state_scan/ppermute | solution.py:176
  42.9 2.7 %collective-permute-start.2 = (f32[16,4096]{1,0:T(8,128)S(1)}, f32[16,4096]{1,0:T(8,128)S(1)}, u32[]{:S(2)}, u32[]{:S(2)}) collective-permute-start(f32[16,4096]{1,0:T(8,128)S(1)} %select_select_fusion), channel_id=1, source_target_pairs={{0,16},{8,24},{16,0},{24,8},{1,17},{9,25},{17,1},{25,9},{2,18},{10... | collective-permute-start | bytes 786440 | tf_op jit(solution)/shard_map/modal_state_scan/ppermute | solution.py:176
  45.7 4.6 %collective-permute-done.2 = f32[16,4096]{1,0:T(8,128)S(1)} collective-permute-done((f32[16,4096]{1,0:T(8,128)S(1)}, f32[16,4096]{1,0:T(8,128)S(1)}, u32[]{:S(2)}, u32[]{:S(2)}) %collective-permute-start.2) | collective-permute-done | bytes 262176 | tf_op jit(solution)/shard_map/modal_state_scan/ppermute | solution.py:176
  51.3 46.5 %shard_map.136 = (bf16[128,4096]{1,0:T(8,128)(2,1)}, bf16[128,4096]{1,0:T(8,128)(2,1)}, bf16[128,4096]{1,0:T(8,128)(2,1)}, bf16[128,4096]{1,0:T(8,128)(2,1)}, f3...) custom-call(bf16[128,4096]{1,0:T(8,128)(2,1)} %bitcast.42, bf16[128,4096]{1,0:T(8,128)(2,1)} %bitcast.44, ...), custom_call_target="tpu_custom_call" | custom-call | tf_op jit(solution)/shard_map/pallas_call | solution.py:157
  99.1 1.5 %collective-permute-done.4 = f32[608,128]{1,0:T(8,128)S(1)} collective-permute-done((f32[608,128]{1,0:T(8,128)S(1)}, f32[608,128]{1,0:T(8,128)S(1)}, u32[]{:S(2)}, u32[]{:S(2)}) %collective-permute-start.4) | collective-permute-done | bytes 311328 | tf_op jit(solution)/shard_map/filter_grad_sum/ppermute | solution.py:176
  101.6 5.2 %collective-permute-done.5 = f32[304,128]{1,0:T(8,128)S(1)} collective-permute-done((f32[304,128]{1,0:T(8,128)S(1)}, f32[304,128]{1,0:T(8,128)S(1)}, u32[]{:S(2)}, u32[]{:S(2)}) %collective-permute-start.5) | collective-permute-done | bytes 155680 | tf_op jit(solution)/shard_map/filter_grad_sum/ppermute | solution.py:176
  106.9 1.8 %collective-permute-start.6 = (f32[152,128]{1,0:T(8,128)S(1)}, f32[152,128]{1,0:T(8,128)S(1)}, u32[]{:S(2)}, u32[]{:S(2)}) collective-permute-start(f32[152,128]{1,0:T(8,128)S(1)} %slice_select_fusion.3), channel_id=1, source_target_pairs={{0,16},{8,24},{16,0},{24,8},{1,17},{9,25},{17,1},{25,9},{2,18},{10... | collective-permute-start | bytes 233480 | tf_op jit(solution)/shard_map/filter_grad_sum/ppermute | solution.py:176
  108.8 2.6 %collective-permute-done.6 = f32[152,128]{1,0:T(8,128)S(1)} collective-permute-done((f32[152,128]{1,0:T(8,128)S(1)}, f32[152,128]{1,0:T(8,128)S(1)}, u32[]{:S(2)}, u32[]{:S(2)}) %collective-permute-start.6) | collective-permute-done | bytes 77856 | tf_op jit(solution)/shard_map/filter_grad_sum/ppermute | solution.py:176
  111.4 1.6 %collective-permute-start.7 = (f32[76,128]{1,0:T(8,128)S(1)}, f32[76,128]{1,0:T(8,128)S(1)}, u32[]{:S(2)}, u32[]{:S(2)}) collective-permute-start(f32[76,128]{1,0:T(8,128)S(1)} %slice_select_fusion.4), channel_id=1, source_target_pairs={{0,2},{1,3},{2,0},{3,1},{4,6},{5,7},{6,4},{7,5},{8,10},{9,11},{10,... | collective-permute-start | bytes 116744 | tf_op jit(solution)/shard_map/filter_grad_sum/ppermute | solution.py:176
  113.1 2.4 %collective-permute-done.7 = f32[76,128]{1,0:T(8,128)S(1)} collective-permute-done((f32[76,128]{1,0:T(8,128)S(1)}, f32[76,128]{1,0:T(8,128)S(1)}, u32[]{:S(2)}, u32[]{:S(2)}) %collective-permute-start.7) | collective-permute-done | bytes 38944 | tf_op jit(solution)/shard_map/filter_grad_sum/ppermute | solution.py:176
  115.5 2.9 %collective-permute-start.8 = (f32[38,128]{1,0:T(8,128)S(1)}, f32[38,128]{1,0:T(8,128)S(1)}, u32[]{:S(2)}, u32[]{:S(2)}) collective-permute-start(f32[38,128]{1,0:T(8,128)S(1)} %slice_select_fusion.5), channel_id=1, source_target_pairs={{0,4},{1,5},{2,6},{3,7},{4,0},{5,1},{6,2},{7,3},{8,12},{9,13},{10,... | collective-permute-start | bytes 58376 | tf_op jit(solution)/shard_map/filter_grad_sum/ppermute | solution.py:176
  118.8 1.5 %collective-permute-done.8 = f32[38,128]{1,0:T(8,128)S(1)} collective-permute-done((f32[38,128]{1,0:T(8,128)S(1)}, f32[38,128]{1,0:T(8,128)S(1)}, u32[]{:S(2)}, u32[]{:S(2)}) %collective-permute-start.8) | collective-permute-done | bytes 19488 | tf_op jit(solution)/shard_map/filter_grad_sum/ppermute | solution.py:176
  120.3 3.0 %collective-permute-start.9 = (f32[38,128]{1,0:T(8,128)S(1)}, f32[38,128]{1,0:T(8,128)S(1)}, u32[]{:S(2)}, u32[]{:S(2)}) collective-permute-start(f32[38,128]{1,0:T(8,128)S(1)} %select_add_fusion.5), channel_id=1, source_target_pairs={{0,4},{1,5},{2,6},{3,7},{4,0},{5,1},{6,2},{7,3},{8,12},{9,13},{10,... | collective-permute-start | bytes 58376 | tf_op jit(solution)/shard_map/filter_grad_sum/ppermute | solution.py:176
  123.3 1.7 %collective-permute-done.9 = f32[38,128]{1,0:T(8,128)S(1)} collective-permute-done((f32[38,128]{1,0:T(8,128)S(1)}, f32[38,128]{1,0:T(8,128)S(1)}, u32[]{:S(2)}, u32[]{:S(2)}) %collective-permute-start.9) | collective-permute-done | bytes 19488 | tf_op jit(solution)/shard_map/filter_grad_sum/ppermute | solution.py:176
  125.0 1.7 %collective-permute-start.10 = (f32[76,128]{1,0:T(8,128)S(1)}, f32[76,128]{1,0:T(8,128)S(1)}, u32[]{:S(2)}, u32[]{:S(2)}) collective-permute-start(f32[76,128]{1,0:T(8,128)S(1)} %maximum_select_fusion.4), channel_id=1, source_target_pairs={{0,2},{1,3},{2,0},{3,1},{4,6},{5,7},{6,4},{7,5},{8,10},{9,11},{10,... | collective-permute-start | bytes 116744 | tf_op jit(solution)/shard_map/filter_grad_sum/ppermute | solution.py:176
  129.1 2.0 %collective-permute-start.11 = (f32[152,128]{1,0:T(8,128)S(1)}, f32[152,128]{1,0:T(8,128)S(1)}, u32[]{:S(2)}, u32[]{:S(2)}) collective-permute-start(f32[152,128]{1,0:T(8,128)S(1)} %maximum_select_fusion.3), channel_id=1, source_target_pairs={{0,16},{8,24},{16,0},{24,8},{1,17},{9,25},{17,1},{25,9},{2,18},{10... | collective-permute-start | bytes 233480 | tf_op jit(solution)/shard_map/filter_grad_sum/ppermute | solution.py:176
  131.3 2.3 %collective-permute-done.11 = f32[152,128]{1,0:T(8,128)S(1)} collective-permute-done((f32[152,128]{1,0:T(8,128)S(1)}, f32[152,128]{1,0:T(8,128)S(1)}, u32[]{:S(2)}, u32[]{:S(2)}) %collective-permute-start.11) | collective-permute-done | bytes 77856 | tf_op jit(solution)/shard_map/filter_grad_sum/ppermute | solution.py:176
  133.6 2.9 %collective-permute-start.12 = (f32[304,128]{1,0:T(8,128)S(1)}, f32[304,128]{1,0:T(8,128)S(1)}, u32[]{:S(2)}, u32[]{:S(2)}) collective-permute-start(f32[304,128]{1,0:T(8,128)S(1)} %maximum_select_fusion.2), channel_id=1, source_target_pairs={{0,8},{8,0},{16,24},{24,16},{1,9},{9,1},{17,25},{25,17},{2,10},{10... | collective-permute-start | bytes 466952 | tf_op jit(solution)/shard_map/filter_grad_sum/ppermute | solution.py:176
  136.5 1.7 %collective-permute-done.3 = f32[3,8,4096]{2,1,0:T(8,128)S(1)} collective-permute-done((f32[3,8,4096]{2,1,0:T(8,128)S(1)}, f32[3,8,4096]{2,1,0:T(8,128)S(1)}, u32[]{:S(2)}, u32[]{:S(2)}) %collective-permute-start.3) | collective-permute-done | bytes 393248 | tf_op jit(solution)/shard_map/ppermute | solution.py:19
  (57 shorter events, 16.4 us)
Async XLA Ops:
  3.2 9.0 %collective-permute-start = (bf16[3,8,4096]{2,1,0:T(8,128)(2,1)S(1)}, bf16[3,8,4096]{2,1,0:T(8,128)(2,1)S(1)}, u32[]{:S(2)}, u32[]{:S(2)}) collective-permute-start(bf16[3,8,4096]{2,1,0:T(8,128)(2,1)S(1)} %pad_maximum_fusion.1), channel_id=1, source_target_pairs={{0,8},{8,16},{16,24},{1,9},{9,17},{17,25},{2,10},{10,18},{18,26},{... | collective-permute-start | bytes 589832 | tf_op jit(solution)/shard_map/ppermute | solution.py:19
  12.2 0.7 copy-start.4
  28.0 14.8 %copy-start.1 = (f32[16,4096]{1,0:T(8,128)S(1)}, f32[16,4096]{1,0:T(8,128)}, u32[]{:S(2)}) copy-start(f32[16,4096]{1,0:T(8,128)} %param.15) | copy-start | bytes 786436
  28.0 14.8 %copy-start.2 = (f32[16,4096]{1,0:T(8,128)S(1)}, f32[16,4096]{1,0:T(8,128)}, u32[]{:S(2)}) copy-start(f32[16,4096]{1,0:T(8,128)} %get-tuple-element.16) | copy-start | bytes 786436
  28.0 14.8 %copy-start.3 = (f32[16,4096]{1,0:T(8,128)S(1)}, f32[16,4096]{1,0:T(8,128)}, u32[]{:S(2)}) copy-start(f32[16,4096]{1,0:T(8,128)} %get-tuple-element.17) | copy-start | bytes 786436
  29.2 13.6 %collective-permute-start.1 = (f32[2,16,4096]{2,1,0:T(8,128)S(1)}, f32[2,16,4096]{2,1,0:T(8,128)S(1)}, u32[]{:S(2)}, u32[]{:S(2)}) collective-permute-start(f32[2,16,4096]{2,1,0:T(8,128)S(1)} %pad_maximum_fusion), channel_id=1, source_target_pairs={{0,8},{8,0},{16,24},{24,16},{1,9},{9,1},{17,25},{25,17},{2,10},{10... | collective-permute-start | bytes 1572872 | tf_op jit(solution)/shard_map/modal_state_scan/ppermute | solution.py:176
  42.9 7.3 %collective-permute-start.2 = (f32[16,4096]{1,0:T(8,128)S(1)}, f32[16,4096]{1,0:T(8,128)S(1)}, u32[]{:S(2)}, u32[]{:S(2)}) collective-permute-start(f32[16,4096]{1,0:T(8,128)S(1)} %select_select_fusion), channel_id=1, source_target_pairs={{0,16},{8,24},{16,0},{24,8},{1,17},{9,25},{17,1},{25,9},{2,18},{10... | collective-permute-start | bytes 786440 | tf_op jit(solution)/shard_map/modal_state_scan/ppermute | solution.py:176
  99.0 1.7 %collective-permute-start.4 = (f32[608,128]{1,0:T(8,128)S(1)}, f32[608,128]{1,0:T(8,128)S(1)}, u32[]{:S(2)}, u32[]{:S(2)}) collective-permute-start(f32[608,128]{1,0:T(8,128)S(1)} %select_n.211), channel_id=1, source_target_pairs={{0,1},{1,0},{2,3},{3,2},{4,5},{5,4},{6,7},{7,6},{8,9},{9,8},{10,11... | collective-permute-start | bytes 933896 | tf_op jit(solution)/shard_map/filter_grad_sum/ppermute | solution.py:176
  100.7 17.7 %copy-start = (f32[3,7,4096]{2,1,0:T(8,128)S(1)}, f32[3,7,4096]{2,1,0:T(8,128)}, u32[]{:S(2)}) copy-start(f32[3,7,4096]{2,1,0:T(8,128)} %taps_ref.3) | copy-start | bytes 1032196
  100.7 6.1 %collective-permute-start.5 = (f32[304,128]{1,0:T(8,128)S(1)}, f32[304,128]{1,0:T(8,128)S(1)}, u32[]{:S(2)}, u32[]{:S(2)}) collective-permute-start(f32[304,128]{1,0:T(8,128)S(1)} %slice_select_fusion.2), channel_id=1, source_target_pairs={{0,8},{8,0},{16,24},{24,16},{1,9},{9,1},{17,25},{25,17},{2,10},{10... | collective-permute-start | bytes 466952 | tf_op jit(solution)/shard_map/filter_grad_sum/ppermute | solution.py:176
  106.9 19.9 %copy-start.6 = (f32[3,8,4096]{2,1,0:T(8,128)S(1)}, f32[3,8,4096]{2,1,0:T(8,128)}, u32[]{:S(2)}) copy-start(f32[3,8,4096]{2,1,0:T(8,128)} %get-tuple-element.21) | copy-start | bytes 1179652
  106.9 4.5 %collective-permute-start.6 = (f32[152,128]{1,0:T(8,128)S(1)}, f32[152,128]{1,0:T(8,128)S(1)}, u32[]{:S(2)}, u32[]{:S(2)}) collective-permute-start(f32[152,128]{1,0:T(8,128)S(1)} %slice_select_fusion.3), channel_id=1, source_target_pairs={{0,16},{8,24},{16,0},{24,8},{1,17},{9,25},{17,1},{25,9},{2,18},{10... | collective-permute-start | bytes 233480 | tf_op jit(solution)/shard_map/filter_grad_sum/ppermute | solution.py:176
  111.4 4.1 %collective-permute-start.7 = (f32[76,128]{1,0:T(8,128)S(1)}, f32[76,128]{1,0:T(8,128)S(1)}, u32[]{:S(2)}, u32[]{:S(2)}) collective-permute-start(f32[76,128]{1,0:T(8,128)S(1)} %slice_select_fusion.4), channel_id=1, source_target_pairs={{0,2},{1,3},{2,0},{3,1},{4,6},{5,7},{6,4},{7,5},{8,10},{9,11},{10,... | collective-permute-start | bytes 116744 | tf_op jit(solution)/shard_map/filter_grad_sum/ppermute | solution.py:176
  115.5 22.7 %copy-start.5 = (f32[3,16,4096]{2,1,0:T(8,128)S(1)}, f32[3,16,4096]{2,1,0:T(8,128)}, u32[]{:S(2)}) copy-start(f32[3,16,4096]{2,1,0:T(8,128)} %get-tuple-element.20) | copy-start | bytes 2359300
  115.5 4.7 %collective-permute-start.8 = (f32[38,128]{1,0:T(8,128)S(1)}, f32[38,128]{1,0:T(8,128)S(1)}, u32[]{:S(2)}, u32[]{:S(2)}) collective-permute-start(f32[38,128]{1,0:T(8,128)S(1)} %slice_select_fusion.5), channel_id=1, source_target_pairs={{0,4},{1,5},{2,6},{3,7},{4,0},{5,1},{6,2},{7,3},{8,12},{9,13},{10,... | collective-permute-start | bytes 58376 | tf_op jit(solution)/shard_map/filter_grad_sum/ppermute | solution.py:176
  120.3 4.7 %collective-permute-start.9 = (f32[38,128]{1,0:T(8,128)S(1)}, f32[38,128]{1,0:T(8,128)S(1)}, u32[]{:S(2)}, u32[]{:S(2)}) collective-permute-start(f32[38,128]{1,0:T(8,128)S(1)} %select_add_fusion.5), channel_id=1, source_target_pairs={{0,4},{1,5},{2,6},{3,7},{4,0},{5,1},{6,2},{7,3},{8,12},{9,13},{10,... | collective-permute-start | bytes 58376 | tf_op jit(solution)/shard_map/filter_grad_sum/ppermute | solution.py:176
  125.0 4.1 %collective-permute-start.10 = (f32[76,128]{1,0:T(8,128)S(1)}, f32[76,128]{1,0:T(8,128)S(1)}, u32[]{:S(2)}, u32[]{:S(2)}) collective-permute-start(f32[76,128]{1,0:T(8,128)S(1)} %maximum_select_fusion.4), channel_id=1, source_target_pairs={{0,2},{1,3},{2,0},{3,1},{4,6},{5,7},{6,4},{7,5},{8,10},{9,11},{10,... | collective-permute-start | bytes 116744 | tf_op jit(solution)/shard_map/filter_grad_sum/ppermute | solution.py:176
  126.9 11.3 %collective-permute-start.3 = (f32[3,8,4096]{2,1,0:T(8,128)S(1)}, f32[3,8,4096]{2,1,0:T(8,128)S(1)}, u32[]{:S(2)}, u32[]{:S(2)}) collective-permute-start(f32[3,8,4096]{2,1,0:T(8,128)S(1)} %copy-done.6), channel_id=1, source_target_pairs={{8,0},{16,8},{24,16},{9,1},{17,9},{25,17},{10,2},{18,10},{26,18},{... | collective-permute-start | bytes 1179656 | tf_op jit(solution)/shard_map/ppermute | solution.py:19
  129.1 4.5 %collective-permute-start.11 = (f32[152,128]{1,0:T(8,128)S(1)}, f32[152,128]{1,0:T(8,128)S(1)}, u32[]{:S(2)}, u32[]{:S(2)}) collective-permute-start(f32[152,128]{1,0:T(8,128)S(1)} %maximum_select_fusion.3), channel_id=1, source_target_pairs={{0,16},{8,24},{16,0},{24,8},{1,17},{9,25},{17,1},{25,9},{2,18},{10... | collective-permute-start | bytes 233480 | tf_op jit(solution)/shard_map/filter_grad_sum/ppermute | solution.py:176
  133.6 6.3 %collective-permute-start.12 = (f32[304,128]{1,0:T(8,128)S(1)}, f32[304,128]{1,0:T(8,128)S(1)}, u32[]{:S(2)}, u32[]{:S(2)}) collective-permute-start(f32[304,128]{1,0:T(8,128)S(1)} %maximum_select_fusion.2), channel_id=1, source_target_pairs={{0,8},{8,0},{16,24},{24,16},{1,9},{9,1},{17,25},{25,17},{2,10},{10... | collective-permute-start | bytes 466952 | tf_op jit(solution)/shard_map/filter_grad_sum/ppermute | solution.py:176
  139.9 1.7 %collective-permute-start.13 = (f32[608,128]{1,0:T(8,128)S(1)}, f32[608,128]{1,0:T(8,128)S(1)}, u32[]{:S(2)}, u32[]{:S(2)}) collective-permute-start(f32[608,128]{1,0:T(8,128)S(1)} %maximum_select_fusion.1), channel_id=1, source_target_pairs={{0,1},{1,0},{2,3},{3,2},{4,5},{5,4},{6,7},{7,6},{8,9},{9,8},{10,11... | collective-permute-start | bytes 933896 | tf_op jit(solution)/shard_map/filter_grad_sum/ppermute | solution.py:176

commit v3 on v2

--- a/solution.py
+++ b/solution.py
@@ -248,9 +248,26 @@
     count = taps.shape[1]
     poles = decay.shape[0]
     q, k, v, c = queries[0], keys[0], values[0], cotangent[0]
-    rim = passed_along(jnp.stack([q[rows - RIM :], k[rows - RIM :], v[rows - RIM :]], 0), "seq", 1)
+    lead = jnp.stack([q[rows - RIM :], k[rows - RIM :], v[rows - RIM :]], 0)
+    rim = passed_along(lead, "seq", 1)
     a = jnp.exp(-decay)
-    f_local, b_local = run_states(q, k, v, c, rim, taps, a)
+    f_bare, b_bare = run_states(q, k, v, c, jnp.zeros_like(lead), taps, a)
+    with jax.named_scope("rim_share_of_states"):
+        first = jnp.stack([q[:RIM], k[:RIM], v[:RIM]], 0).astype(F32)
+
+        def head_feats(before):
+            padded = jnp.concatenate([before, first], 1)
+            return sum(taps[:, lag, None, :] * padded[:, RIM - lag : 2 * RIM - lag] for lag in range(count))
+
+        with_rim = head_feats(rim.astype(F32))
+        without = head_feats(jnp.zeros_like(first))
+        d_product = with_rim[1] * with_rim[2] - without[1] * without[2]
+        d_adjoint = c[:RIM].astype(F32) * (with_rim[0] - without[0])
+        lags = jnp.arange(RIM, dtype=F32)
+        f_local = f_bare + jnp.sum(
+            jnp.exp(-decay[None] * (rows - 1 - lags)[:, None, None]) * d_product[:, None, :], 0
+        )
+        b_local = b_bare + jnp.sum(jnp.exp(-decay[None] * lags[:, None, None]) * d_adjoint[:, None, :], 0)
     with jax.named_scope("modal_state_scan"):
         s_in, g_in = scan_states(f_local, b_local, decay, rows, "seq")
     mixed, gq, gk, gv, tails, heads, grads = run_main(

time: 144 us -> 142 us (0.986)
  starting transfers between devices: 28.5 us -> 26.3 us
    ppermute x12, starting transfers between devices: 22.4 us -> 20.1 us  [exchange(): return lax.ppermute(x, axis, [(i, i ^ size) for i in range(count)])]
    ppermute x2, waiting for transfers between devices: 4.1 us -> 1.99 us  [passed_along(): return lax.ppermute(x, axis, pairs)]
    ppermute x12, waiting for transfers between devices: 35.9 us -> 37.8 us  [exchange(): return lax.ppermute(x, axis, [(i, i ^ size) for i in range(count)])]
    exp x1 -> x0, other arithmetic: 1.7 us -> none  [per_device(): a = jnp.exp(-decay)]
  transfers between devices with their start and end apart: 14 -> 14, of which waited for: 14 -> 13; matrix products, arithmetic and copies ran while one was open for 3% -> 2% of each run, Pallas kernels for 0% -> 11%
where the time goes in v3:
time: 142 us
  Pallas kernels  61.6 us (43%)
  waiting for transfers between devices  39.7 us (28%)
  starting transfers between devices  26.3 us (19%)
  local copies, waits for them, and re-layouts  6.56 us (5%)
  other arithmetic  6.47 us (5%)
    pallas_call x1, Pallas kernels, run_main(): pl.pallas_call(main_kernel, grid=(width // lanes,), in_specs=[tile(x.shap...  46.5 us
    ppermute x12, waiting for transfers between devices, exchange(): return lax.ppermute(x, axis, [(i, i ^ size) for i in range(count)])  37.8 us
    ppermute x12, starting transfers between devices, exchange(): return lax.ppermute(x, axis, [(i, i ^ size) for i in range(count)])  20.1 us
    pallas_call x1, Pallas kernels, run_states(): pl.pallas_call(states_kernel, grid=(width // lanes,), in_specs=[tile(x.sh...  15.1 us
    ppermute x2, starting transfers between devices, passed_along(): return lax.ppermute(x, axis, pairs)  6.16 us
  transfers between devices with their start and end apart: 14, of which 13 were waited for; matrix products, arithmetic and copies ran while one was open for 2% of the time, Pallas kernels for 11%

profile of v3, /device:TPU:0, one launch (start us, length us, event | category | flops | bytes accessed | tf_op | source)
XLA Modules:
  0.0 141.6 jit_solution(11287512903578859740)
XLA Ops:
  2.6 4.9 %collective-permute-start = (bf16[3,8,4096]{2,1,0:T(8,128)(2,1)S(1)}, bf16[3,8,4096]{2,1,0:T(8,128)(2,1)S(1)}, u32[]{:S(2)}, u32[]{:S(2)}) collective-permute-start(bf16[3,8,4096]{2,1,0:T(8,128)(2,1)S(1)} %pad_maximum_fusion.2), channel_id=1, source_target_pairs={{0,8},{8,16},{16,24},{1,9},{9,17},{17,25},{2,10},{10,18},{18,26},{... | collective-permute-start | bytes 589832 | tf_op jit(solution)/shard_map/ppermute | solution.py:19
  9.6 15.1 %shard_map.135 = (f32[16,4096]{1,0:T(8,128)}, f32[16,4096]{1,0:T(8,128)}) custom-call(bf16[128,4096]{1,0:T(8,128)(2,1)} %bitcast.47, bf16[128,4096]{1,0:T(8,128)(2,1)} %bitcast.49, bf16[128,4096]{1,0:T(8,128)(2,1)} %bitcast.51, bf16[128,4096]{1,0:T(8,128)(2,1)} %bitcast.53, bf16[3,8,4096]{2,1,0:T(8,128)(2,1)} %broadcast_in_dim.32.rim_ref, ...), custom_call_target="tpu_custom_call" | custom-call | tf_op jit(solution)/shard_map/pallas_call | solution.py:128
  27.6 1.5 %collective-permute-start.1 = (f32[2,16,4096]{2,1,0:T(8,128)S(1)}, f32[2,16,4096]{2,1,0:T(8,128)S(1)}, u32[]{:S(2)}, u32[]{:S(2)}) collective-permute-start(f32[2,16,4096]{2,1,0:T(8,128)S(1)} %pad_maximum_fusion), channel_id=1, source_target_pairs={{0,8},{8,0},{16,24},{24,16},{1,9},{9,1},{17,25},{25,17},{2,10},{10... | collective-permute-start | bytes 1572872 | tf_op jit(solution)/shard_map/modal_state_scan/ppermute | solution.py:176
  29.2 11.9 %collective-permute-done.1 = f32[2,16,4096]{2,1,0:T(8,128)S(1)} collective-permute-done((f32[2,16,4096]{2,1,0:T(8,128)S(1)}, f32[2,16,4096]{2,1,0:T(8,128)S(1)}, u32[]{:S(2)}, u32[]{:S(2)}) %collective-permute-start.1) | collective-permute-done | bytes 524320 | tf_op jit(solution)/shard_map/modal_state_scan/ppermute | solution.py:176
  41.2 1.6 %collective-permute-start.2 = (f32[16,4096]{1,0:T(8,128)S(1)}, f32[16,4096]{1,0:T(8,128)S(1)}, u32[]{:S(2)}, u32[]{:S(2)}) collective-permute-start(f32[16,4096]{1,0:T(8,128)S(1)} %select_select_fusion), channel_id=1, source_target_pairs={{0,16},{8,24},{16,0},{24,8},{1,17},{9,25},{17,1},{25,9},{2,18},{10... | collective-permute-start | bytes 786440 | tf_op jit(solution)/shard_map/modal_state_scan/ppermute | solution.py:176
  42.8 5.4 %collective-permute-done.2 = f32[16,4096]{1,0:T(8,128)S(1)} collective-permute-done((f32[16,4096]{1,0:T(8,128)S(1)}, f32[16,4096]{1,0:T(8,128)S(1)}, u32[]{:S(2)}, u32[]{:S(2)}) %collective-permute-start.2) | collective-permute-done | bytes 262176 | tf_op jit(solution)/shard_map/modal_state_scan/ppermute | solution.py:176
  49.2 46.5 %shard_map.136 = (bf16[128,4096]{1,0:T(8,128)(2,1)}, bf16[128,4096]{1,0:T(8,128)(2,1)}, bf16[128,4096]{1,0:T(8,128)(2,1)}, bf16[128,4096]{1,0:T(8,128)(2,1)}, f3...) custom-call(bf16[128,4096]{1,0:T(8,128)(2,1)} %bitcast.48, bf16[128,4096]{1,0:T(8,128)(2,1)} %bitcast.50, ...), custom_call_target="tpu_custom_call" | custom-call | tf_op jit(solution)/shard_map/pallas_call | solution.py:157
  97.0 1.5 %collective-permute-done.4 = f32[608,128]{1,0:T(8,128)S(1)} collective-permute-done((f32[608,128]{1,0:T(8,128)S(1)}, f32[608,128]{1,0:T(8,128)S(1)}, u32[]{:S(2)}, u32[]{:S(2)}) %collective-permute-start.4) | collective-permute-done | bytes 311328 | tf_op jit(solution)/shard_map/filter_grad_sum/ppermute | solution.py:176
  98.6 1.5 %collective-permute-start.5 = (f32[304,128]{1,0:T(8,128)S(1)}, f32[304,128]{1,0:T(8,128)S(1)}, u32[]{:S(2)}, u32[]{:S(2)}) collective-permute-start(f32[304,128]{1,0:T(8,128)S(1)} %slice_select_fusion.2), channel_id=1, source_target_pairs={{0,8},{8,0},{16,24},{24,16},{1,9},{9,1},{17,25},{25,17},{2,10},{10... | collective-permute-start | bytes 466952 | tf_op jit(solution)/shard_map/filter_grad_sum/ppermute | solution.py:176
  100.2 4.6 %collective-permute-done.5 = f32[304,128]{1,0:T(8,128)S(1)} collective-permute-done((f32[304,128]{1,0:T(8,128)S(1)}, f32[304,128]{1,0:T(8,128)S(1)}, u32[]{:S(2)}, u32[]{:S(2)}) %collective-permute-start.5) | collective-permute-done | bytes 155680 | tf_op jit(solution)/shard_map/filter_grad_sum/ppermute | solution.py:176
  104.8 1.6 %collective-permute-start.6 = (f32[152,128]{1,0:T(8,128)S(1)}, f32[152,128]{1,0:T(8,128)S(1)}, u32[]{:S(2)}, u32[]{:S(2)}) collective-permute-start(f32[152,128]{1,0:T(8,128)S(1)} %slice_select_fusion.3), channel_id=1, source_target_pairs={{0,16},{8,24},{16,0},{24,8},{1,17},{9,25},{17,1},{25,9},{2,18},{10... | collective-permute-start | bytes 233480 | tf_op jit(solution)/shard_map/filter_grad_sum/ppermute | solution.py:176
  106.4 2.9 %collective-permute-done.6 = f32[152,128]{1,0:T(8,128)S(1)} collective-permute-done((f32[152,128]{1,0:T(8,128)S(1)}, f32[152,128]{1,0:T(8,128)S(1)}, u32[]{:S(2)}, u32[]{:S(2)}) %collective-permute-start.6) | collective-permute-done | bytes 77856 | tf_op jit(solution)/shard_map/filter_grad_sum/ppermute | solution.py:176
  109.3 1.6 %collective-permute-start.7 = (f32[76,128]{1,0:T(8,128)S(1)}, f32[76,128]{1,0:T(8,128)S(1)}, u32[]{:S(2)}, u32[]{:S(2)}) collective-permute-start(f32[76,128]{1,0:T(8,128)S(1)} %slice_select_fusion.4), channel_id=1, source_target_pairs={{0,2},{1,3},{2,0},{3,1},{4,6},{5,7},{6,4},{7,5},{8,10},{9,11},{10,... | collective-permute-start | bytes 116744 | tf_op jit(solution)/shard_map/filter_grad_sum/ppermute | solution.py:176
  111.0 2.4 %collective-permute-done.7 = f32[76,128]{1,0:T(8,128)S(1)} collective-permute-done((f32[76,128]{1,0:T(8,128)S(1)}, f32[76,128]{1,0:T(8,128)S(1)}, u32[]{:S(2)}, u32[]{:S(2)}) %collective-permute-start.7) | collective-permute-done | bytes 38944 | tf_op jit(solution)/shard_map/filter_grad_sum/ppermute | solution.py:176
  113.4 2.9 %collective-permute-start.8 = (f32[38,128]{1,0:T(8,128)S(1)}, f32[38,128]{1,0:T(8,128)S(1)}, u32[]{:S(2)}, u32[]{:S(2)}) collective-permute-start(f32[38,128]{1,0:T(8,128)S(1)} %slice_select_fusion.5), channel_id=1, source_target_pairs={{0,4},{1,5},{2,6},{3,7},{4,0},{5,1},{6,2},{7,3},{8,12},{9,13},{10,... | collective-permute-start | bytes 58376 | tf_op jit(solution)/shard_map/filter_grad_sum/ppermute | solution.py:176
  116.3 1.9 %collective-permute-done.8 = f32[38,128]{1,0:T(8,128)S(1)} collective-permute-done((f32[38,128]{1,0:T(8,128)S(1)}, f32[38,128]{1,0:T(8,128)S(1)}, u32[]{:S(2)}, u32[]{:S(2)}) %collective-permute-start.8) | collective-permute-done | bytes 19488 | tf_op jit(solution)/shard_map/filter_grad_sum/ppermute | solution.py:176
  118.2 3.0 %collective-permute-start.9 = (f32[38,128]{1,0:T(8,128)S(1)}, f32[38,128]{1,0:T(8,128)S(1)}, u32[]{:S(2)}, u32[]{:S(2)}) collective-permute-start(f32[38,128]{1,0:T(8,128)S(1)} %select_add_fusion.5), channel_id=1, source_target_pairs={{0,4},{1,5},{2,6},{3,7},{4,0},{5,1},{6,2},{7,3},{8,12},{9,13},{10,... | collective-permute-start | bytes 58376 | tf_op jit(solution)/shard_map/filter_grad_sum/ppermute | solution.py:176
  121.1 1.8 %collective-permute-done.9 = f32[38,128]{1,0:T(8,128)S(1)} collective-permute-done((f32[38,128]{1,0:T(8,128)S(1)}, f32[38,128]{1,0:T(8,128)S(1)}, u32[]{:S(2)}, u32[]{:S(2)}) %collective-permute-start.9) | collective-permute-done | bytes 19488 | tf_op jit(solution)/shard_map/filter_grad_sum/ppermute | solution.py:176
  122.9 1.7 %collective-permute-start.10 = (f32[76,128]{1,0:T(8,128)S(1)}, f32[76,128]{1,0:T(8,128)S(1)}, u32[]{:S(2)}, u32[]{:S(2)}) collective-permute-start(f32[76,128]{1,0:T(8,128)S(1)} %maximum_select_fusion.4), channel_id=1, source_target_pairs={{0,2},{1,3},{2,0},{3,1},{4,6},{5,7},{6,4},{7,5},{8,10},{9,11},{10,... | collective-permute-start | bytes 116744 | tf_op jit(solution)/shard_map/filter_grad_sum/ppermute | solution.py:176
  124.6 1.3 collective-permute-start.3
  127.0 2.6 %collective-permute-start.11 = (f32[152,128]{1,0:T(8,128)S(1)}, f32[152,128]{1,0:T(8,128)S(1)}, u32[]{:S(2)}, u32[]{:S(2)}) collective-permute-start(f32[152,128]{1,0:T(8,128)S(1)} %maximum_select_fusion.3), channel_id=1, source_target_pairs={{0,16},{8,24},{16,0},{24,8},{1,17},{9,25},{17,1},{25,9},{2,18},{10... | collective-permute-start | bytes 233480 | tf_op jit(solution)/shard_map/filter_grad_sum/ppermute | solution.py:176
  129.6 2.3 %collective-permute-done.11 = f32[152,128]{1,0:T(8,128)S(1)} collective-permute-done((f32[152,128]{1,0:T(8,128)S(1)}, f32[152,128]{1,0:T(8,128)S(1)}, u32[]{:S(2)}, u32[]{:S(2)}) %collective-permute-start.11) | collective-permute-done | bytes 77856 | tf_op jit(solution)/shard_map/filter_grad_sum/ppermute | solution.py:176
  132.0 2.0 %collective-permute-start.12 = (f32[304,128]{1,0:T(8,128)S(1)}, f32[304,128]{1,0:T(8,128)S(1)}, u32[]{:S(2)}, u32[]{:S(2)}) collective-permute-start(f32[304,128]{1,0:T(8,128)S(1)} %maximum_select_fusion.2), channel_id=1, source_target_pairs={{0,8},{8,0},{16,24},{24,16},{1,9},{9,1},{17,25},{25,17},{2,10},{10... | collective-permute-start | bytes 466952 | tf_op jit(solution)/shard_map/filter_grad_sum/ppermute | solution.py:176
  134.0 2.0 %collective-permute-done.3 = f32[3,8,4096]{2,1,0:T(8,128)S(1)} collective-permute-done((f32[3,8,4096]{2,1,0:T(8,128)S(1)}, f32[3,8,4096]{2,1,0:T(8,128)S(1)}, u32[]{:S(2)}, u32[]{:S(2)}) %collective-permute-start.3) | collective-permute-done | bytes 393248 | tf_op jit(solution)/shard_map/ppermute | solution.py:19
  (66 shorter events, 16.2 us)
Async XLA Ops:
  0.6 6.9 %copy-start.1 = (f32[16,4096]{1,0:T(8,128)S(1)}, f32[16,4096]{1,0:T(8,128)}, u32[]{:S(2)}) copy-start(f32[16,4096]{1,0:T(8,128)} %param.15) | copy-start | bytes 786436
  0.6 7.6 %copy-start = (f32[3,7,4096]{2,1,0:T(8,128)S(1)}, f32[3,7,4096]{2,1,0:T(8,128)}, u32[]{:S(2)}) copy-start(f32[3,7,4096]{2,1,0:T(8,128)} %taps_ref.3) | copy-start | bytes 1032196
  2.6 22.1 %collective-permute-start = (bf16[3,8,4096]{2,1,0:T(8,128)(2,1)S(1)}, bf16[3,8,4096]{2,1,0:T(8,128)(2,1)S(1)}, u32[]{:S(2)}, u32[]{:S(2)}) collective-permute-start(bf16[3,8,4096]{2,1,0:T(8,128)(2,1)S(1)} %pad_maximum_fusion.2), channel_id=1, source_target_pairs={{0,8},{8,16},{16,24},{1,9},{9,17},{17,25},{2,10},{10,18},{18,26},{... | collective-permute-start | bytes 589832 | tf_op jit(solution)/shard_map/ppermute | solution.py:19
  24.7 0.9 copy-start.2
  26.5 1.0 copy-start.5
  26.5 1.0 copy-start.4
  27.6 13.4 %collective-permute-start.1 = (f32[2,16,4096]{2,1,0:T(8,128)S(1)}, f32[2,16,4096]{2,1,0:T(8,128)S(1)}, u32[]{:S(2)}, u32[]{:S(2)}) collective-permute-start(f32[2,16,4096]{2,1,0:T(8,128)S(1)} %pad_maximum_fusion), channel_id=1, source_target_pairs={{0,8},{8,0},{16,24},{24,16},{1,9},{9,1},{17,25},{25,17},{2,10},{10... | collective-permute-start | bytes 1572872 | tf_op jit(solution)/shard_map/modal_state_scan/ppermute | solution.py:176
  41.2 7.0 %collective-permute-start.2 = (f32[16,4096]{1,0:T(8,128)S(1)}, f32[16,4096]{1,0:T(8,128)S(1)}, u32[]{:S(2)}, u32[]{:S(2)}) collective-permute-start(f32[16,4096]{1,0:T(8,128)S(1)} %select_select_fusion), channel_id=1, source_target_pairs={{0,16},{8,24},{16,0},{24,8},{1,17},{9,25},{17,1},{25,9},{2,18},{10... | collective-permute-start | bytes 786440 | tf_op jit(solution)/shard_map/modal_state_scan/ppermute | solution.py:176
  96.9 1.7 %collective-permute-start.4 = (f32[608,128]{1,0:T(8,128)S(1)}, f32[608,128]{1,0:T(8,128)S(1)}, u32[]{:S(2)}, u32[]{:S(2)}) collective-permute-start(f32[608,128]{1,0:T(8,128)S(1)} %select_n.211), channel_id=1, source_target_pairs={{0,1},{1,0},{2,3},{3,2},{4,5},{5,4},{6,7},{7,6},{8,9},{9,8},{10,11... | collective-permute-start | bytes 933896 | tf_op jit(solution)/shard_map/filter_grad_sum/ppermute | solution.py:176
  98.6 26.0 %copy-start.6 = (f32[3,8,4096]{2,1,0:T(8,128)S(1)}, f32[3,8,4096]{2,1,0:T(8,128)}, u32[]{:S(2)}) copy-start(f32[3,8,4096]{2,1,0:T(8,128)} %get-tuple-element.21) | copy-start | bytes 1179652
  98.6 37.3 %copy-start.3 = (f32[3,16,4096]{2,1,0:T(8,128)S(1)}, f32[3,16,4096]{2,1,0:T(8,128)}, u32[]{:S(2)}) copy-start(f32[3,16,4096]{2,1,0:T(8,128)} %get-tuple-element.20) | copy-start | bytes 2359300
  98.6 6.1 %collective-permute-start.5 = (f32[304,128]{1,0:T(8,128)S(1)}, f32[304,128]{1,0:T(8,128)S(1)}, u32[]{:S(2)}, u32[]{:S(2)}) collective-permute-start(f32[304,128]{1,0:T(8,128)S(1)} %slice_select_fusion.2), channel_id=1, source_target_pairs={{0,8},{8,0},{16,24},{24,16},{1,9},{9,1},{17,25},{25,17},{2,10},{10... | collective-permute-start | bytes 466952 | tf_op jit(solution)/shard_map/filter_grad_sum/ppermute | solution.py:176
  104.8 4.5 %collective-permute-start.6 = (f32[152,128]{1,0:T(8,128)S(1)}, f32[152,128]{1,0:T(8,128)S(1)}, u32[]{:S(2)}, u32[]{:S(2)}) collective-permute-start(f32[152,128]{1,0:T(8,128)S(1)} %slice_select_fusion.3), channel_id=1, source_target_pairs={{0,16},{8,24},{16,0},{24,8},{1,17},{9,25},{17,1},{25,9},{2,18},{10... | collective-permute-start | bytes 233480 | tf_op jit(solution)/shard_map/filter_grad_sum/ppermute | solution.py:176
  109.3 4.1 %collective-permute-start.7 = (f32[76,128]{1,0:T(8,128)S(1)}, f32[76,128]{1,0:T(8,128)S(1)}, u32[]{:S(2)}, u32[]{:S(2)}) collective-permute-start(f32[76,128]{1,0:T(8,128)S(1)} %slice_select_fusion.4), channel_id=1, source_target_pairs={{0,2},{1,3},{2,0},{3,1},{4,6},{5,7},{6,4},{7,5},{8,10},{9,11},{10,... | collective-permute-start | bytes 116744 | tf_op jit(solution)/shard_map/filter_grad_sum/ppermute | solution.py:176
  113.4 4.7 %collective-permute-start.8 = (f32[38,128]{1,0:T(8,128)S(1)}, f32[38,128]{1,0:T(8,128)S(1)}, u32[]{:S(2)}, u32[]{:S(2)}) collective-permute-start(f32[38,128]{1,0:T(8,128)S(1)} %slice_select_fusion.5), channel_id=1, source_target_pairs={{0,4},{1,5},{2,6},{3,7},{4,0},{5,1},{6,2},{7,3},{8,12},{9,13},{10,... | collective-permute-start | bytes 58376 | tf_op jit(solution)/shard_map/filter_grad_sum/ppermute | solution.py:176
  118.2 4.7 %collective-permute-start.9 = (f32[38,128]{1,0:T(8,128)S(1)}, f32[38,128]{1,0:T(8,128)S(1)}, u32[]{:S(2)}, u32[]{:S(2)}) collective-permute-start(f32[38,128]{1,0:T(8,128)S(1)} %select_add_fusion.5), channel_id=1, source_target_pairs={{0,4},{1,5},{2,6},{3,7},{4,0},{5,1},{6,2},{7,3},{8,12},{9,13},{10,... | collective-permute-start | bytes 58376 | tf_op jit(solution)/shard_map/filter_grad_sum/ppermute | solution.py:176
  122.9 4.1 %collective-permute-start.10 = (f32[76,128]{1,0:T(8,128)S(1)}, f32[76,128]{1,0:T(8,128)S(1)}, u32[]{:S(2)}, u32[]{:S(2)}) collective-permute-start(f32[76,128]{1,0:T(8,128)S(1)} %maximum_select_fusion.4), channel_id=1, source_target_pairs={{0,2},{1,3},{2,0},{3,1},{4,6},{5,7},{6,4},{7,5},{8,10},{9,11},{10,... | collective-permute-start | bytes 116744 | tf_op jit(solution)/shard_map/filter_grad_sum/ppermute | solution.py:176
  124.6 11.3 %collective-permute-start.3 = (f32[3,8,4096]{2,1,0:T(8,128)S(1)}, f32[3,8,4096]{2,1,0:T(8,128)S(1)}, u32[]{:S(2)}, u32[]{:S(2)}) collective-permute-start(f32[3,8,4096]{2,1,0:T(8,128)S(1)} %copy-done.6), channel_id=1, source_target_pairs={{8,0},{16,8},{24,16},{9,1},{17,9},{25,17},{10,2},{18,10},{26,18},{... | collective-permute-start | bytes 1179656 | tf_op jit(solution)/shard_map/ppermute | solution.py:19
  127.0 4.9 %collective-permute-start.11 = (f32[152,128]{1,0:T(8,128)S(1)}, f32[152,128]{1,0:T(8,128)S(1)}, u32[]{:S(2)}, u32[]{:S(2)}) collective-permute-start(f32[152,128]{1,0:T(8,128)S(1)} %maximum_select_fusion.3), channel_id=1, source_target_pairs={{0,16},{8,24},{16,0},{24,8},{1,17},{9,25},{17,1},{25,9},{2,18},{10... | collective-permute-start | bytes 233480 | tf_op jit(solution)/shard_map/filter_grad_sum/ppermute | solution.py:176
  132.0 5.7 %collective-permute-start.12 = (f32[304,128]{1,0:T(8,128)S(1)}, f32[304,128]{1,0:T(8,128)S(1)}, u32[]{:S(2)}, u32[]{:S(2)}) collective-permute-start(f32[304,128]{1,0:T(8,128)S(1)} %maximum_select_fusion.2), channel_id=1, source_target_pairs={{0,8},{8,0},{16,24},{24,16},{1,9},{9,1},{17,25},{25,17},{2,10},{10... | collective-permute-start | bytes 466952 | tf_op jit(solution)/shard_map/filter_grad_sum/ppermute | solution.py:176
  137.7 1.7 %collective-permute-start.13 = (f32[608,128]{1,0:T(8,128)S(1)}, f32[608,128]{1,0:T(8,128)S(1)}, u32[]{:S(2)}, u32[]{:S(2)}) collective-permute-start(f32[608,128]{1,0:T(8,128)S(1)} %maximum_select_fusion.1), channel_id=1, source_target_pairs={{0,1},{1,0},{2,3},{3,2},{4,5},{5,4},{6,7},{7,6},{8,9},{9,8},{10,11... | collective-permute-start | bytes 933896 | tf_op jit(solution)/shard_map/filter_grad_sum/ppermute | solution.py:176

commit v4 on v3

--- a/solution.py
+++ b/solution.py
@@ -10,6 +10,7 @@
 LANES = 512
 RIM = 8
 TAIL = 16
+BR = 16
 F32 = jnp.float32
 
 
@@ -19,29 +20,30 @@
     return lax.ppermute(x, axis, pairs)
 
 
-def load_padded(x_ref, rim_ref, pad_ref, s):
-    rows = x_ref.shape[0]
-    pad_ref[s, 0:RIM, :] = rim_ref[s].astype(F32)
-    pad_ref[s, RIM : RIM + rows, :] = x_ref[...].astype(F32)
-
-
-def featurize(pad_ref, taps_ref, s, rows):
+def fill_rows(x_refs, pad_ref, lo):
+    for s, x_ref in enumerate(x_refs):
+        pad_ref[s, RIM + lo : RIM + lo + BR, :] = x_ref[lo : lo + BR, :].astype(F32)
+
+
+def block_feature(pad_ref, taps_ref, s, lo):
     count = taps_ref.shape[1]
-    total = taps_ref[s, 0:1, :] * pad_ref[s, RIM : RIM + rows, :]
+    total = taps_ref[s, 0:1, :] * pad_ref[s, RIM + lo : RIM + lo + BR, :]
     for lag in range(1, count):
-        total = total + taps_ref[s, lag : lag + 1, :] * pad_ref[s, RIM - lag : RIM - lag + rows, :]
+        total = total + taps_ref[s, lag : lag + 1, :] * pad_ref[s, RIM + lo - lag : RIM + lo - lag + BR, :]
     return total
 
 
 def states_kernel(q_ref, k_ref, v_ref, c_ref, rim_ref, taps_ref, a_ref, f_ref, b_ref, pad_ref, p_ref, z_ref):
     rows = q_ref.shape[0]
-    for s, x_ref in enumerate((q_ref, k_ref, v_ref)):
-        load_padded(x_ref, rim_ref, pad_ref, s)
-    fq = featurize(pad_ref, taps_ref, 0, rows)
-    fk = featurize(pad_ref, taps_ref, 1, rows)
-    fv = featurize(pad_ref, taps_ref, 2, rows)
-    p_ref[...] = fk * fv
-    z_ref[...] = c_ref[...].astype(F32) * fq
+    for s in range(3):
+        pad_ref[s, 0:RIM, :] = rim_ref[s].astype(F32)
+    for lo in range(0, rows, BR):
+        fill_rows((q_ref, k_ref, v_ref), pad_ref, lo)
+        fq = block_feature(pad_ref, taps_ref, 0, lo)
+        fk = block_feature(pad_ref, taps_ref, 1, lo)
+        fv = block_feature(pad_ref, taps_ref, 2, lo)
+        p_ref[lo : lo + BR, :] = fk * fv
+        z_ref[lo : lo + BR, :] = c_ref[lo : lo + BR, :].astype(F32) * fq
     a = a_ref[...]
 
     def step(i, carry):
@@ -56,22 +58,35 @@
     b_ref[...] = g
 
 
+def fold(x):
+    return x[0:8] + x[8:16]
+
+
 def main_kernel(
     q_ref, k_ref, v_ref, c_ref, rim_ref, taps_ref, a_ref, r_ref, skip_ref, s_ref, g_ref,
     mixed_ref, gq_ref, gk_ref, gv_ref, tail_ref, head_ref, grads_ref,
-    pad_ref, p_ref, z_ref, y_ref, u_ref, adj_ref,
+    pad_ref, p_ref, z_ref, y_ref, u_ref, adj_ref, feat_ref,
 ):
     rows = q_ref.shape[0]
     count = taps_ref.shape[1]
     poles = a_ref.shape[0]
-    for s, x_ref in enumerate((q_ref, k_ref, v_ref)):
-        load_padded(x_ref, rim_ref, pad_ref, s)
-    fq = featurize(pad_ref, taps_ref, 0, rows)
-    fk = featurize(pad_ref, taps_ref, 1, rows)
-    fv = featurize(pad_ref, taps_ref, 2, rows)
-    cot = c_ref[...].astype(F32)
-    p_ref[...] = fk * fv
-    z_ref[...] = cot * fq
+    lanes = q_ref.shape[1]
+    for s in range(3):
+        pad_ref[s, 0:RIM, :] = rim_ref[s].astype(F32)
+    skip_sum = jnp.zeros((8, lanes), F32)
+    for lo in range(0, rows, BR):
+        fill_rows((q_ref, k_ref, v_ref), pad_ref, lo)
+        fq = block_feature(pad_ref, taps_ref, 0, lo)
+        fk = block_feature(pad_ref, taps_ref, 1, lo)
+        fv = block_feature(pad_ref, taps_ref, 2, lo)
+        feat_ref[0, lo : lo + BR, :] = fq
+        feat_ref[1, lo : lo + BR, :] = fk
+        feat_ref[2, lo : lo + BR, :] = fv
+        p = fk * fv
+        z = c_ref[lo : lo + BR, :].astype(F32) * fq
+        p_ref[lo : lo + BR, :] = p
+        z_ref[lo : lo + BR, :] = z
+        skip_sum = skip_sum + fold(z * p)
     a = a_ref[...]
     r = r_ref[...]
 
@@ -89,30 +104,41 @@
         0, rows, step, (s_ref[...], g_ref[...], jnp.zeros_like(a)), unroll=8
     )
     skip = skip_ref[...]
-    p = p_ref[...]
-    z = z_ref[...]
-    conv = y_ref[...] + skip * p
-    mixed_ref[...] = (fq * conv).astype(mixed_ref.dtype)
-    adj_u = u_ref[...] + skip * z
-    adjoints = (cot * conv, adj_u * fv, adj_u * fk)
-    zeros_rim = jnp.zeros((RIM, adj_ref.shape[2]), F32)
+    for lo in range(0, rows, BR):
+        fq = feat_ref[0, lo : lo + BR, :]
+        conv = y_ref[lo : lo + BR, :] + skip * p_ref[lo : lo + BR, :]
+        mixed_ref[lo : lo + BR, :] = (fq * conv).astype(mixed_ref.dtype)
+        adj_u = u_ref[lo : lo + BR, :] + skip * z_ref[lo : lo + BR, :]
+        adj_ref[0, lo : lo + BR, :] = c_ref[lo : lo + BR, :].astype(F32) * conv
+        adj_ref[1, lo : lo + BR, :] = adj_u * feat_ref[2, lo : lo + BR, :]
+        adj_ref[2, lo : lo + BR, :] = adj_u * feat_ref[1, lo : lo + BR, :]
+    zeros_rim = jnp.zeros((RIM, lanes), F32)
     outs = (gq_ref, gk_ref, gv_ref)
     for s in range(3):
-        adj_ref[s, 0:rows, :] = adjoints[s]
         adj_ref[s, rows : rows + RIM, :] = zeros_rim
-        head_ref[s] = adjoints[s][0:RIM]
-        total = taps_ref[s, 0:1, :] * adjoints[s]
-        for lag in range(1, count):
-            total = total + taps_ref[s, lag : lag + 1, :] * adj_ref[s, lag : lag + rows, :]
-        outs[s][...] = total.astype(outs[s].dtype)
-        tail_ref[s] = total[rows - TAIL : rows]
+        head_ref[s] = adj_ref[s, 0:RIM, :]
+        sums = [jnp.zeros((8, lanes), F32) for _ in range(count)]
+        for lo in range(0, rows, BR):
+            x = pad_ref[s, RIM + lo : RIM + lo + BR, :]
+            total = None
+            for lag in range(count):
+                window = adj_ref[s, lo + lag : lo + lag + BR, :]
+                term = taps_ref[s, lag : lag + 1, :] * window
+                total = term if total is None else total + term
+                sums[lag] = sums[lag] + fold(window * x)
+            outs[s][lo : lo + BR, :] = total.astype(outs[s].dtype)
+            if lo + BR == rows:
+                tail_ref[s] = total[BR - TAIL :]
         for lag in range(count):
-            window = pad_ref[s, RIM - lag : RIM - lag + rows, :]
+            value = jnp.sum(sums[lag], axis=0, keepdims=True)
+            if lag > 0:
+                edge = adj_ref[s, 0:lag, :] * pad_ref[s, RIM - lag : RIM, :]
+                value = value + jnp.sum(edge, axis=0, keepdims=True)
             row = s * count + lag
-            grads_ref[row : row + 1, :] = jnp.sum(adjoints[s] * window, axis=0, keepdims=True)
+            grads_ref[row : row + 1, :] = value
     base = 3 * count
     grads_ref[base : base + poles, :] = acc
-    grads_ref[base + poles : base + poles + 1, :] = jnp.sum(z * p, axis=0, keepdims=True)
+    grads_ref[base + poles : base + poles + 1, :] = jnp.sum(skip_sum, axis=0, keepdims=True)
 
 
 def tile(shape, lanes):
@@ -167,6 +193,7 @@
             pltpu.VMEM((rows, lanes), F32),
             pltpu.VMEM((rows, lanes), F32),
             pltpu.VMEM((3, rows + RIM, lanes), F32),
+            pltpu.VMEM((3, rows, lanes), F32),
         ],
     )(*ins)
 

time: 142 us -> 139 us (0.979)
  Pallas kernels: 61.6 us -> 58.4 us
    pallas_call x1, Pallas kernels: 46.5 us -> 44.7 us  [run_main(): pl.pallas_call(main_kernel, grid=(width // lanes,), in_specs=[tile(x.shap...]
  transfers between devices with their start and end apart: 14 -> 14, of which waited for: 13 -> 13; matrix products, arithmetic and copies ran while one was open for 2% -> 2% of each run, Pallas kernels for 11% -> 10%
where the time goes in v4:
time: 139 us; the launch traced here: 138 us
  Pallas kernels  58.4 us (42%)
  waiting for transfers between devices  39.7 us (29%)
  starting transfers between devices  26.3 us (19%)
  local copies, waits for them, and re-layouts  6.56 us (5%)
  other arithmetic  6.47 us (5%)
    pallas_call x1, Pallas kernels, run_main(): pl.pallas_call(main_kernel, grid=(width // lanes,), in_specs=[tile(x.shap...  44.7 us
    ppermute x12, waiting for transfers between devices, exchange(): return lax.ppermute(x, axis, [(i, i ^ size) for i in range(count)])  37.8 us
    ppermute x12, starting transfers between devices, exchange(): return lax.ppermute(x, axis, [(i, i ^ size) for i in range(count)])  20.1 us
    pallas_call x1, Pallas kernels, run_states(): pl.pallas_call(states_kernel, grid=(width // lanes,), in_specs=[tile(x.sh...  13.7 us
    ppermute x2, starting transfers between devices, passed_along(): return lax.ppermute(x, axis, pairs)  6.16 us
  transfers between devices with their start and end apart: 14, of which 13 were waited for; matrix products, arithmetic and copies ran while one was open for 2% of the time, Pallas kernels for 10%

profile of v4, /device:TPU:0, one launch (start us, length us, event | category | flops | bytes accessed | tf_op | source)
XLA Modules:
  0.0 138.5 jit_solution(15081076894345324672)
XLA Ops:
  2.6 4.9 %collective-permute-start = (bf16[3,8,4096]{2,1,0:T(8,128)(2,1)S(1)}, bf16[3,8,4096]{2,1,0:T(8,128)(2,1)S(1)}, u32[]{:S(2)}, u32[]{:S(2)}) collective-permute-start(bf16[3,8,4096]{2,1,0:T(8,128)(2,1)S(1)} %pad_maximum_fusion.2), channel_id=1, source_target_pairs={{0,8},{8,16},{16,24},{1,9},{9,17},{17,25},{2,10},{10,18},{18,26},{... | collective-permute-start | bytes 589832 | tf_op jit(solution)/shard_map/ppermute | solution.py:20
  9.6 13.7 %shard_map.135 = (f32[16,4096]{1,0:T(8,128)}, f32[16,4096]{1,0:T(8,128)}) custom-call(bf16[128,4096]{1,0:T(8,128)(2,1)} %bitcast.47, bf16[128,4096]{1,0:T(8,128)(2,1)} %bitcast.49, bf16[128,4096]{1,0:T(8,128)(2,1)} %bitcast.51, bf16[128,4096]{1,0:T(8,128)(2,1)} %bitcast.53, bf16[3,8,4096]{2,1,0:T(8,128)(2,1)} %broadcast_in_dim.32.rim_ref, ...), custom_call_target="tpu_custom_call" | custom-call | tf_op jit(solution)/shard_map/pallas_call | solution.py:154
  26.2 1.5 %collective-permute-start.1 = (f32[2,16,4096]{2,1,0:T(8,128)S(1)}, f32[2,16,4096]{2,1,0:T(8,128)S(1)}, u32[]{:S(2)}, u32[]{:S(2)}) collective-permute-start(f32[2,16,4096]{2,1,0:T(8,128)S(1)} %pad_maximum_fusion), channel_id=1, source_target_pairs={{0,8},{8,0},{16,24},{24,16},{1,9},{9,1},{17,25},{25,17},{2,10},{10... | collective-permute-start | bytes 1572872 | tf_op jit(solution)/shard_map/modal_state_scan/ppermute | solution.py:203
  27.8 11.9 %collective-permute-done.1 = f32[2,16,4096]{2,1,0:T(8,128)S(1)} collective-permute-done((f32[2,16,4096]{2,1,0:T(8,128)S(1)}, f32[2,16,4096]{2,1,0:T(8,128)S(1)}, u32[]{:S(2)}, u32[]{:S(2)}) %collective-permute-start.1) | collective-permute-done | bytes 524320 | tf_op jit(solution)/shard_map/modal_state_scan/ppermute | solution.py:203
  39.8 1.6 %collective-permute-start.2 = (f32[16,4096]{1,0:T(8,128)S(1)}, f32[16,4096]{1,0:T(8,128)S(1)}, u32[]{:S(2)}, u32[]{:S(2)}) collective-permute-start(f32[16,4096]{1,0:T(8,128)S(1)} %select_select_fusion), channel_id=1, source_target_pairs={{0,16},{8,24},{16,0},{24,8},{1,17},{9,25},{17,1},{25,9},{2,18},{10... | collective-permute-start | bytes 786440 | tf_op jit(solution)/shard_map/modal_state_scan/ppermute | solution.py:203
  41.4 5.4 %collective-permute-done.2 = f32[16,4096]{1,0:T(8,128)S(1)} collective-permute-done((f32[16,4096]{1,0:T(8,128)S(1)}, f32[16,4096]{1,0:T(8,128)S(1)}, u32[]{:S(2)}, u32[]{:S(2)}) %collective-permute-start.2) | collective-permute-done | bytes 262176 | tf_op jit(solution)/shard_map/modal_state_scan/ppermute | solution.py:203
  47.8 44.7 %shard_map.136 = (bf16[128,4096]{1,0:T(8,128)(2,1)}, bf16[128,4096]{1,0:T(8,128)(2,1)}, bf16[128,4096]{1,0:T(8,128)(2,1)}, bf16[128,4096]{1,0:T(8,128)(2,1)}, f3...) custom-call(bf16[128,4096]{1,0:T(8,128)(2,1)} %bitcast.48, bf16[128,4096]{1,0:T(8,128)(2,1)} %bitcast.50, ...), custom_call_target="tpu_custom_call" | custom-call | tf_op jit(solution)/shard_map/pallas_call | solution.py:183
  93.9 1.5 %collective-permute-done.4 = f32[608,128]{1,0:T(8,128)S(1)} collective-permute-done((f32[608,128]{1,0:T(8,128)S(1)}, f32[608,128]{1,0:T(8,128)S(1)}, u32[]{:S(2)}, u32[]{:S(2)}) %collective-permute-start.4) | collective-permute-done | bytes 311328 | tf_op jit(solution)/shard_map/filter_grad_sum/ppermute | solution.py:203
  95.5 1.5 %collective-permute-start.5 = (f32[304,128]{1,0:T(8,128)S(1)}, f32[304,128]{1,0:T(8,128)S(1)}, u32[]{:S(2)}, u32[]{:S(2)}) collective-permute-start(f32[304,128]{1,0:T(8,128)S(1)} %slice_select_fusion.2), channel_id=1, source_target_pairs={{0,8},{8,0},{16,24},{24,16},{1,9},{9,1},{17,25},{25,17},{2,10},{10... | collective-permute-start | bytes 466952 | tf_op jit(solution)/shard_map/filter_grad_sum/ppermute | solution.py:203
  97.0 4.6 %collective-permute-done.5 = f32[304,128]{1,0:T(8,128)S(1)} collective-permute-done((f32[304,128]{1,0:T(8,128)S(1)}, f32[304,128]{1,0:T(8,128)S(1)}, u32[]{:S(2)}, u32[]{:S(2)}) %collective-permute-start.5) | collective-permute-done | bytes 155680 | tf_op jit(solution)/shard_map/filter_grad_sum/ppermute | solution.py:203
  101.7 1.6 %collective-permute-start.6 = (f32[152,128]{1,0:T(8,128)S(1)}, f32[152,128]{1,0:T(8,128)S(1)}, u32[]{:S(2)}, u32[]{:S(2)}) collective-permute-start(f32[152,128]{1,0:T(8,128)S(1)} %slice_select_fusion.3), channel_id=1, source_target_pairs={{0,16},{8,24},{16,0},{24,8},{1,17},{9,25},{17,1},{25,9},{2,18},{10... | collective-permute-start | bytes 233480 | tf_op jit(solution)/shard_map/filter_grad_sum/ppermute | solution.py:203
  103.3 2.9 %collective-permute-done.6 = f32[152,128]{1,0:T(8,128)S(1)} collective-permute-done((f32[152,128]{1,0:T(8,128)S(1)}, f32[152,128]{1,0:T(8,128)S(1)}, u32[]{:S(2)}, u32[]{:S(2)}) %collective-permute-start.6) | collective-permute-done | bytes 77856 | tf_op jit(solution)/shard_map/filter_grad_sum/ppermute | solution.py:203
  106.2 1.6 %collective-permute-start.7 = (f32[76,128]{1,0:T(8,128)S(1)}, f32[76,128]{1,0:T(8,128)S(1)}, u32[]{:S(2)}, u32[]{:S(2)}) collective-permute-start(f32[76,128]{1,0:T(8,128)S(1)} %slice_select_fusion.4), channel_id=1, source_target_pairs={{0,2},{1,3},{2,0},{3,1},{4,6},{5,7},{6,4},{7,5},{8,10},{9,11},{10,... | collective-permute-start | bytes 116744 | tf_op jit(solution)/shard_map/filter_grad_sum/ppermute | solution.py:203
  107.8 2.4 %collective-permute-done.7 = f32[76,128]{1,0:T(8,128)S(1)} collective-permute-done((f32[76,128]{1,0:T(8,128)S(1)}, f32[76,128]{1,0:T(8,128)S(1)}, u32[]{:S(2)}, u32[]{:S(2)}) %collective-permute-start.7) | collective-permute-done | bytes 38944 | tf_op jit(solution)/shard_map/filter_grad_sum/ppermute | solution.py:203
  110.3 2.9 %collective-permute-start.8 = (f32[38,128]{1,0:T(8,128)S(1)}, f32[38,128]{1,0:T(8,128)S(1)}, u32[]{:S(2)}, u32[]{:S(2)}) collective-permute-start(f32[38,128]{1,0:T(8,128)S(1)} %slice_select_fusion.5), channel_id=1, source_target_pairs={{0,4},{1,5},{2,6},{3,7},{4,0},{5,1},{6,2},{7,3},{8,12},{9,13},{10,... | collective-permute-start | bytes 58376 | tf_op jit(solution)/shard_map/filter_grad_sum/ppermute | solution.py:203
  113.1 1.9 %collective-permute-done.8 = f32[38,128]{1,0:T(8,128)S(1)} collective-permute-done((f32[38,128]{1,0:T(8,128)S(1)}, f32[38,128]{1,0:T(8,128)S(1)}, u32[]{:S(2)}, u32[]{:S(2)}) %collective-permute-start.8) | collective-permute-done | bytes 19488 | tf_op jit(solution)/shard_map/filter_grad_sum/ppermute | solution.py:203
  115.0 3.0 %collective-permute-start.9 = (f32[38,128]{1,0:T(8,128)S(1)}, f32[38,128]{1,0:T(8,128)S(1)}, u32[]{:S(2)}, u32[]{:S(2)}) collective-permute-start(f32[38,128]{1,0:T(8,128)S(1)} %select_add_fusion.5), channel_id=1, source_target_pairs={{0,4},{1,5},{2,6},{3,7},{4,0},{5,1},{6,2},{7,3},{8,12},{9,13},{10,... | collective-permute-start | bytes 58376 | tf_op jit(solution)/shard_map/filter_grad_sum/ppermute | solution.py:203
  118.0 1.8 %collective-permute-done.9 = f32[38,128]{1,0:T(8,128)S(1)} collective-permute-done((f32[38,128]{1,0:T(8,128)S(1)}, f32[38,128]{1,0:T(8,128)S(1)}, u32[]{:S(2)}, u32[]{:S(2)}) %collective-permute-start.9) | collective-permute-done | bytes 19488 | tf_op jit(solution)/shard_map/filter_grad_sum/ppermute | solution.py:203
  119.8 1.7 %collective-permute-start.10 = (f32[76,128]{1,0:T(8,128)S(1)}, f32[76,128]{1,0:T(8,128)S(1)}, u32[]{:S(2)}, u32[]{:S(2)}) collective-permute-start(f32[76,128]{1,0:T(8,128)S(1)} %maximum_select_fusion.4), channel_id=1, source_target_pairs={{0,2},{1,3},{2,0},{3,1},{4,6},{5,7},{6,4},{7,5},{8,10},{9,11},{10,... | collective-permute-start | bytes 116744 | tf_op jit(solution)/shard_map/filter_grad_sum/ppermute | solution.py:203
  121.5 1.3 collective-permute-start.3
  123.9 2.6 %collective-permute-start.11 = (f32[152,128]{1,0:T(8,128)S(1)}, f32[152,128]{1,0:T(8,128)S(1)}, u32[]{:S(2)}, u32[]{:S(2)}) collective-permute-start(f32[152,128]{1,0:T(8,128)S(1)} %maximum_select_fusion.3), channel_id=1, source_target_pairs={{0,16},{8,24},{16,0},{24,8},{1,17},{9,25},{17,1},{25,9},{2,18},{10... | collective-permute-start | bytes 233480 | tf_op jit(solution)/shard_map/filter_grad_sum/ppermute | solution.py:203
  126.5 2.3 %collective-permute-done.11 = f32[152,128]{1,0:T(8,128)S(1)} collective-permute-done((f32[152,128]{1,0:T(8,128)S(1)}, f32[152,128]{1,0:T(8,128)S(1)}, u32[]{:S(2)}, u32[]{:S(2)}) %collective-permute-start.11) | collective-permute-done | bytes 77856 | tf_op jit(solution)/shard_map/filter_grad_sum/ppermute | solution.py:203
  128.8 2.0 %collective-permute-start.12 = (f32[304,128]{1,0:T(8,128)S(1)}, f32[304,128]{1,0:T(8,128)S(1)}, u32[]{:S(2)}, u32[]{:S(2)}) collective-permute-start(f32[304,128]{1,0:T(8,128)S(1)} %maximum_select_fusion.2), channel_id=1, source_target_pairs={{0,8},{8,0},{16,24},{24,16},{1,9},{9,1},{17,25},{25,17},{2,10},{10... | collective-permute-start | bytes 466952 | tf_op jit(solution)/shard_map/filter_grad_sum/ppermute | solution.py:203
  130.8 2.0 %collective-permute-done.3 = f32[3,8,4096]{2,1,0:T(8,128)S(1)} collective-permute-done((f32[3,8,4096]{2,1,0:T(8,128)S(1)}, f32[3,8,4096]{2,1,0:T(8,128)S(1)}, u32[]{:S(2)}, u32[]{:S(2)}) %collective-permute-start.3) | collective-permute-done | bytes 393248 | tf_op jit(solution)/shard_map/ppermute | solution.py:20
  (66 shorter events, 16.2 us)
Async XLA Ops:
  0.6 6.9 %copy-start.1 = (f32[16,4096]{1,0:T(8,128)S(1)}, f32[16,4096]{1,0:T(8,128)}, u32[]{:S(2)}) copy-start(f32[16,4096]{1,0:T(8,128)} %param.15) | copy-start | bytes 786436
  0.6 7.6 %copy-start = (f32[3,7,4096]{2,1,0:T(8,128)S(1)}, f32[3,7,4096]{2,1,0:T(8,128)}, u32[]{:S(2)}) copy-start(f32[3,7,4096]{2,1,0:T(8,128)} %taps_ref.3) | copy-start | bytes 1032196
  2.6 20.7 %collective-permute-start = (bf16[3,8,4096]{2,1,0:T(8,128)(2,1)S(1)}, bf16[3,8,4096]{2,1,0:T(8,128)(2,1)S(1)}, u32[]{:S(2)}, u32[]{:S(2)}) collective-permute-start(bf16[3,8,4096]{2,1,0:T(8,128)(2,1)S(1)} %pad_maximum_fusion.2), channel_id=1, source_target_pairs={{0,8},{8,16},{16,24},{1,9},{9,17},{17,25},{2,10},{10,18},{18,26},{... | collective-permute-start | bytes 589832 | tf_op jit(solution)/shard_map/ppermute | solution.py:20
  23.3 0.9 copy-start.2
  25.1 1.0 copy-start.5
  25.1 1.0 copy-start.4
  26.2 13.4 %collective-permute-start.1 = (f32[2,16,4096]{2,1,0:T(8,128)S(1)}, f32[2,16,4096]{2,1,0:T(8,128)S(1)}, u32[]{:S(2)}, u32[]{:S(2)}) collective-permute-start(f32[2,16,4096]{2,1,0:T(8,128)S(1)} %pad_maximum_fusion), channel_id=1, source_target_pairs={{0,8},{8,0},{16,24},{24,16},{1,9},{9,1},{17,25},{25,17},{2,10},{10... | collective-permute-start | bytes 1572872 | tf_op jit(solution)/shard_map/modal_state_scan/ppermute | solution.py:203
  39.8 7.0 %collective-permute-start.2 = (f32[16,4096]{1,0:T(8,128)S(1)}, f32[16,4096]{1,0:T(8,128)S(1)}, u32[]{:S(2)}, u32[]{:S(2)}) collective-permute-start(f32[16,4096]{1,0:T(8,128)S(1)} %select_select_fusion), channel_id=1, source_target_pairs={{0,16},{8,24},{16,0},{24,8},{1,17},{9,25},{17,1},{25,9},{2,18},{10... | collective-permute-start | bytes 786440 | tf_op jit(solution)/shard_map/modal_state_scan/ppermute | solution.py:203
  93.7 1.7 %collective-permute-start.4 = (f32[608,128]{1,0:T(8,128)S(1)}, f32[608,128]{1,0:T(8,128)S(1)}, u32[]{:S(2)}, u32[]{:S(2)}) collective-permute-start(f32[608,128]{1,0:T(8,128)S(1)} %select_n.211), channel_id=1, source_target_pairs={{0,1},{1,0},{2,3},{3,2},{4,5},{5,4},{6,7},{7,6},{8,9},{9,8},{10,11... | collective-permute-start | bytes 933896 | tf_op jit(solution)/shard_map/filter_grad_sum/ppermute | solution.py:203
  95.4 26.0 %copy-start.6 = (f32[3,8,4096]{2,1,0:T(8,128)S(1)}, f32[3,8,4096]{2,1,0:T(8,128)}, u32[]{:S(2)}) copy-start(f32[3,8,4096]{2,1,0:T(8,128)} %get-tuple-element.21) | copy-start | bytes 1179652
  95.5 37.3 %copy-start.3 = (f32[3,16,4096]{2,1,0:T(8,128)S(1)}, f32[3,16,4096]{2,1,0:T(8,128)}, u32[]{:S(2)}) copy-start(f32[3,16,4096]{2,1,0:T(8,128)} %get-tuple-element.20) | copy-start | bytes 2359300
  95.5 6.1 %collective-permute-start.5 = (f32[304,128]{1,0:T(8,128)S(1)}, f32[304,128]{1,0:T(8,128)S(1)}, u32[]{:S(2)}, u32[]{:S(2)}) collective-permute-start(f32[304,128]{1,0:T(8,128)S(1)} %slice_select_fusion.2), channel_id=1, source_target_pairs={{0,8},{8,0},{16,24},{24,16},{1,9},{9,1},{17,25},{25,17},{2,10},{10... | collective-permute-start | bytes 466952 | tf_op jit(solution)/shard_map/filter_grad_sum/ppermute | solution.py:203
  101.7 4.5 %collective-permute-start.6 = (f32[152,128]{1,0:T(8,128)S(1)}, f32[152,128]{1,0:T(8,128)S(1)}, u32[]{:S(2)}, u32[]{:S(2)}) collective-permute-start(f32[152,128]{1,0:T(8,128)S(1)} %slice_select_fusion.3), channel_id=1, source_target_pairs={{0,16},{8,24},{16,0},{24,8},{1,17},{9,25},{17,1},{25,9},{2,18},{10... | collective-permute-start | bytes 233480 | tf_op jit(solution)/shard_map/filter_grad_sum/ppermute | solution.py:203
  106.2 4.1 %collective-permute-start.7 = (f32[76,128]{1,0:T(8,128)S(1)}, f32[76,128]{1,0:T(8,128)S(1)}, u32[]{:S(2)}, u32[]{:S(2)}) collective-permute-start(f32[76,128]{1,0:T(8,128)S(1)} %slice_select_fusion.4), channel_id=1, source_target_pairs={{0,2},{1,3},{2,0},{3,1},{4,6},{5,7},{6,4},{7,5},{8,10},{9,11},{10,... | collective-permute-start | bytes 116744 | tf_op jit(solution)/shard_map/filter_grad_sum/ppermute | solution.py:203
  110.3 4.7 %collective-permute-start.8 = (f32[38,128]{1,0:T(8,128)S(1)}, f32[38,128]{1,0:T(8,128)S(1)}, u32[]{:S(2)}, u32[]{:S(2)}) collective-permute-start(f32[38,128]{1,0:T(8,128)S(1)} %slice_select_fusion.5), channel_id=1, source_target_pairs={{0,4},{1,5},{2,6},{3,7},{4,0},{5,1},{6,2},{7,3},{8,12},{9,13},{10,... | collective-permute-start | bytes 58376 | tf_op jit(solution)/shard_map/filter_grad_sum/ppermute | solution.py:203
  115.0 4.7 %collective-permute-start.9 = (f32[38,128]{1,0:T(8,128)S(1)}, f32[38,128]{1,0:T(8,128)S(1)}, u32[]{:S(2)}, u32[]{:S(2)}) collective-permute-start(f32[38,128]{1,0:T(8,128)S(1)} %select_add_fusion.5), channel_id=1, source_target_pairs={{0,4},{1,5},{2,6},{3,7},{4,0},{5,1},{6,2},{7,3},{8,12},{9,13},{10,... | collective-permute-start | bytes 58376 | tf_op jit(solution)/shard_map/filter_grad_sum/ppermute | solution.py:203
  119.8 4.1 %collective-permute-start.10 = (f32[76,128]{1,0:T(8,128)S(1)}, f32[76,128]{1,0:T(8,128)S(1)}, u32[]{:S(2)}, u32[]{:S(2)}) collective-permute-start(f32[76,128]{1,0:T(8,128)S(1)} %maximum_select_fusion.4), channel_id=1, source_target_pairs={{0,2},{1,3},{2,0},{3,1},{4,6},{5,7},{6,4},{7,5},{8,10},{9,11},{10,... | collective-permute-start | bytes 116744 | tf_op jit(solution)/shard_map/filter_grad_sum/ppermute | solution.py:203
  121.5 11.3 %collective-permute-start.3 = (f32[3,8,4096]{2,1,0:T(8,128)S(1)}, f32[3,8,4096]{2,1,0:T(8,128)S(1)}, u32[]{:S(2)}, u32[]{:S(2)}) collective-permute-start(f32[3,8,4096]{2,1,0:T(8,128)S(1)} %copy-done.6), channel_id=1, source_target_pairs={{8,0},{16,8},{24,16},{9,1},{17,9},{25,17},{10,2},{18,10},{26,18},{... | collective-permute-start | bytes 1179656 | tf_op jit(solution)/shard_map/ppermute | solution.py:20
  123.9 4.9 %collective-permute-start.11 = (f32[152,128]{1,0:T(8,128)S(1)}, f32[152,128]{1,0:T(8,128)S(1)}, u32[]{:S(2)}, u32[]{:S(2)}) collective-permute-start(f32[152,128]{1,0:T(8,128)S(1)} %maximum_select_fusion.3), channel_id=1, source_target_pairs={{0,16},{8,24},{16,0},{24,8},{1,17},{9,25},{17,1},{25,9},{2,18},{10... | collective-permute-start | bytes 233480 | tf_op jit(solution)/shard_map/filter_grad_sum/ppermute | solution.py:203
  128.8 5.7 %collective-permute-start.12 = (f32[304,128]{1,0:T(8,128)S(1)}, f32[304,128]{1,0:T(8,128)S(1)}, u32[]{:S(2)}, u32[]{:S(2)}) collective-permute-start(f32[304,128]{1,0:T(8,128)S(1)} %maximum_select_fusion.2), channel_id=1, source_target_pairs={{0,8},{8,0},{16,24},{24,16},{1,9},{9,1},{17,25},{25,17},{2,10},{10... | collective-permute-start | bytes 466952 | tf_op jit(solution)/shard_map/filter_grad_sum/ppermute | solution.py:203
  134.5 1.7 %collective-permute-start.13 = (f32[608,128]{1,0:T(8,128)S(1)}, f32[608,128]{1,0:T(8,128)S(1)}, u32[]{:S(2)}, u32[]{:S(2)}) collective-permute-start(f32[608,128]{1,0:T(8,128)S(1)} %maximum_select_fusion.1), channel_id=1, source_target_pairs={{0,1},{1,0},{2,3},{3,2},{4,5},{5,4},{6,7},{7,6},{8,9},{9,8},{10,11... | collective-permute-start | bytes 933896 | tf_op jit(solution)/shard_map/filter_grad_sum/ppermute | solution.py:203

commit v5 on v4

--- a/solution.py
+++ b/solution.py
@@ -219,11 +219,15 @@
         upper = (mine // size) % 2 == 1
         pos = mine % size
         if level == levels - 1:
-            got = exchange(jnp.where(upper, block_b, block_f), axis, size)
+            sent = jnp.where(upper, block_b, block_f)
+            half = sent.shape[1] // 2
+            got = jnp.concatenate(
+                [exchange(sent[:, :half], axis, size), exchange(sent[:, half:], axis, size)], 1
+            )
             got_f, got_b = (got, got)
         else:
-            got = exchange(jnp.stack([block_f, block_b]), axis, size)
-            got_f, got_b = (got[0], got[1])
+            got_f = exchange(block_f, axis, size)
+            got_b = exchange(block_b, axis, size)
         incoming_f = incoming_f + jnp.where(upper, decayed(decay, rows, pos) * got_f, 0.0)
         incoming_b = incoming_b + jnp.where(upper, 0.0, decayed(decay, rows, size - 1 - pos) * got_b)
         if level < levels - 1:

time: 139 us -> 139 us (level)
    ppermute x12 -> x14, waiting for transfers between devices: 37.8 us -> 36.6 us  [exchange(): return lax.ppermute(x, axis, [(i, i ^ size) for i in range(count)])]
    ppermute x12 -> x14, starting transfers between devices: 20.1 us -> 21.2 us  [exchange(): return lax.ppermute(x, axis, [(i, i ^ size) for i in range(count)])]
  transfers between devices with their start and end apart: 14 -> 16, of which waited for: 13 -> 15; matrix products, arithmetic and copies ran while one was open for 2% -> 3% of each run, Pallas kernels for 10% -> 10%
where the time goes in v5:
time: 139 us; the launch traced here: 138 us
  Pallas kernels  58.4 us (42%)
  waiting for transfers between devices  38.6 us (28%)
  starting transfers between devices  27.4 us (20%)
  local copies, waits for them, and re-layouts  6.55 us (5%)
  other arithmetic  6.46 us (5%)
    pallas_call x1, Pallas kernels, run_main(): pl.pallas_call(main_kernel, grid=(width // lanes,), in_specs=[tile(x.shap...  44.7 us
    ppermute x14, waiting for transfers between devices, exchange(): return lax.ppermute(x, axis, [(i, i ^ size) for i in range(count)])  36.6 us
    ppermute x14, starting transfers between devices, exchange(): return lax.ppermute(x, axis, [(i, i ^ size) for i in range(count)])  21.2 us
    pallas_call x1, Pallas kernels, run_states(): pl.pallas_call(states_kernel, grid=(width // lanes,), in_specs=[tile(x.sh...  13.7 us
    ppermute x2, starting transfers between devices, passed_along(): return lax.ppermute(x, axis, pairs)  6.16 us
  transfers between devices with their start and end apart: 16, of which 15 were waited for; matrix products, arithmetic and copies ran while one was open for 3% of the time, Pallas kernels for 10%

profile of v5, /device:TPU:0, one launch (start us, length us, event | category | flops | bytes accessed | tf_op | source)
XLA Modules:
  0.0 138.4 jit_solution(10554625978786231390)
XLA Ops:
  2.6 4.9 %collective-permute-start = (bf16[3,8,4096]{2,1,0:T(8,128)(2,1)S(1)}, bf16[3,8,4096]{2,1,0:T(8,128)(2,1)S(1)}, u32[]{:S(2)}, u32[]{:S(2)}) collective-permute-start(bf16[3,8,4096]{2,1,0:T(8,128)(2,1)S(1)} %pad_maximum_fusion.1), channel_id=1, source_target_pairs={{0,8},{8,16},{16,24},{1,9},{9,17},{17,25},{2,10},{10,18},{18,26},{... | collective-permute-start | bytes 589832 | tf_op jit(solution)/shard_map/ppermute | solution.py:20
  9.6 13.7 %shard_map.135 = (f32[16,4096]{1,0:T(8,128)}, f32[16,4096]{1,0:T(8,128)}) custom-call(bf16[128,4096]{1,0:T(8,128)(2,1)} %bitcast.33, bf16[128,4096]{1,0:T(8,128)(2,1)} %bitcast.35, bf16[128,4096]{1,0:T(8,128)(2,1)} %bitcast.37, bf16[128,4096]{1,0:T(8,128)(2,1)} %bitcast.39, bf16[3,8,4096]{2,1,0:T(8,128)(2,1)} %broadcast_in_dim.32.rim_ref, ...), custom_call_target="tpu_custom_call" | custom-call | tf_op jit(solution)/shard_map/pallas_call | solution.py:154
  26.1 1.5 %collective-permute-start.1 = (f32[16,4096]{1,0:T(8,128)S(1)}, f32[16,4096]{1,0:T(8,128)S(1)}, u32[]{:S(2)}, u32[]{:S(2)}) collective-permute-start(f32[16,4096]{1,0:T(8,128)S(1)} %add.138), channel_id=1, source_target_pairs={{0,8},{8,0},{16,24},{24,16},{1,9},{9,1},{17,25},{25,17},{2,10},{10... | collective-permute-start | bytes 786440 | tf_op jit(solution)/shard_map/modal_state_scan/ppermute | solution.py:203
  28.3 7.0 %collective-permute-done.1 = f32[16,4096]{1,0:T(8,128)S(1)} collective-permute-done((f32[16,4096]{1,0:T(8,128)S(1)}, f32[16,4096]{1,0:T(8,128)S(1)}, u32[]{:S(2)}, u32[]{:S(2)}) %collective-permute-start.1) | collective-permute-done | bytes 262176 | tf_op jit(solution)/shard_map/modal_state_scan/ppermute | solution.py:203
  35.3 4.2 %collective-permute-done.2 = f32[16,4096]{1,0:T(8,128)S(1)} collective-permute-done((f32[16,4096]{1,0:T(8,128)S(1)}, f32[16,4096]{1,0:T(8,128)S(1)}, u32[]{:S(2)}, u32[]{:S(2)}) %collective-permute-start.2) | collective-permute-done | bytes 262176 | tf_op jit(solution)/shard_map/modal_state_scan/ppermute | solution.py:203
  39.7 1.6 %collective-permute-start.3 = (f32[16,2048]{1,0:T(8,128)S(1)}, f32[16,2048]{1,0:T(8,128)S(1)}, u32[]{:S(2)}, u32[]{:S(2)}) collective-permute-start(f32[16,2048]{1,0:T(8,128)S(1)} %get-tuple-element.52), channel_id=1, source_target_pairs={{0,16},{8,24},{16,0},{24,8},{1,17},{9,25},{17,1},{25,9},{2,18},{10... | collective-permute-start | bytes 393224 | tf_op jit(solution)/shard_map/modal_state_scan/ppermute | solution.py:203
  41.8 3.5 %collective-permute-done.3 = f32[16,2048]{1,0:T(8,128)S(1)} collective-permute-done((f32[16,2048]{1,0:T(8,128)S(1)}, f32[16,2048]{1,0:T(8,128)S(1)}, u32[]{:S(2)}, u32[]{:S(2)}) %collective-permute-start.3) | collective-permute-done | bytes 131104 | tf_op jit(solution)/shard_map/modal_state_scan/ppermute | solution.py:203
  47.7 44.7 %shard_map.136 = (bf16[128,4096]{1,0:T(8,128)(2,1)}, bf16[128,4096]{1,0:T(8,128)(2,1)}, bf16[128,4096]{1,0:T(8,128)(2,1)}, bf16[128,4096]{1,0:T(8,128)(2,1)}, f3...) custom-call(bf16[128,4096]{1,0:T(8,128)(2,1)} %bitcast.34, bf16[128,4096]{1,0:T(8,128)(2,1)} %bitcast.36, ...), custom_call_target="tpu_custom_call" | custom-call | tf_op jit(solution)/shard_map/pallas_call | solution.py:183
  93.8 1.5 %collective-permute-done.6 = f32[608,128]{1,0:T(8,128)S(1)} collective-permute-done((f32[608,128]{1,0:T(8,128)S(1)}, f32[608,128]{1,0:T(8,128)S(1)}, u32[]{:S(2)}, u32[]{:S(2)}) %collective-permute-start.6) | collective-permute-done | bytes 311328 | tf_op jit(solution)/shard_map/filter_grad_sum/ppermute | solution.py:203
  95.4 1.5 %collective-permute-start.7 = (f32[304,128]{1,0:T(8,128)S(1)}, f32[304,128]{1,0:T(8,128)S(1)}, u32[]{:S(2)}, u32[]{:S(2)}) collective-permute-start(f32[304,128]{1,0:T(8,128)S(1)} %slice_select_fusion.2), channel_id=1, source_target_pairs={{0,8},{8,0},{16,24},{24,16},{1,9},{9,1},{17,25},{25,17},{2,10},{10... | collective-permute-start | bytes 466952 | tf_op jit(solution)/shard_map/filter_grad_sum/ppermute | solution.py:203
  97.0 4.6 %collective-permute-done.7 = f32[304,128]{1,0:T(8,128)S(1)} collective-permute-done((f32[304,128]{1,0:T(8,128)S(1)}, f32[304,128]{1,0:T(8,128)S(1)}, u32[]{:S(2)}, u32[]{:S(2)}) %collective-permute-start.7) | collective-permute-done | bytes 155680 | tf_op jit(solution)/shard_map/filter_grad_sum/ppermute | solution.py:203
  101.6 1.6 %collective-permute-start.8 = (f32[152,128]{1,0:T(8,128)S(1)}, f32[152,128]{1,0:T(8,128)S(1)}, u32[]{:S(2)}, u32[]{:S(2)}) collective-permute-start(f32[152,128]{1,0:T(8,128)S(1)} %slice_select_fusion.3), channel_id=1, source_target_pairs={{0,16},{8,24},{16,0},{24,8},{1,17},{9,25},{17,1},{25,9},{2,18},{10... | collective-permute-start | bytes 233480 | tf_op jit(solution)/shard_map/filter_grad_sum/ppermute | solution.py:203
  103.2 2.9 %collective-permute-done.8 = f32[152,128]{1,0:T(8,128)S(1)} collective-permute-done((f32[152,128]{1,0:T(8,128)S(1)}, f32[152,128]{1,0:T(8,128)S(1)}, u32[]{:S(2)}, u32[]{:S(2)}) %collective-permute-start.8) | collective-permute-done | bytes 77856 | tf_op jit(solution)/shard_map/filter_grad_sum/ppermute | solution.py:203
  106.1 1.6 %collective-permute-start.9 = (f32[76,128]{1,0:T(8,128)S(1)}, f32[76,128]{1,0:T(8,128)S(1)}, u32[]{:S(2)}, u32[]{:S(2)}) collective-permute-start(f32[76,128]{1,0:T(8,128)S(1)} %slice_select_fusion.4), channel_id=1, source_target_pairs={{0,2},{1,3},{2,0},{3,1},{4,6},{5,7},{6,4},{7,5},{8,10},{9,11},{10,... | collective-permute-start | bytes 116744 | tf_op jit(solution)/shard_map/filter_grad_sum/ppermute | solution.py:203
  107.7 2.4 %collective-permute-done.9 = f32[76,128]{1,0:T(8,128)S(1)} collective-permute-done((f32[76,128]{1,0:T(8,128)S(1)}, f32[76,128]{1,0:T(8,128)S(1)}, u32[]{:S(2)}, u32[]{:S(2)}) %collective-permute-start.9) | collective-permute-done | bytes 38944 | tf_op jit(solution)/shard_map/filter_grad_sum/ppermute | solution.py:203
  110.2 2.9 %collective-permute-start.10 = (f32[38,128]{1,0:T(8,128)S(1)}, f32[38,128]{1,0:T(8,128)S(1)}, u32[]{:S(2)}, u32[]{:S(2)}) collective-permute-start(f32[38,128]{1,0:T(8,128)S(1)} %slice_select_fusion.5), channel_id=1, source_target_pairs={{0,4},{1,5},{2,6},{3,7},{4,0},{5,1},{6,2},{7,3},{8,12},{9,13},{10,... | collective-permute-start | bytes 58376 | tf_op jit(solution)/shard_map/filter_grad_sum/ppermute | solution.py:203
  113.1 1.9 %collective-permute-done.10 = f32[38,128]{1,0:T(8,128)S(1)} collective-permute-done((f32[38,128]{1,0:T(8,128)S(1)}, f32[38,128]{1,0:T(8,128)S(1)}, u32[]{:S(2)}, u32[]{:S(2)}) %collective-permute-start.10) | collective-permute-done | bytes 19488 | tf_op jit(solution)/shard_map/filter_grad_sum/ppermute | solution.py:203
  114.9 3.0 %collective-permute-start.11 = (f32[38,128]{1,0:T(8,128)S(1)}, f32[38,128]{1,0:T(8,128)S(1)}, u32[]{:S(2)}, u32[]{:S(2)}) collective-permute-start(f32[38,128]{1,0:T(8,128)S(1)} %select_add_fusion.5), channel_id=1, source_target_pairs={{0,4},{1,5},{2,6},{3,7},{4,0},{5,1},{6,2},{7,3},{8,12},{9,13},{10,... | collective-permute-start | bytes 58376 | tf_op jit(solution)/shard_map/filter_grad_sum/ppermute | solution.py:203
  117.9 1.8 %collective-permute-done.11 = f32[38,128]{1,0:T(8,128)S(1)} collective-permute-done((f32[38,128]{1,0:T(8,128)S(1)}, f32[38,128]{1,0:T(8,128)S(1)}, u32[]{:S(2)}, u32[]{:S(2)}) %collective-permute-start.11) | collective-permute-done | bytes 19488 | tf_op jit(solution)/shard_map/filter_grad_sum/ppermute | solution.py:203
  119.7 1.7 %collective-permute-start.12 = (f32[76,128]{1,0:T(8,128)S(1)}, f32[76,128]{1,0:T(8,128)S(1)}, u32[]{:S(2)}, u32[]{:S(2)}) collective-permute-start(f32[76,128]{1,0:T(8,128)S(1)} %maximum_select_fusion.4), channel_id=1, source_target_pairs={{0,2},{1,3},{2,0},{3,1},{4,6},{5,7},{6,4},{7,5},{8,10},{9,11},{10,... | collective-permute-start | bytes 116744 | tf_op jit(solution)/shard_map/filter_grad_sum/ppermute | solution.py:203
  123.8 2.6 %collective-permute-start.13 = (f32[152,128]{1,0:T(8,128)S(1)}, f32[152,128]{1,0:T(8,128)S(1)}, u32[]{:S(2)}, u32[]{:S(2)}) collective-permute-start(f32[152,128]{1,0:T(8,128)S(1)} %maximum_select_fusion.3), channel_id=1, source_target_pairs={{0,16},{8,24},{16,0},{24,8},{1,17},{9,25},{17,1},{25,9},{2,18},{10... | collective-permute-start | bytes 233480 | tf_op jit(solution)/shard_map/filter_grad_sum/ppermute | solution.py:203
  126.4 2.3 %collective-permute-done.13 = f32[152,128]{1,0:T(8,128)S(1)} collective-permute-done((f32[152,128]{1,0:T(8,128)S(1)}, f32[152,128]{1,0:T(8,128)S(1)}, u32[]{:S(2)}, u32[]{:S(2)}) %collective-permute-start.13) | collective-permute-done | bytes 77856 | tf_op jit(solution)/shard_map/filter_grad_sum/ppermute | solution.py:203
  128.7 2.0 %collective-permute-start.14 = (f32[304,128]{1,0:T(8,128)S(1)}, f32[304,128]{1,0:T(8,128)S(1)}, u32[]{:S(2)}, u32[]{:S(2)}) collective-permute-start(f32[304,128]{1,0:T(8,128)S(1)} %maximum_select_fusion.2), channel_id=1, source_target_pairs={{0,8},{8,0},{16,24},{24,16},{1,9},{9,1},{17,25},{25,17},{2,10},{10... | collective-permute-start | bytes 466952 | tf_op jit(solution)/shard_map/filter_grad_sum/ppermute | solution.py:203
  130.7 2.0 %collective-permute-done.5 = f32[3,8,4096]{2,1,0:T(8,128)S(1)} collective-permute-done((f32[3,8,4096]{2,1,0:T(8,128)S(1)}, f32[3,8,4096]{2,1,0:T(8,128)S(1)}, u32[]{:S(2)}, u32[]{:S(2)}) %collective-permute-start.5) | collective-permute-done | bytes 393248 | tf_op jit(solution)/shard_map/ppermute | solution.py:20
  (72 shorter events, 20.0 us)
Async XLA Ops:
  0.6 6.9 %copy-start.1 = (f32[16,4096]{1,0:T(8,128)S(1)}, f32[16,4096]{1,0:T(8,128)}, u32[]{:S(2)}) copy-start(f32[16,4096]{1,0:T(8,128)} %param.15) | copy-start | bytes 786436
  0.6 7.6 %copy-start = (f32[3,7,4096]{2,1,0:T(8,128)S(1)}, f32[3,7,4096]{2,1,0:T(8,128)}, u32[]{:S(2)}) copy-start(f32[3,7,4096]{2,1,0:T(8,128)} %taps_ref.3) | copy-start | bytes 1032196
  2.6 20.7 %collective-permute-start = (bf16[3,8,4096]{2,1,0:T(8,128)(2,1)S(1)}, bf16[3,8,4096]{2,1,0:T(8,128)(2,1)S(1)}, u32[]{:S(2)}, u32[]{:S(2)}) collective-permute-start(bf16[3,8,4096]{2,1,0:T(8,128)(2,1)S(1)} %pad_maximum_fusion.1), channel_id=1, source_target_pairs={{0,8},{8,16},{16,24},{1,9},{9,17},{17,25},{2,10},{10,18},{18,26},{... | collective-permute-start | bytes 589832 | tf_op jit(solution)/shard_map/ppermute | solution.py:20
  23.3 0.9 copy-start.2
  25.1 1.0 copy-start.5
  25.1 2.5 %copy-start.4 = (f32[16,4096]{1,0:T(8,128)S(1)}, f32[16,4096]{1,0:T(8,128)}, u32[]{:S(2)}) copy-start(f32[16,4096]{1,0:T(8,128)} %get-tuple-element.17) | copy-start | bytes 786436
  26.1 9.2 %collective-permute-start.1 = (f32[16,4096]{1,0:T(8,128)S(1)}, f32[16,4096]{1,0:T(8,128)S(1)}, u32[]{:S(2)}, u32[]{:S(2)}) collective-permute-start(f32[16,4096]{1,0:T(8,128)S(1)} %add.138), channel_id=1, source_target_pairs={{0,8},{8,0},{16,24},{24,16},{1,9},{9,1},{17,25},{25,17},{2,10},{10... | collective-permute-start | bytes 786440 | tf_op jit(solution)/shard_map/modal_state_scan/ppermute | solution.py:203
  27.7 11.9 %collective-permute-start.2 = (f32[16,4096]{1,0:T(8,128)S(1)}, f32[16,4096]{1,0:T(8,128)S(1)}, u32[]{:S(2)}, u32[]{:S(2)}) collective-permute-start(f32[16,4096]{1,0:T(8,128)S(1)} %add.140), channel_id=1, source_target_pairs={{0,8},{8,0},{16,24},{24,16},{1,9},{9,1},{17,25},{25,17},{2,10},{10... | collective-permute-start | bytes 786440 | tf_op jit(solution)/shard_map/modal_state_scan/ppermute | solution.py:203
  39.7 5.6 %collective-permute-start.3 = (f32[16,2048]{1,0:T(8,128)S(1)}, f32[16,2048]{1,0:T(8,128)S(1)}, u32[]{:S(2)}, u32[]{:S(2)}) collective-permute-start(f32[16,2048]{1,0:T(8,128)S(1)} %get-tuple-element.52), channel_id=1, source_target_pairs={{0,16},{8,24},{16,0},{24,8},{1,17},{9,25},{17,1},{25,9},{2,18},{10... | collective-permute-start | bytes 393224 | tf_op jit(solution)/shard_map/modal_state_scan/ppermute | solution.py:203
  41.3 5.4 %collective-permute-start.4 = (f32[16,2048]{1,0:T(8,128)S(1)}, f32[16,2048]{1,0:T(8,128)S(1)}, u32[]{:S(2)}, u32[]{:S(2)}) collective-permute-start(f32[16,2048]{1,0:T(8,128)S(1)} %get-tuple-element.51), channel_id=1, source_target_pairs={{0,16},{8,24},{16,0},{24,8},{1,17},{9,25},{17,1},{25,9},{2,18},{10... | collective-permute-start | bytes 393224 | tf_op jit(solution)/shard_map/modal_state_scan/ppermute | solution.py:203
  93.7 1.7 %collective-permute-start.6 = (f32[608,128]{1,0:T(8,128)S(1)}, f32[608,128]{1,0:T(8,128)S(1)}, u32[]{:S(2)}, u32[]{:S(2)}) collective-permute-start(f32[608,128]{1,0:T(8,128)S(1)} %select_n.211), channel_id=1, source_target_pairs={{0,1},{1,0},{2,3},{3,2},{4,5},{5,4},{6,7},{7,6},{8,9},{9,8},{10,11... | collective-permute-start | bytes 933896 | tf_op jit(solution)/shard_map/filter_grad_sum/ppermute | solution.py:203
  95.4 26.0 %copy-start.6 = (f32[3,8,4096]{2,1,0:T(8,128)S(1)}, f32[3,8,4096]{2,1,0:T(8,128)}, u32[]{:S(2)}) copy-start(f32[3,8,4096]{2,1,0:T(8,128)} %get-tuple-element.21) | copy-start | bytes 1179652
  95.4 37.3 %copy-start.3 = (f32[3,16,4096]{2,1,0:T(8,128)S(1)}, f32[3,16,4096]{2,1,0:T(8,128)}, u32[]{:S(2)}) copy-start(f32[3,16,4096]{2,1,0:T(8,128)} %get-tuple-element.20) | copy-start | bytes 2359300
  95.4 6.1 %collective-permute-start.7 = (f32[304,128]{1,0:T(8,128)S(1)}, f32[304,128]{1,0:T(8,128)S(1)}, u32[]{:S(2)}, u32[]{:S(2)}) collective-permute-start(f32[304,128]{1,0:T(8,128)S(1)} %slice_select_fusion.2), channel_id=1, source_target_pairs={{0,8},{8,0},{16,24},{24,16},{1,9},{9,1},{17,25},{25,17},{2,10},{10... | collective-permute-start | bytes 466952 | tf_op jit(solution)/shard_map/filter_grad_sum/ppermute | solution.py:203
  101.6 4.5 %collective-permute-start.8 = (f32[152,128]{1,0:T(8,128)S(1)}, f32[152,128]{1,0:T(8,128)S(1)}, u32[]{:S(2)}, u32[]{:S(2)}) collective-permute-start(f32[152,128]{1,0:T(8,128)S(1)} %slice_select_fusion.3), channel_id=1, source_target_pairs={{0,16},{8,24},{16,0},{24,8},{1,17},{9,25},{17,1},{25,9},{2,18},{10... | collective-permute-start | bytes 233480 | tf_op jit(solution)/shard_map/filter_grad_sum/ppermute | solution.py:203
  106.1 4.1 %collective-permute-start.9 = (f32[76,128]{1,0:T(8,128)S(1)}, f32[76,128]{1,0:T(8,128)S(1)}, u32[]{:S(2)}, u32[]{:S(2)}) collective-permute-start(f32[76,128]{1,0:T(8,128)S(1)} %slice_select_fusion.4), channel_id=1, source_target_pairs={{0,2},{1,3},{2,0},{3,1},{4,6},{5,7},{6,4},{7,5},{8,10},{9,11},{10,... | collective-permute-start | bytes 116744 | tf_op jit(solution)/shard_map/filter_grad_sum/ppermute | solution.py:203
  110.2 4.7 %collective-permute-start.10 = (f32[38,128]{1,0:T(8,128)S(1)}, f32[38,128]{1,0:T(8,128)S(1)}, u32[]{:S(2)}, u32[]{:S(2)}) collective-permute-start(f32[38,128]{1,0:T(8,128)S(1)} %slice_select_fusion.5), channel_id=1, source_target_pairs={{0,4},{1,5},{2,6},{3,7},{4,0},{5,1},{6,2},{7,3},{8,12},{9,13},{10,... | collective-permute-start | bytes 58376 | tf_op jit(solution)/shard_map/filter_grad_sum/ppermute | solution.py:203
  114.9 4.7 %collective-permute-start.11 = (f32[38,128]{1,0:T(8,128)S(1)}, f32[38,128]{1,0:T(8,128)S(1)}, u32[]{:S(2)}, u32[]{:S(2)}) collective-permute-start(f32[38,128]{1,0:T(8,128)S(1)} %select_add_fusion.5), channel_id=1, source_target_pairs={{0,4},{1,5},{2,6},{3,7},{4,0},{5,1},{6,2},{7,3},{8,12},{9,13},{10,... | collective-permute-start | bytes 58376 | tf_op jit(solution)/shard_map/filter_grad_sum/ppermute | solution.py:203
  119.7 4.1 %collective-permute-start.12 = (f32[76,128]{1,0:T(8,128)S(1)}, f32[76,128]{1,0:T(8,128)S(1)}, u32[]{:S(2)}, u32[]{:S(2)}) collective-permute-start(f32[76,128]{1,0:T(8,128)S(1)} %maximum_select_fusion.4), channel_id=1, source_target_pairs={{0,2},{1,3},{2,0},{3,1},{4,6},{5,7},{6,4},{7,5},{8,10},{9,11},{10,... | collective-permute-start | bytes 116744 | tf_op jit(solution)/shard_map/filter_grad_sum/ppermute | solution.py:203
  121.4 11.3 %collective-permute-start.5 = (f32[3,8,4096]{2,1,0:T(8,128)S(1)}, f32[3,8,4096]{2,1,0:T(8,128)S(1)}, u32[]{:S(2)}, u32[]{:S(2)}) collective-permute-start(f32[3,8,4096]{2,1,0:T(8,128)S(1)} %copy-done.6), channel_id=1, source_target_pairs={{8,0},{16,8},{24,16},{9,1},{17,9},{25,17},{10,2},{18,10},{26,18},{... | collective-permute-start | bytes 1179656 | tf_op jit(solution)/shard_map/ppermute | solution.py:20
  123.8 4.9 %collective-permute-start.13 = (f32[152,128]{1,0:T(8,128)S(1)}, f32[152,128]{1,0:T(8,128)S(1)}, u32[]{:S(2)}, u32[]{:S(2)}) collective-permute-start(f32[152,128]{1,0:T(8,128)S(1)} %maximum_select_fusion.3), channel_id=1, source_target_pairs={{0,16},{8,24},{16,0},{24,8},{1,17},{9,25},{17,1},{25,9},{2,18},{10... | collective-permute-start | bytes 233480 | tf_op jit(solution)/shard_map/filter_grad_sum/ppermute | solution.py:203
  128.7 5.6 %collective-permute-start.14 = (f32[304,128]{1,0:T(8,128)S(1)}, f32[304,128]{1,0:T(8,128)S(1)}, u32[]{:S(2)}, u32[]{:S(2)}) collective-permute-start(f32[304,128]{1,0:T(8,128)S(1)} %maximum_select_fusion.2), channel_id=1, source_target_pairs={{0,8},{8,0},{16,24},{24,16},{1,9},{9,1},{17,25},{25,17},{2,10},{10... | collective-permute-start | bytes 466952 | tf_op jit(solution)/shard_map/filter_grad_sum/ppermute | solution.py:203
  134.4 1.7 %collective-permute-start.15 = (f32[608,128]{1,0:T(8,128)S(1)}, f32[608,128]{1,0:T(8,128)S(1)}, u32[]{:S(2)}, u32[]{:S(2)}) collective-permute-start(f32[608,128]{1,0:T(8,128)S(1)} %maximum_select_fusion.1), channel_id=1, source_target_pairs={{0,1},{1,0},{2,3},{3,2},{4,5},{5,4},{6,7},{7,6},{8,9},{9,8},{10,11... | collective-permute-start | bytes 933896 | tf_op jit(solution)/shard_map/filter_grad_sum/ppermute | solution.py:203

commit v6 on v5

--- a/solution.py
+++ b/solution.py
@@ -20,6 +20,33 @@
     return lax.ppermute(x, axis, pairs)
 
 
+CHUNK = 256
+
+
+def sublanes(lanes):
+    return lax.broadcasted_iota(jnp.int32, (8, lanes), 0)
+
+
+def feature_stream(pad_ref, taps_ref, s, out_ref):
+    rows = out_ref.shape[1]
+    count = taps_ref.shape[1]
+    for c0 in range(0, out_ref.shape[2], CHUNK):
+        cols = slice(c0, c0 + CHUNK)
+        sub = sublanes(CHUNK)
+        taps = [taps_ref[s, lag : lag + 1, cols] for lag in range(count)]
+        prev = [pltpu.roll(pad_ref[s, 0:8, cols], lag, 0) for lag in range(1, count)]
+        for i in range(rows // 8):
+            cur = pad_ref[s, 8 * (i + 1) : 8 * (i + 2), cols]
+            total = taps[0] * cur
+            rolled = []
+            for lag in range(1, count):
+                turned = pltpu.roll(cur, lag, 0)
+                total = total + taps[lag] * jnp.where(sub < lag, prev[lag - 1], turned)
+                rolled.append(turned)
+            prev = rolled
+            out_ref[s, 8 * i : 8 * (i + 1), cols] = total
+
+
 def fill_rows(x_refs, pad_ref, lo):
     for s, x_ref in enumerate(x_refs):
         pad_ref[s, RIM + lo : RIM + lo + BR, :] = x_ref[lo : lo + BR, :].astype(F32)
@@ -33,17 +60,19 @@
     return total
 
 
-def states_kernel(q_ref, k_ref, v_ref, c_ref, rim_ref, taps_ref, a_ref, f_ref, b_ref, pad_ref, p_ref, z_ref):
+def states_kernel(
+    q_ref, k_ref, v_ref, c_ref, rim_ref, taps_ref, a_ref, f_ref, b_ref, pad_ref, p_ref, z_ref, feat_ref
+):
     rows = q_ref.shape[0]
     for s in range(3):
         pad_ref[s, 0:RIM, :] = rim_ref[s].astype(F32)
     for lo in range(0, rows, BR):
         fill_rows((q_ref, k_ref, v_ref), pad_ref, lo)
-        fq = block_feature(pad_ref, taps_ref, 0, lo)
-        fk = block_feature(pad_ref, taps_ref, 1, lo)
-        fv = block_feature(pad_ref, taps_ref, 2, lo)
-        p_ref[lo : lo + BR, :] = fk * fv
-        z_ref[lo : lo + BR, :] = c_ref[lo : lo + BR, :].astype(F32) * fq
+    for s in range(3):
+        feature_stream(pad_ref, taps_ref, s, feat_ref)
+    for lo in range(0, rows, BR):
+        p_ref[lo : lo + BR, :] = feat_ref[1, lo : lo + BR, :] * feat_ref[2, lo : lo + BR, :]
+        z_ref[lo : lo + BR, :] = c_ref[lo : lo + BR, :].astype(F32) * feat_ref[0, lo : lo + BR, :]
     a = a_ref[...]
 
     def step(i, carry):
@@ -76,12 +105,12 @@
     skip_sum = jnp.zeros((8, lanes), F32)
     for lo in range(0, rows, BR):
         fill_rows((q_ref, k_ref, v_ref), pad_ref, lo)
-        fq = block_feature(pad_ref, taps_ref, 0, lo)
-        fk = block_feature(pad_ref, taps_ref, 1, lo)
-        fv = block_feature(pad_ref, taps_ref, 2, lo)
-        feat_ref[0, lo : lo + BR, :] = fq
-        feat_ref[1, lo : lo + BR, :] = fk
-        feat_ref[2, lo : lo + BR, :] = fv
+    for s in range(3):
+        feature_stream(pad_ref, taps_ref, s, feat_ref)
+    for lo in range(0, rows, BR):
+        fq = feat_ref[0, lo : lo + BR, :]
+        fk = feat_ref[1, lo : lo + BR, :]
+        fv = feat_ref[2, lo : lo + BR, :]
         p = fk * fv
         z = c_ref[lo : lo + BR, :].astype(F32) * fq
         p_ref[lo : lo + BR, :] = p
@@ -117,25 +146,43 @@
     for s in range(3):
         adj_ref[s, rows : rows + RIM, :] = zeros_rim
         head_ref[s] = adj_ref[s, 0:RIM, :]
-        sums = [jnp.zeros((8, lanes), F32) for _ in range(count)]
-        for lo in range(0, rows, BR):
-            x = pad_ref[s, RIM + lo : RIM + lo + BR, :]
-            total = None
+    for s in range(3):
+        for c0 in range(0, lanes, CHUNK):
+            cols = slice(c0, c0 + CHUNK)
+            sub = sublanes(CHUNK)
+            taps = [taps_ref[s, lag : lag + 1, cols] for lag in range(count)]
+            sums = [jnp.zeros((8, CHUNK), F32) for _ in range(count)]
+            prev = [pltpu.roll(adj_ref[s, 0:8, cols], 8 - lag, 0) for lag in range(1, count)]
+            done = []
+            for i in range(rows // 8):
+                cur = adj_ref[s, 8 * i : 8 * (i + 1), cols]
+                after = adj_ref[s, 8 * (i + 1) : 8 * (i + 2), cols]
+                x = pad_ref[s, RIM + 8 * i : RIM + 8 * (i + 1), cols]
+                total = taps[0] * cur
+                sums[0] = sums[0] + cur * x
+                rolled = []
+                for lag in range(1, count):
+                    turned = pltpu.roll(after, 8 - lag, 0)
+                    window = jnp.where(sub < 8 - lag, prev[lag - 1], turned)
+                    total = total + taps[lag] * window
+                    sums[lag] = sums[lag] + window * x
+                    rolled.append(turned)
+                prev = rolled
+                done.append(total)
+                if len(done) == 2:
+                    both = jnp.concatenate(done, 0)
+                    lo = 8 * (i - 1)
+                    outs[s][lo : lo + BR, cols] = both.astype(outs[s].dtype)
+                    if lo + BR == rows:
+                        tail_ref[s, :, cols] = both[BR - TAIL :]
+                    done = []
             for lag in range(count):
-                window = adj_ref[s, lo + lag : lo + lag + BR, :]
-                term = taps_ref[s, lag : lag + 1, :] * window
-                total = term if total is None else total + term
-                sums[lag] = sums[lag] + fold(window * x)
-            outs[s][lo : lo + BR, :] = total.astype(outs[s].dtype)
-            if lo + BR == rows:
-                tail_ref[s] = total[BR - TAIL :]
-        for lag in range(count):
-            value = jnp.sum(sums[lag], axis=0, keepdims=True)
-            if lag > 0:
-                edge = adj_ref[s, 0:lag, :] * pad_ref[s, RIM - lag : RIM, :]
-                value = value + jnp.sum(edge, axis=0, keepdims=True)
-            row = s * count + lag
-            grads_ref[row : row + 1, :] = value
+                value = jnp.sum(sums[lag], axis=0, keepdims=True)
+                if lag > 0:
+                    edge = adj_ref[s, 0:lag, cols] * pad_ref[s, RIM - lag : RIM, cols]
+                    value = value + jnp.sum(edge, axis=0, keepdims=True)
+                row = s * count + lag
+                grads_ref[row : row + 1, cols] = value
     base = 3 * count
     grads_ref[base : base + poles, :] = acc
     grads_ref[base + poles : base + poles + 1, :] = jnp.sum(skip_sum, axis=0, keepdims=True)
@@ -161,6 +208,7 @@
             pltpu.VMEM((3, rows + RIM, lanes), F32),
             pltpu.VMEM((rows, lanes), F32),
             pltpu.VMEM((rows, lanes), F32),
+            pltpu.VMEM((3, rows, lanes), F32),
         ],
     )(*ins)
 

time: 139 us -> 132 us (0.950)
  Pallas kernels: 58.4 us -> 52.2 us
    pallas_call x1, Pallas kernels: 44.7 us -> 38.5 us  [run_main(): pl.pallas_call(main_kernel, grid=(width // lanes,), in_specs=[tile(x.shap...]
where the time goes in v6:
time: 132 us
  Pallas kernels  52.2 us (40%)
  waiting for transfers between devices  38.6 us (29%)
  starting transfers between devices  27.4 us (21%)
  local copies, waits for them, and re-layouts  6.55 us (5%)
  other arithmetic  6.46 us (5%)
    pallas_call x1, Pallas kernels, run_main(): pl.pallas_call(main_kernel, grid=(width // lanes,), in_specs=[tile(x.shap...  38.5 us
    ppermute x14, waiting for transfers between devices, exchange(): return lax.ppermute(x, axis, [(i, i ^ size) for i in range(count)])  36.6 us
    ppermute x14, starting transfers between devices, exchange(): return lax.ppermute(x, axis, [(i, i ^ size) for i in range(count)])  21.2 us
    pallas_call x1, Pallas kernels, run_states(): pl.pallas_call(states_kernel, grid=(width // lanes,), in_specs=[tile(x.sh...  13.7 us
    ppermute x2, starting transfers between devices, passed_along(): return lax.ppermute(x, axis, pairs)  6.16 us
  transfers between devices with their start and end apart: 16, of which 15 were waited for; matrix products, arithmetic and copies ran while one was open for 3% of the time, Pallas kernels for 10%

profile of v6, /device:TPU:0, one launch (start us, length us, event | category | flops | bytes accessed | tf_op | source)
XLA Modules:
  0.0 132.1 jit_solution(10555631509209899941)
XLA Ops:
  2.6 4.9 %collective-permute-start = (bf16[3,8,4096]{2,1,0:T(8,128)(2,1)S(1)}, bf16[3,8,4096]{2,1,0:T(8,128)(2,1)S(1)}, u32[]{:S(2)}, u32[]{:S(2)}) collective-permute-start(bf16[3,8,4096]{2,1,0:T(8,128)(2,1)S(1)} %pad_maximum_fusion.1), channel_id=1, source_target_pairs={{0,8},{8,16},{16,24},{1,9},{9,17},{17,25},{2,10},{10,18},{18,26},{... | collective-permute-start | bytes 589832 | tf_op jit(solution)/shard_map/ppermute | solution.py:20
  9.6 13.7 %shard_map.135 = (f32[16,4096]{1,0:T(8,128)}, f32[16,4096]{1,0:T(8,128)}) custom-call(bf16[128,4096]{1,0:T(8,128)(2,1)} %bitcast.33, bf16[128,4096]{1,0:T(8,128)(2,1)} %bitcast.35, bf16[128,4096]{1,0:T(8,128)(2,1)} %bitcast.37, bf16[128,4096]{1,0:T(8,128)(2,1)} %bitcast.39, bf16[3,8,4096]{2,1,0:T(8,128)(2,1)} %broadcast_in_dim.32.rim_ref, ...), custom_call_target="tpu_custom_call" | custom-call | tf_op jit(solution)/shard_map/pallas_call | solution.py:201
  26.1 1.5 %collective-permute-start.1 = (f32[16,4096]{1,0:T(8,128)S(1)}, f32[16,4096]{1,0:T(8,128)S(1)}, u32[]{:S(2)}, u32[]{:S(2)}) collective-permute-start(f32[16,4096]{1,0:T(8,128)S(1)} %add.138), channel_id=1, source_target_pairs={{0,8},{8,0},{16,24},{24,16},{1,9},{9,1},{17,25},{25,17},{2,10},{10... | collective-permute-start | bytes 786440 | tf_op jit(solution)/shard_map/modal_state_scan/ppermute | solution.py:251
  28.2 7.0 %collective-permute-done.1 = f32[16,4096]{1,0:T(8,128)S(1)} collective-permute-done((f32[16,4096]{1,0:T(8,128)S(1)}, f32[16,4096]{1,0:T(8,128)S(1)}, u32[]{:S(2)}, u32[]{:S(2)}) %collective-permute-start.1) | collective-permute-done | bytes 262176 | tf_op jit(solution)/shard_map/modal_state_scan/ppermute | solution.py:251
  35.3 4.2 %collective-permute-done.2 = f32[16,4096]{1,0:T(8,128)S(1)} collective-permute-done((f32[16,4096]{1,0:T(8,128)S(1)}, f32[16,4096]{1,0:T(8,128)S(1)}, u32[]{:S(2)}, u32[]{:S(2)}) %collective-permute-start.2) | collective-permute-done | bytes 262176 | tf_op jit(solution)/shard_map/modal_state_scan/ppermute | solution.py:251
  39.7 1.6 %collective-permute-start.3 = (f32[16,2048]{1,0:T(8,128)S(1)}, f32[16,2048]{1,0:T(8,128)S(1)}, u32[]{:S(2)}, u32[]{:S(2)}) collective-permute-start(f32[16,2048]{1,0:T(8,128)S(1)} %get-tuple-element.52), channel_id=1, source_target_pairs={{0,16},{8,24},{16,0},{24,8},{1,17},{9,25},{17,1},{25,9},{2,18},{10... | collective-permute-start | bytes 393224 | tf_op jit(solution)/shard_map/modal_state_scan/ppermute | solution.py:251
  41.8 3.5 %collective-permute-done.3 = f32[16,2048]{1,0:T(8,128)S(1)} collective-permute-done((f32[16,2048]{1,0:T(8,128)S(1)}, f32[16,2048]{1,0:T(8,128)S(1)}, u32[]{:S(2)}, u32[]{:S(2)}) %collective-permute-start.3) | collective-permute-done | bytes 131104 | tf_op jit(solution)/shard_map/modal_state_scan/ppermute | solution.py:251
  47.6 38.5 %shard_map.136 = (bf16[128,4096]{1,0:T(8,128)(2,1)}, bf16[128,4096]{1,0:T(8,128)(2,1)}, bf16[128,4096]{1,0:T(8,128)(2,1)}, bf16[128,4096]{1,0:T(8,128)(2,1)}, f3...) custom-call(bf16[128,4096]{1,0:T(8,128)(2,1)} %bitcast.34, bf16[128,4096]{1,0:T(8,128)(2,1)} %bitcast.36, ...), custom_call_target="tpu_custom_call" | custom-call | tf_op jit(solution)/shard_map/pallas_call | solution.py:231
  87.6 1.5 %collective-permute-done.6 = f32[608,128]{1,0:T(8,128)S(1)} collective-permute-done((f32[608,128]{1,0:T(8,128)S(1)}, f32[608,128]{1,0:T(8,128)S(1)}, u32[]{:S(2)}, u32[]{:S(2)}) %collective-permute-start.6) | collective-permute-done | bytes 311328 | tf_op jit(solution)/shard_map/filter_grad_sum/ppermute | solution.py:251
  89.2 1.5 %collective-permute-start.7 = (f32[304,128]{1,0:T(8,128)S(1)}, f32[304,128]{1,0:T(8,128)S(1)}, u32[]{:S(2)}, u32[]{:S(2)}) collective-permute-start(f32[304,128]{1,0:T(8,128)S(1)} %slice_select_fusion.2), channel_id=1, source_target_pairs={{0,8},{8,0},{16,24},{24,16},{1,9},{9,1},{17,25},{25,17},{2,10},{10... | collective-permute-start | bytes 466952 | tf_op jit(solution)/shard_map/filter_grad_sum/ppermute | solution.py:251
  90.7 4.6 %collective-permute-done.7 = f32[304,128]{1,0:T(8,128)S(1)} collective-permute-done((f32[304,128]{1,0:T(8,128)S(1)}, f32[304,128]{1,0:T(8,128)S(1)}, u32[]{:S(2)}, u32[]{:S(2)}) %collective-permute-start.7) | collective-permute-done | bytes 155680 | tf_op jit(solution)/shard_map/filter_grad_sum/ppermute | solution.py:251
  95.3 1.6 %collective-permute-start.8 = (f32[152,128]{1,0:T(8,128)S(1)}, f32[152,128]{1,0:T(8,128)S(1)}, u32[]{:S(2)}, u32[]{:S(2)}) collective-permute-start(f32[152,128]{1,0:T(8,128)S(1)} %slice_select_fusion.3), channel_id=1, source_target_pairs={{0,16},{8,24},{16,0},{24,8},{1,17},{9,25},{17,1},{25,9},{2,18},{10... | collective-permute-start | bytes 233480 | tf_op jit(solution)/shard_map/filter_grad_sum/ppermute | solution.py:251
  96.9 2.9 %collective-permute-done.8 = f32[152,128]{1,0:T(8,128)S(1)} collective-permute-done((f32[152,128]{1,0:T(8,128)S(1)}, f32[152,128]{1,0:T(8,128)S(1)}, u32[]{:S(2)}, u32[]{:S(2)}) %collective-permute-start.8) | collective-permute-done | bytes 77856 | tf_op jit(solution)/shard_map/filter_grad_sum/ppermute | solution.py:251
  99.8 1.6 %collective-permute-start.9 = (f32[76,128]{1,0:T(8,128)S(1)}, f32[76,128]{1,0:T(8,128)S(1)}, u32[]{:S(2)}, u32[]{:S(2)}) collective-permute-start(f32[76,128]{1,0:T(8,128)S(1)} %slice_select_fusion.4), channel_id=1, source_target_pairs={{0,2},{1,3},{2,0},{3,1},{4,6},{5,7},{6,4},{7,5},{8,10},{9,11},{10,... | collective-permute-start | bytes 116744 | tf_op jit(solution)/shard_map/filter_grad_sum/ppermute | solution.py:251
  101.5 2.4 %collective-permute-done.9 = f32[76,128]{1,0:T(8,128)S(1)} collective-permute-done((f32[76,128]{1,0:T(8,128)S(1)}, f32[76,128]{1,0:T(8,128)S(1)}, u32[]{:S(2)}, u32[]{:S(2)}) %collective-permute-start.9) | collective-permute-done | bytes 38944 | tf_op jit(solution)/shard_map/filter_grad_sum/ppermute | solution.py:251
  103.9 2.9 %collective-permute-start.10 = (f32[38,128]{1,0:T(8,128)S(1)}, f32[38,128]{1,0:T(8,128)S(1)}, u32[]{:S(2)}, u32[]{:S(2)}) collective-permute-start(f32[38,128]{1,0:T(8,128)S(1)} %slice_select_fusion.5), channel_id=1, source_target_pairs={{0,4},{1,5},{2,6},{3,7},{4,0},{5,1},{6,2},{7,3},{8,12},{9,13},{10,... | collective-permute-start | bytes 58376 | tf_op jit(solution)/shard_map/filter_grad_sum/ppermute | solution.py:251
  106.8 1.9 %collective-permute-done.10 = f32[38,128]{1,0:T(8,128)S(1)} collective-permute-done((f32[38,128]{1,0:T(8,128)S(1)}, f32[38,128]{1,0:T(8,128)S(1)}, u32[]{:S(2)}, u32[]{:S(2)}) %collective-permute-start.10) | collective-permute-done | bytes 19488 | tf_op jit(solution)/shard_map/filter_grad_sum/ppermute | solution.py:251
  108.7 3.0 %collective-permute-start.11 = (f32[38,128]{1,0:T(8,128)S(1)}, f32[38,128]{1,0:T(8,128)S(1)}, u32[]{:S(2)}, u32[]{:S(2)}) collective-permute-start(f32[38,128]{1,0:T(8,128)S(1)} %select_add_fusion.5), channel_id=1, source_target_pairs={{0,4},{1,5},{2,6},{3,7},{4,0},{5,1},{6,2},{7,3},{8,12},{9,13},{10,... | collective-permute-start | bytes 58376 | tf_op jit(solution)/shard_map/filter_grad_sum/ppermute | solution.py:251
  111.7 1.8 %collective-permute-done.11 = f32[38,128]{1,0:T(8,128)S(1)} collective-permute-done((f32[38,128]{1,0:T(8,128)S(1)}, f32[38,128]{1,0:T(8,128)S(1)}, u32[]{:S(2)}, u32[]{:S(2)}) %collective-permute-start.11) | collective-permute-done | bytes 19488 | tf_op jit(solution)/shard_map/filter_grad_sum/ppermute | solution.py:251
  113.5 1.7 %collective-permute-start.12 = (f32[76,128]{1,0:T(8,128)S(1)}, f32[76,128]{1,0:T(8,128)S(1)}, u32[]{:S(2)}, u32[]{:S(2)}) collective-permute-start(f32[76,128]{1,0:T(8,128)S(1)} %maximum_select_fusion.4), channel_id=1, source_target_pairs={{0,2},{1,3},{2,0},{3,1},{4,6},{5,7},{6,4},{7,5},{8,10},{9,11},{10,... | collective-permute-start | bytes 116744 | tf_op jit(solution)/shard_map/filter_grad_sum/ppermute | solution.py:251
  117.5 2.6 %collective-permute-start.13 = (f32[152,128]{1,0:T(8,128)S(1)}, f32[152,128]{1,0:T(8,128)S(1)}, u32[]{:S(2)}, u32[]{:S(2)}) collective-permute-start(f32[152,128]{1,0:T(8,128)S(1)} %maximum_select_fusion.3), channel_id=1, source_target_pairs={{0,16},{8,24},{16,0},{24,8},{1,17},{9,25},{17,1},{25,9},{2,18},{10... | collective-permute-start | bytes 233480 | tf_op jit(solution)/shard_map/filter_grad_sum/ppermute | solution.py:251
  120.1 2.3 %collective-permute-done.13 = f32[152,128]{1,0:T(8,128)S(1)} collective-permute-done((f32[152,128]{1,0:T(8,128)S(1)}, f32[152,128]{1,0:T(8,128)S(1)}, u32[]{:S(2)}, u32[]{:S(2)}) %collective-permute-start.13) | collective-permute-done | bytes 77856 | tf_op jit(solution)/shard_map/filter_grad_sum/ppermute | solution.py:251
  122.5 2.0 %collective-permute-start.14 = (f32[304,128]{1,0:T(8,128)S(1)}, f32[304,128]{1,0:T(8,128)S(1)}, u32[]{:S(2)}, u32[]{:S(2)}) collective-permute-start(f32[304,128]{1,0:T(8,128)S(1)} %maximum_select_fusion.2), channel_id=1, source_target_pairs={{0,8},{8,0},{16,24},{24,16},{1,9},{9,1},{17,25},{25,17},{2,10},{10... | collective-permute-start | bytes 466952 | tf_op jit(solution)/shard_map/filter_grad_sum/ppermute | solution.py:251
  124.5 2.0 %collective-permute-done.5 = f32[3,8,4096]{2,1,0:T(8,128)S(1)} collective-permute-done((f32[3,8,4096]{2,1,0:T(8,128)S(1)}, f32[3,8,4096]{2,1,0:T(8,128)S(1)}, u32[]{:S(2)}, u32[]{:S(2)}) %collective-permute-start.5) | collective-permute-done | bytes 393248 | tf_op jit(solution)/shard_map/ppermute | solution.py:20
  (72 shorter events, 20.0 us)
Async XLA Ops:
  0.6 6.9 %copy-start.1 = (f32[16,4096]{1,0:T(8,128)S(1)}, f32[16,4096]{1,0:T(8,128)}, u32[]{:S(2)}) copy-start(f32[16,4096]{1,0:T(8,128)} %param.15) | copy-start | bytes 786436
  0.6 7.6 %copy-start = (f32[3,7,4096]{2,1,0:T(8,128)S(1)}, f32[3,7,4096]{2,1,0:T(8,128)}, u32[]{:S(2)}) copy-start(f32[3,7,4096]{2,1,0:T(8,128)} %taps_ref.3) | copy-start | bytes 1032196
  2.6 20.6 %collective-permute-start = (bf16[3,8,4096]{2,1,0:T(8,128)(2,1)S(1)}, bf16[3,8,4096]{2,1,0:T(8,128)(2,1)S(1)}, u32[]{:S(2)}, u32[]{:S(2)}) collective-permute-start(bf16[3,8,4096]{2,1,0:T(8,128)(2,1)S(1)} %pad_maximum_fusion.1), channel_id=1, source_target_pairs={{0,8},{8,16},{16,24},{1,9},{9,17},{17,25},{2,10},{10,18},{18,26},{... | collective-permute-start | bytes 589832 | tf_op jit(solution)/shard_map/ppermute | solution.py:20
  23.2 0.9 copy-start.2
  25.1 1.0 copy-start.5
  25.1 2.5 %copy-start.4 = (f32[16,4096]{1,0:T(8,128)S(1)}, f32[16,4096]{1,0:T(8,128)}, u32[]{:S(2)}) copy-start(f32[16,4096]{1,0:T(8,128)} %get-tuple-element.17) | copy-start | bytes 786436
  26.1 9.2 %collective-permute-start.1 = (f32[16,4096]{1,0:T(8,128)S(1)}, f32[16,4096]{1,0:T(8,128)S(1)}, u32[]{:S(2)}, u32[]{:S(2)}) collective-permute-start(f32[16,4096]{1,0:T(8,128)S(1)} %add.138), channel_id=1, source_target_pairs={{0,8},{8,0},{16,24},{24,16},{1,9},{9,1},{17,25},{25,17},{2,10},{10... | collective-permute-start | bytes 786440 | tf_op jit(solution)/shard_map/modal_state_scan/ppermute | solution.py:251
  27.6 11.9 %collective-permute-start.2 = (f32[16,4096]{1,0:T(8,128)S(1)}, f32[16,4096]{1,0:T(8,128)S(1)}, u32[]{:S(2)}, u32[]{:S(2)}) collective-permute-start(f32[16,4096]{1,0:T(8,128)S(1)} %add.140), channel_id=1, source_target_pairs={{0,8},{8,0},{16,24},{24,16},{1,9},{9,1},{17,25},{25,17},{2,10},{10... | collective-permute-start | bytes 786440 | tf_op jit(solution)/shard_map/modal_state_scan/ppermute | solution.py:251
  39.7 5.6 %collective-permute-start.3 = (f32[16,2048]{1,0:T(8,128)S(1)}, f32[16,2048]{1,0:T(8,128)S(1)}, u32[]{:S(2)}, u32[]{:S(2)}) collective-permute-start(f32[16,2048]{1,0:T(8,128)S(1)} %get-tuple-element.52), channel_id=1, source_target_pairs={{0,16},{8,24},{16,0},{24,8},{1,17},{9,25},{17,1},{25,9},{2,18},{10... | collective-permute-start | bytes 393224 | tf_op jit(solution)/shard_map/modal_state_scan/ppermute | solution.py:251
  41.2 5.4 %collective-permute-start.4 = (f32[16,2048]{1,0:T(8,128)S(1)}, f32[16,2048]{1,0:T(8,128)S(1)}, u32[]{:S(2)}, u32[]{:S(2)}) collective-permute-start(f32[16,2048]{1,0:T(8,128)S(1)} %get-tuple-element.51), channel_id=1, source_target_pairs={{0,16},{8,24},{16,0},{24,8},{1,17},{9,25},{17,1},{25,9},{2,18},{10... | collective-permute-start | bytes 393224 | tf_op jit(solution)/shard_map/modal_state_scan/ppermute | solution.py:251
  87.4 1.7 %collective-permute-start.6 = (f32[608,128]{1,0:T(8,128)S(1)}, f32[608,128]{1,0:T(8,128)S(1)}, u32[]{:S(2)}, u32[]{:S(2)}) collective-permute-start(f32[608,128]{1,0:T(8,128)S(1)} %select_n.211), channel_id=1, source_target_pairs={{0,1},{1,0},{2,3},{3,2},{4,5},{5,4},{6,7},{7,6},{8,9},{9,8},{10,11... | collective-permute-start | bytes 933896 | tf_op jit(solution)/shard_map/filter_grad_sum/ppermute | solution.py:251
  89.1 26.0 %copy-start.6 = (f32[3,8,4096]{2,1,0:T(8,128)S(1)}, f32[3,8,4096]{2,1,0:T(8,128)}, u32[]{:S(2)}) copy-start(f32[3,8,4096]{2,1,0:T(8,128)} %get-tuple-element.21) | copy-start | bytes 1179652
  89.2 37.3 %copy-start.3 = (f32[3,16,4096]{2,1,0:T(8,128)S(1)}, f32[3,16,4096]{2,1,0:T(8,128)}, u32[]{:S(2)}) copy-start(f32[3,16,4096]{2,1,0:T(8,128)} %get-tuple-element.20) | copy-start | bytes 2359300
  89.2 6.1 %collective-permute-start.7 = (f32[304,128]{1,0:T(8,128)S(1)}, f32[304,128]{1,0:T(8,128)S(1)}, u32[]{:S(2)}, u32[]{:S(2)}) collective-permute-start(f32[304,128]{1,0:T(8,128)S(1)} %slice_select_fusion.2), channel_id=1, source_target_pairs={{0,8},{8,0},{16,24},{24,16},{1,9},{9,1},{17,25},{25,17},{2,10},{10... | collective-permute-start | bytes 466952 | tf_op jit(solution)/shard_map/filter_grad_sum/ppermute | solution.py:251
  95.3 4.5 %collective-permute-start.8 = (f32[152,128]{1,0:T(8,128)S(1)}, f32[152,128]{1,0:T(8,128)S(1)}, u32[]{:S(2)}, u32[]{:S(2)}) collective-permute-start(f32[152,128]{1,0:T(8,128)S(1)} %slice_select_fusion.3), channel_id=1, source_target_pairs={{0,16},{8,24},{16,0},{24,8},{1,17},{9,25},{17,1},{25,9},{2,18},{10... | collective-permute-start | bytes 233480 | tf_op jit(solution)/shard_map/filter_grad_sum/ppermute | solution.py:251
  99.8 4.1 %collective-permute-start.9 = (f32[76,128]{1,0:T(8,128)S(1)}, f32[76,128]{1,0:T(8,128)S(1)}, u32[]{:S(2)}, u32[]{:S(2)}) collective-permute-start(f32[76,128]{1,0:T(8,128)S(1)} %slice_select_fusion.4), channel_id=1, source_target_pairs={{0,2},{1,3},{2,0},{3,1},{4,6},{5,7},{6,4},{7,5},{8,10},{9,11},{10,... | collective-permute-start | bytes 116744 | tf_op jit(solution)/shard_map/filter_grad_sum/ppermute | solution.py:251
  103.9 4.7 %collective-permute-start.10 = (f32[38,128]{1,0:T(8,128)S(1)}, f32[38,128]{1,0:T(8,128)S(1)}, u32[]{:S(2)}, u32[]{:S(2)}) collective-permute-start(f32[38,128]{1,0:T(8,128)S(1)} %slice_select_fusion.5), channel_id=1, source_target_pairs={{0,4},{1,5},{2,6},{3,7},{4,0},{5,1},{6,2},{7,3},{8,12},{9,13},{10,... | collective-permute-start | bytes 58376 | tf_op jit(solution)/shard_map/filter_grad_sum/ppermute | solution.py:251
  108.7 4.7 %collective-permute-start.11 = (f32[38,128]{1,0:T(8,128)S(1)}, f32[38,128]{1,0:T(8,128)S(1)}, u32[]{:S(2)}, u32[]{:S(2)}) collective-permute-start(f32[38,128]{1,0:T(8,128)S(1)} %select_add_fusion.5), channel_id=1, source_target_pairs={{0,4},{1,5},{2,6},{3,7},{4,0},{5,1},{6,2},{7,3},{8,12},{9,13},{10,... | collective-permute-start | bytes 58376 | tf_op jit(solution)/shard_map/filter_grad_sum/ppermute | solution.py:251
  113.5 4.1 %collective-permute-start.12 = (f32[76,128]{1,0:T(8,128)S(1)}, f32[76,128]{1,0:T(8,128)S(1)}, u32[]{:S(2)}, u32[]{:S(2)}) collective-permute-start(f32[76,128]{1,0:T(8,128)S(1)} %maximum_select_fusion.4), channel_id=1, source_target_pairs={{0,2},{1,3},{2,0},{3,1},{4,6},{5,7},{6,4},{7,5},{8,10},{9,11},{10,... | collective-permute-start | bytes 116744 | tf_op jit(solution)/shard_map/filter_grad_sum/ppermute | solution.py:251
  115.2 11.3 %collective-permute-start.5 = (f32[3,8,4096]{2,1,0:T(8,128)S(1)}, f32[3,8,4096]{2,1,0:T(8,128)S(1)}, u32[]{:S(2)}, u32[]{:S(2)}) collective-permute-start(f32[3,8,4096]{2,1,0:T(8,128)S(1)} %copy-done.6), channel_id=1, source_target_pairs={{8,0},{16,8},{24,16},{9,1},{17,9},{25,17},{10,2},{18,10},{26,18},{... | collective-permute-start | bytes 1179656 | tf_op jit(solution)/shard_map/ppermute | solution.py:20
  117.5 4.9 %collective-permute-start.13 = (f32[152,128]{1,0:T(8,128)S(1)}, f32[152,128]{1,0:T(8,128)S(1)}, u32[]{:S(2)}, u32[]{:S(2)}) collective-permute-start(f32[152,128]{1,0:T(8,128)S(1)} %maximum_select_fusion.3), channel_id=1, source_target_pairs={{0,16},{8,24},{16,0},{24,8},{1,17},{9,25},{17,1},{25,9},{2,18},{10... | collective-permute-start | bytes 233480 | tf_op jit(solution)/shard_map/filter_grad_sum/ppermute | solution.py:251
  122.5 5.6 %collective-permute-start.14 = (f32[304,128]{1,0:T(8,128)S(1)}, f32[304,128]{1,0:T(8,128)S(1)}, u32[]{:S(2)}, u32[]{:S(2)}) collective-permute-start(f32[304,128]{1,0:T(8,128)S(1)} %maximum_select_fusion.2), channel_id=1, source_target_pairs={{0,8},{8,0},{16,24},{24,16},{1,9},{9,1},{17,25},{25,17},{2,10},{10... | collective-permute-start | bytes 466952 | tf_op jit(solution)/shard_map/filter_grad_sum/ppermute | solution.py:251
  128.2 1.7 %collective-permute-start.15 = (f32[608,128]{1,0:T(8,128)S(1)}, f32[608,128]{1,0:T(8,128)S(1)}, u32[]{:S(2)}, u32[]{:S(2)}) collective-permute-start(f32[608,128]{1,0:T(8,128)S(1)} %maximum_select_fusion.1), channel_id=1, source_target_pairs={{0,1},{1,0},{2,3},{3,2},{4,5},{5,4},{6,7},{7,6},{8,9},{9,8},{10,11... | collective-permute-start | bytes 933896 | tf_op jit(solution)/shard_map/filter_grad_sum/ppermute | solution.py:251

commit v7 on v6

--- a/solution.py
+++ b/solution.py
@@ -255,9 +255,29 @@
     return jnp.exp(-decay * (rows * steps).astype(F32))
 
 
+def scan_four(final_f, final_b, decay, rows, axis, mine):
+    jump = jnp.exp(-decay * float(rows))
+    got = exchange(jnp.where(mine % 2 == 1, final_b, final_f), axis, 1)
+    pair_f = final_f + jump * got
+    pair_b = final_b + jump * got
+    sent = jnp.where(mine == 1, pair_f, pair_b)
+    across = lax.ppermute(sent, axis, [(1, 3), (2, 0)])
+    diagonal = lax.ppermute(sent, axis, [(1, 2), (2, 1)])
+    zero = jnp.zeros_like(final_f)
+    incoming_f = jnp.where(
+        mine == 3, got + jump * across, jnp.where(mine == 2, diagonal, jnp.where(mine == 1, got, zero))
+    )
+    incoming_b = jnp.where(
+        mine == 0, got + jump * across, jnp.where(mine == 1, diagonal, jnp.where(mine == 2, got, zero))
+    )
+    return (incoming_f, incoming_b)
+
+
 def scan_states(final_f, final_b, decay, rows, axis):
     count = lax.axis_size(axis)
     mine = lax.axis_index(axis)
+    if count == 4:
+        return scan_four(final_f, final_b, decay, rows, axis, mine)
     block_f, block_b = (final_f, final_b)
     incoming_f = jnp.zeros_like(final_f)
     incoming_b = jnp.zeros_like(final_b)

time: 132 us -> 131 us (level)
  starting transfers between devices: 27.4 us -> 23.6 us
  waiting for transfers between devices: 38.6 us -> 40.8 us
    ppermute x0 -> x2, waiting for transfers between devices: none -> 9.01 us  [the longest x1 9.01 us: scan_four(): across = lax.ppermute(sent, axis, [(1, 3), (2, 0)])]
    ppermute x14 -> x11, waiting for transfers between devices: 36.6 us -> 29.8 us  [exchange(): return lax.ppermute(x, axis, [(i, i ^ size) for i in range(count)])]
    ppermute x14 -> x11, starting transfers between devices: 21.2 us -> 15.5 us  [exchange(): return lax.ppermute(x, axis, [(i, i ^ size) for i in range(count)])]
    ppermute x0 -> x2, starting transfers between devices: none -> 1.97 us  [the longest x1 1.29 us: scan_four(): across = lax.ppermute(sent, axis, [(1, 3), (2, 0)])]
  transfers between devices with their start and end apart: 16 -> 15, of which waited for: 15 -> 13; matrix products, arithmetic and copies ran while one was open for 3% -> 3% of each run, Pallas kernels for 10% -> 10%
where the time goes in v7:
time: 131 us; the launch traced here: 130 us
  Pallas kernels  52.2 us (40%)
  waiting for transfers between devices  40.8 us (31%)
  starting transfers between devices  23.6 us (18%)
  local copies, waits for them, and re-layouts  6.55 us (5%)
  other arithmetic  6.29 us (5%)
    pallas_call x1, Pallas kernels, run_main(): pl.pallas_call(main_kernel, grid=(width // lanes,), in_specs=[tile(x.shap...  38.5 us
    ppermute x11, waiting for transfers between devices, exchange(): return lax.ppermute(x, axis, [(i, i ^ size) for i in range(count)])  29.8 us
    ppermute x11, starting transfers between devices, exchange(): return lax.ppermute(x, axis, [(i, i ^ size) for i in range(count)])  15.5 us
    pallas_call x1, Pallas kernels, run_states(): pl.pallas_call(states_kernel, grid=(width // lanes,), in_specs=[tile(x.sh...  13.7 us
    ppermute x1, waiting for transfers between devices, scan_four(): across = lax.ppermute(sent, axis, [(1, 3), (2, 0)])  9.01 us
    ppermute x2, starting transfers between devices, passed_along(): return lax.ppermute(x, axis, pairs)  6.16 us
  transfers between devices with their start and end apart: 15, of which 13 were waited for; matrix products, arithmetic and copies ran while one was open for 3% of the time, Pallas kernels for 10%

profile of v7, /device:TPU:0, one launch (start us, length us, event | category | flops | bytes accessed | tf_op | source)
XLA Modules:
  0.0 130.4 jit_solution(586067001340428045)
XLA Ops:
  2.6 4.9 %collective-permute-start = (bf16[3,8,4096]{2,1,0:T(8,128)(2,1)S(1)}, bf16[3,8,4096]{2,1,0:T(8,128)(2,1)S(1)}, u32[]{:S(2)}, u32[]{:S(2)}) collective-permute-start(bf16[3,8,4096]{2,1,0:T(8,128)(2,1)S(1)} %pad_maximum_fusion.1), channel_id=1, source_target_pairs={{0,8},{8,16},{16,24},{1,9},{9,17},{17,25},{2,10},{10,18},{18,26},{... | collective-permute-start | bytes 589832 | tf_op jit(solution)/shard_map/ppermute | solution.py:20
  9.6 13.7 %shard_map.135 = (f32[16,4096]{1,0:T(8,128)}, f32[16,4096]{1,0:T(8,128)}) custom-call(bf16[128,4096]{1,0:T(8,128)(2,1)} %bitcast.33, bf16[128,4096]{1,0:T(8,128)(2,1)} %bitcast.35, bf16[128,4096]{1,0:T(8,128)(2,1)} %bitcast.37, bf16[128,4096]{1,0:T(8,128)(2,1)} %bitcast.39, bf16[3,8,4096]{2,1,0:T(8,128)(2,1)} %broadcast_in_dim.14.rim_ref, ...), custom_call_target="tpu_custom_call" | custom-call | tf_op jit(solution)/shard_map/pallas_call | solution.py:201
  26.1 1.5 %collective-permute-start.1 = (f32[16,4096]{1,0:T(8,128)S(1)}, f32[16,4096]{1,0:T(8,128)S(1)}, u32[]{:S(2)}, u32[]{:S(2)}) collective-permute-start(f32[16,4096]{1,0:T(8,128)S(1)} %get-tuple-element.27), channel_id=1, source_target_pairs={{0,8},{8,0},{16,24},{24,16},{1,9},{9,1},{17,25},{25,17},{2,10},{10... | collective-permute-start | bytes 786440 | tf_op jit(solution)/shard_map/modal_state_scan/ppermute | solution.py:251
  27.7 6.3 %collective-permute-done.1 = f32[16,4096]{1,0:T(8,128)S(1)} collective-permute-done((f32[16,4096]{1,0:T(8,128)S(1)}, f32[16,4096]{1,0:T(8,128)S(1)}, u32[]{:S(2)}, u32[]{:S(2)}) %collective-permute-start.1) | collective-permute-done | bytes 262176 | tf_op jit(solution)/shard_map/modal_state_scan/ppermute | solution.py:251
  34.7 1.3 collective-permute-start.2
  36.1 9.0 %collective-permute-done.2 = f32[16,4096]{1,0:T(8,128)S(1)} collective-permute-done((f32[16,4096]{1,0:T(8,128)S(1)}, f32[16,4096]{1,0:T(8,128)S(1)}, u32[]{:S(2)}, u32[]{:S(2)}) %collective-permute-start.2) | collective-permute-done | bytes 262176 | tf_op jit(solution)/shard_map/modal_state_scan/ppermute | solution.py:264
  46.0 38.5 %shard_map.136 = (bf16[128,4096]{1,0:T(8,128)(2,1)}, bf16[128,4096]{1,0:T(8,128)(2,1)}, bf16[128,4096]{1,0:T(8,128)(2,1)}, bf16[128,4096]{1,0:T(8,128)(2,1)}, f3...) custom-call(bf16[128,4096]{1,0:T(8,128)(2,1)} %bitcast.34, bf16[128,4096]{1,0:T(8,128)(2,1)} %bitcast.36, ...), custom_call_target="tpu_custom_call" | custom-call | tf_op jit(solution)/shard_map/pallas_call | solution.py:231
  84.5 1.2 slice_select_fusion
  85.9 1.5 %collective-permute-done.5 = f32[608,128]{1,0:T(8,128)S(1)} collective-permute-done((f32[608,128]{1,0:T(8,128)S(1)}, f32[608,128]{1,0:T(8,128)S(1)}, u32[]{:S(2)}, u32[]{:S(2)}) %collective-permute-start.5) | collective-permute-done | bytes 311328 | tf_op jit(solution)/shard_map/filter_grad_sum/ppermute | solution.py:251
  87.7 5.9 %collective-permute-done.6 = f32[304,128]{1,0:T(8,128)S(1)} collective-permute-done((f32[304,128]{1,0:T(8,128)S(1)}, f32[304,128]{1,0:T(8,128)S(1)}, u32[]{:S(2)}, u32[]{:S(2)}) %collective-permute-start.6) | collective-permute-done | bytes 155680 | tf_op jit(solution)/shard_map/filter_grad_sum/ppermute | solution.py:251
  94.1 4.1 %collective-permute-done.7 = f32[152,128]{1,0:T(8,128)S(1)} collective-permute-done((f32[152,128]{1,0:T(8,128)S(1)}, f32[152,128]{1,0:T(8,128)S(1)}, u32[]{:S(2)}, u32[]{:S(2)}) %collective-permute-start.7) | collective-permute-done | bytes 77856 | tf_op jit(solution)/shard_map/filter_grad_sum/ppermute | solution.py:251
  98.2 1.6 %collective-permute-start.8 = (f32[76,128]{1,0:T(8,128)S(1)}, f32[76,128]{1,0:T(8,128)S(1)}, u32[]{:S(2)}, u32[]{:S(2)}) collective-permute-start(f32[76,128]{1,0:T(8,128)S(1)} %slice_select_fusion.4), channel_id=1, source_target_pairs={{0,2},{1,3},{2,0},{3,1},{4,6},{5,7},{6,4},{7,5},{8,10},{9,11},{10,... | collective-permute-start | bytes 116744 | tf_op jit(solution)/shard_map/filter_grad_sum/ppermute | solution.py:251
  99.8 2.4 %collective-permute-done.8 = f32[76,128]{1,0:T(8,128)S(1)} collective-permute-done((f32[76,128]{1,0:T(8,128)S(1)}, f32[76,128]{1,0:T(8,128)S(1)}, u32[]{:S(2)}, u32[]{:S(2)}) %collective-permute-start.8) | collective-permute-done | bytes 38944 | tf_op jit(solution)/shard_map/filter_grad_sum/ppermute | solution.py:251
  102.3 2.9 %collective-permute-start.9 = (f32[38,128]{1,0:T(8,128)S(1)}, f32[38,128]{1,0:T(8,128)S(1)}, u32[]{:S(2)}, u32[]{:S(2)}) collective-permute-start(f32[38,128]{1,0:T(8,128)S(1)} %slice_select_fusion.5), channel_id=1, source_target_pairs={{0,4},{1,5},{2,6},{3,7},{4,0},{5,1},{6,2},{7,3},{8,12},{9,13},{10,... | collective-permute-start | bytes 58376 | tf_op jit(solution)/shard_map/filter_grad_sum/ppermute | solution.py:251
  105.1 1.9 %collective-permute-done.9 = f32[38,128]{1,0:T(8,128)S(1)} collective-permute-done((f32[38,128]{1,0:T(8,128)S(1)}, f32[38,128]{1,0:T(8,128)S(1)}, u32[]{:S(2)}, u32[]{:S(2)}) %collective-permute-start.9) | collective-permute-done | bytes 19488 | tf_op jit(solution)/shard_map/filter_grad_sum/ppermute | solution.py:251
  107.0 3.0 %collective-permute-start.10 = (f32[38,128]{1,0:T(8,128)S(1)}, f32[38,128]{1,0:T(8,128)S(1)}, u32[]{:S(2)}, u32[]{:S(2)}) collective-permute-start(f32[38,128]{1,0:T(8,128)S(1)} %select_add_fusion.3), channel_id=1, source_target_pairs={{0,4},{1,5},{2,6},{3,7},{4,0},{5,1},{6,2},{7,3},{8,12},{9,13},{10,... | collective-permute-start | bytes 58376 | tf_op jit(solution)/shard_map/filter_grad_sum/ppermute | solution.py:251
  110.0 1.8 %collective-permute-done.10 = f32[38,128]{1,0:T(8,128)S(1)} collective-permute-done((f32[38,128]{1,0:T(8,128)S(1)}, f32[38,128]{1,0:T(8,128)S(1)}, u32[]{:S(2)}, u32[]{:S(2)}) %collective-permute-start.10) | collective-permute-done | bytes 19488 | tf_op jit(solution)/shard_map/filter_grad_sum/ppermute | solution.py:251
  111.8 1.7 %collective-permute-start.11 = (f32[76,128]{1,0:T(8,128)S(1)}, f32[76,128]{1,0:T(8,128)S(1)}, u32[]{:S(2)}, u32[]{:S(2)}) collective-permute-start(f32[76,128]{1,0:T(8,128)S(1)} %maximum_select_fusion.4), channel_id=1, source_target_pairs={{0,2},{1,3},{2,0},{3,1},{4,6},{5,7},{6,4},{7,5},{8,10},{9,11},{10,... | collective-permute-start | bytes 116744 | tf_op jit(solution)/shard_map/filter_grad_sum/ppermute | solution.py:251
  113.5 1.3 collective-permute-start.4
  115.9 1.5 %collective-permute-start.12 = (f32[152,128]{1,0:T(8,128)S(1)}, f32[152,128]{1,0:T(8,128)S(1)}, u32[]{:S(2)}, u32[]{:S(2)}) collective-permute-start(f32[152,128]{1,0:T(8,128)S(1)} %maximum_select_fusion.3), channel_id=1, source_target_pairs={{0,16},{8,24},{16,0},{24,8},{1,17},{9,25},{17,1},{25,9},{2,18},{10... | collective-permute-start | bytes 233480 | tf_op jit(solution)/shard_map/filter_grad_sum/ppermute | solution.py:251
  117.4 2.9 %collective-permute-done.12 = f32[152,128]{1,0:T(8,128)S(1)} collective-permute-done((f32[152,128]{1,0:T(8,128)S(1)}, f32[152,128]{1,0:T(8,128)S(1)}, u32[]{:S(2)}, u32[]{:S(2)}) %collective-permute-start.12) | collective-permute-done | bytes 77856 | tf_op jit(solution)/shard_map/filter_grad_sum/ppermute | solution.py:251
  120.4 2.5 %collective-permute-start.13 = (f32[304,128]{1,0:T(8,128)S(1)}, f32[304,128]{1,0:T(8,128)S(1)}, u32[]{:S(2)}, u32[]{:S(2)}) collective-permute-start(f32[304,128]{1,0:T(8,128)S(1)} %maximum_select_fusion.2), channel_id=1, source_target_pairs={{0,8},{8,0},{16,24},{24,16},{1,9},{9,1},{17,25},{25,17},{2,10},{10... | collective-permute-start | bytes 466952 | tf_op jit(solution)/shard_map/filter_grad_sum/ppermute | solution.py:251
  122.9 1.9 %collective-permute-done.4 = f32[3,8,4096]{2,1,0:T(8,128)S(1)} collective-permute-done((f32[3,8,4096]{2,1,0:T(8,128)S(1)}, f32[3,8,4096]{2,1,0:T(8,128)S(1)}, u32[]{:S(2)}, u32[]{:S(2)}) %collective-permute-start.4) | collective-permute-done | bytes 393248 | tf_op jit(solution)/shard_map/ppermute | solution.py:20
  125.3 1.1 collective-permute-done.13
  (66 shorter events, 15.0 us)
Async XLA Ops:
  0.6 6.9 %copy-start = (f32[3,7,4096]{2,1,0:T(8,128)S(1)}, f32[3,7,4096]{2,1,0:T(8,128)}, u32[]{:S(2)}) copy-start(f32[3,7,4096]{2,1,0:T(8,128)} %taps_ref.3) | copy-start | bytes 1032196
  0.6 7.1 %copy-start.1 = (f32[16,4096]{1,0:T(8,128)S(1)}, f32[16,4096]{1,0:T(8,128)}, u32[]{:S(2)}) copy-start(f32[16,4096]{1,0:T(8,128)} %param.15) | copy-start | bytes 786436
  2.6 20.6 %collective-permute-start = (bf16[3,8,4096]{2,1,0:T(8,128)(2,1)S(1)}, bf16[3,8,4096]{2,1,0:T(8,128)(2,1)S(1)}, u32[]{:S(2)}, u32[]{:S(2)}) collective-permute-start(bf16[3,8,4096]{2,1,0:T(8,128)(2,1)S(1)} %pad_maximum_fusion.1), channel_id=1, source_target_pairs={{0,8},{8,16},{16,24},{1,9},{9,17},{17,25},{2,10},{10,18},{18,26},{... | collective-permute-start | bytes 589832 | tf_op jit(solution)/shard_map/ppermute | solution.py:20
  23.2 0.9 copy-start.2
  25.0 1.0 copy-start.4
  25.1 1.0 copy-start.5
  26.1 7.8 %collective-permute-start.1 = (f32[16,4096]{1,0:T(8,128)S(1)}, f32[16,4096]{1,0:T(8,128)S(1)}, u32[]{:S(2)}, u32[]{:S(2)}) collective-permute-start(f32[16,4096]{1,0:T(8,128)S(1)} %get-tuple-element.27), channel_id=1, source_target_pairs={{0,8},{8,0},{16,24},{24,16},{1,9},{9,1},{17,25},{25,17},{2,10},{10... | collective-permute-start | bytes 786440 | tf_op jit(solution)/shard_map/modal_state_scan/ppermute | solution.py:251
  34.0 2.0 %collective-permute-start.3 = (f32[16,4096]{1,0:T(8,128)S(1)}, f32[16,4096]{1,0:T(8,128)S(1)}, u32[]{:S(2)}, u32[]{:S(2)}) collective-permute-start(f32[16,4096]{1,0:T(8,128)S(1)} %add_select_fusion), channel_id=1, source_target_pairs={{8,16},{16,8},{9,17},{17,9},{10,18},{18,10},{11,19},{19,11},{12,20... | collective-permute-start | bytes 786440 | tf_op jit(solution)/shard_map/modal_state_scan/ppermute | solution.py:265
  34.7 10.3 %collective-permute-start.2 = (f32[16,4096]{1,0:T(8,128)S(1)}, f32[16,4096]{1,0:T(8,128)S(1)}, u32[]{:S(2)}, u32[]{:S(2)}) collective-permute-start(f32[16,4096]{1,0:T(8,128)S(1)} %add_select_fusion), channel_id=1, source_target_pairs={{8,24},{16,0},{9,25},{17,1},{10,26},{18,2},{11,27},{19,3},{12,28},... | collective-permute-start | bytes 786440 | tf_op jit(solution)/shard_map/modal_state_scan/ppermute | solution.py:264
  85.8 1.7 %collective-permute-start.5 = (f32[608,128]{1,0:T(8,128)S(1)}, f32[608,128]{1,0:T(8,128)S(1)}, u32[]{:S(2)}, u32[]{:S(2)}) collective-permute-start(f32[608,128]{1,0:T(8,128)S(1)} %select_n.213), channel_id=1, source_target_pairs={{0,1},{1,0},{2,3},{3,2},{4,5},{5,4},{6,7},{7,6},{8,9},{9,8},{10,11... | collective-permute-start | bytes 933896 | tf_op jit(solution)/shard_map/filter_grad_sum/ppermute | solution.py:251
  87.5 26.0 %copy-start.6 = (f32[3,8,4096]{2,1,0:T(8,128)S(1)}, f32[3,8,4096]{2,1,0:T(8,128)}, u32[]{:S(2)}) copy-start(f32[3,8,4096]{2,1,0:T(8,128)} %get-tuple-element.21) | copy-start | bytes 1179652
  87.5 6.1 %collective-permute-start.6 = (f32[304,128]{1,0:T(8,128)S(1)}, f32[304,128]{1,0:T(8,128)S(1)}, u32[]{:S(2)}, u32[]{:S(2)}) collective-permute-start(f32[304,128]{1,0:T(8,128)S(1)} %slice_select_fusion.2), channel_id=1, source_target_pairs={{0,8},{8,0},{16,24},{24,16},{1,9},{9,1},{17,25},{25,17},{2,10},{10... | collective-permute-start | bytes 466952 | tf_op jit(solution)/shard_map/filter_grad_sum/ppermute | solution.py:251
  87.7 37.1 %copy-start.3 = (f32[3,16,4096]{2,1,0:T(8,128)S(1)}, f32[3,16,4096]{2,1,0:T(8,128)}, u32[]{:S(2)}) copy-start(f32[3,16,4096]{2,1,0:T(8,128)} %get-tuple-element.20) | copy-start | bytes 2359300
  93.7 4.5 %collective-permute-start.7 = (f32[152,128]{1,0:T(8,128)S(1)}, f32[152,128]{1,0:T(8,128)S(1)}, u32[]{:S(2)}, u32[]{:S(2)}) collective-permute-start(f32[152,128]{1,0:T(8,128)S(1)} %slice_select_fusion.3), channel_id=1, source_target_pairs={{0,16},{8,24},{16,0},{24,8},{1,17},{9,25},{17,1},{25,9},{2,18},{10... | collective-permute-start | bytes 233480 | tf_op jit(solution)/shard_map/filter_grad_sum/ppermute | solution.py:251
  98.2 4.1 %collective-permute-start.8 = (f32[76,128]{1,0:T(8,128)S(1)}, f32[76,128]{1,0:T(8,128)S(1)}, u32[]{:S(2)}, u32[]{:S(2)}) collective-permute-start(f32[76,128]{1,0:T(8,128)S(1)} %slice_select_fusion.4), channel_id=1, source_target_pairs={{0,2},{1,3},{2,0},{3,1},{4,6},{5,7},{6,4},{7,5},{8,10},{9,11},{10,... | collective-permute-start | bytes 116744 | tf_op jit(solution)/shard_map/filter_grad_sum/ppermute | solution.py:251
  102.3 4.7 %collective-permute-start.9 = (f32[38,128]{1,0:T(8,128)S(1)}, f32[38,128]{1,0:T(8,128)S(1)}, u32[]{:S(2)}, u32[]{:S(2)}) collective-permute-start(f32[38,128]{1,0:T(8,128)S(1)} %slice_select_fusion.5), channel_id=1, source_target_pairs={{0,4},{1,5},{2,6},{3,7},{4,0},{5,1},{6,2},{7,3},{8,12},{9,13},{10,... | collective-permute-start | bytes 58376 | tf_op jit(solution)/shard_map/filter_grad_sum/ppermute | solution.py:251
  107.0 4.7 %collective-permute-start.10 = (f32[38,128]{1,0:T(8,128)S(1)}, f32[38,128]{1,0:T(8,128)S(1)}, u32[]{:S(2)}, u32[]{:S(2)}) collective-permute-start(f32[38,128]{1,0:T(8,128)S(1)} %select_add_fusion.3), channel_id=1, source_target_pairs={{0,4},{1,5},{2,6},{3,7},{4,0},{5,1},{6,2},{7,3},{8,12},{9,13},{10,... | collective-permute-start | bytes 58376 | tf_op jit(solution)/shard_map/filter_grad_sum/ppermute | solution.py:251
  111.8 4.1 %collective-permute-start.11 = (f32[76,128]{1,0:T(8,128)S(1)}, f32[76,128]{1,0:T(8,128)S(1)}, u32[]{:S(2)}, u32[]{:S(2)}) collective-permute-start(f32[76,128]{1,0:T(8,128)S(1)} %maximum_select_fusion.4), channel_id=1, source_target_pairs={{0,2},{1,3},{2,0},{3,1},{4,6},{5,7},{6,4},{7,5},{8,10},{9,11},{10,... | collective-permute-start | bytes 116744 | tf_op jit(solution)/shard_map/filter_grad_sum/ppermute | solution.py:251
  113.5 11.3 %collective-permute-start.4 = (f32[3,8,4096]{2,1,0:T(8,128)S(1)}, f32[3,8,4096]{2,1,0:T(8,128)S(1)}, u32[]{:S(2)}, u32[]{:S(2)}) collective-permute-start(f32[3,8,4096]{2,1,0:T(8,128)S(1)} %copy-done.6), channel_id=1, source_target_pairs={{8,0},{16,8},{24,16},{9,1},{17,9},{25,17},{10,2},{18,10},{26,18},{... | collective-permute-start | bytes 1179656 | tf_op jit(solution)/shard_map/ppermute | solution.py:20
  115.9 4.5 %collective-permute-start.12 = (f32[152,128]{1,0:T(8,128)S(1)}, f32[152,128]{1,0:T(8,128)S(1)}, u32[]{:S(2)}, u32[]{:S(2)}) collective-permute-start(f32[152,128]{1,0:T(8,128)S(1)} %maximum_select_fusion.3), channel_id=1, source_target_pairs={{0,16},{8,24},{16,0},{24,8},{1,17},{9,25},{17,1},{25,9},{2,18},{10... | collective-permute-start | bytes 233480 | tf_op jit(solution)/shard_map/filter_grad_sum/ppermute | solution.py:251
  120.4 6.1 %collective-permute-start.13 = (f32[304,128]{1,0:T(8,128)S(1)}, f32[304,128]{1,0:T(8,128)S(1)}, u32[]{:S(2)}, u32[]{:S(2)}) collective-permute-start(f32[304,128]{1,0:T(8,128)S(1)} %maximum_select_fusion.2), channel_id=1, source_target_pairs={{0,8},{8,0},{16,24},{24,16},{1,9},{9,1},{17,25},{25,17},{2,10},{10... | collective-permute-start | bytes 466952 | tf_op jit(solution)/shard_map/filter_grad_sum/ppermute | solution.py:251
  126.5 1.7 %collective-permute-start.14 = (f32[608,128]{1,0:T(8,128)S(1)}, f32[608,128]{1,0:T(8,128)S(1)}, u32[]{:S(2)}, u32[]{:S(2)}) collective-permute-start(f32[608,128]{1,0:T(8,128)S(1)} %maximum_select_fusion.1), channel_id=1, source_target_pairs={{0,1},{1,0},{2,3},{3,2},{4,5},{5,4},{6,7},{7,6},{8,9},{9,8},{10,11... | collective-permute-start | bytes 933896 | tf_op jit(solution)/shard_map/filter_grad_sum/ppermute | solution.py:251

commit v8 on v7

--- a/solution.py
+++ b/solution.py
@@ -27,8 +27,8 @@
     return lax.broadcasted_iota(jnp.int32, (8, lanes), 0)
 
 
-def feature_stream(pad_ref, taps_ref, s, out_ref):
-    rows = out_ref.shape[1]
+def feature_stream(pad_ref, taps_ref, s, out_ref, tiles=None):
+    rows = out_ref.shape[1] if tiles is None else 8 * tiles
     count = taps_ref.shape[1]
     for c0 in range(0, out_ref.shape[2], CHUNK):
         cols = slice(c0, c0 + CHUNK)
@@ -52,16 +52,8 @@
         pad_ref[s, RIM + lo : RIM + lo + BR, :] = x_ref[lo : lo + BR, :].astype(F32)
 
 
-def block_feature(pad_ref, taps_ref, s, lo):
-    count = taps_ref.shape[1]
-    total = taps_ref[s, 0:1, :] * pad_ref[s, RIM + lo : RIM + lo + BR, :]
-    for lag in range(1, count):
-        total = total + taps_ref[s, lag : lag + 1, :] * pad_ref[s, RIM + lo - lag : RIM + lo - lag + BR, :]
-    return total
-
-
 def states_kernel(
-    q_ref, k_ref, v_ref, c_ref, rim_ref, taps_ref, a_ref, f_ref, b_ref, pad_ref, p_ref, z_ref, feat_ref
+    q_ref, k_ref, v_ref, c_ref, rim_ref, taps_ref, a_ref, f_ref, b_ref, feat_ref, pad_ref, p_ref, z_ref
 ):
     rows = q_ref.shape[0]
     for s in range(3):
@@ -92,7 +84,7 @@
 
 
 def main_kernel(
-    q_ref, k_ref, v_ref, c_ref, rim_ref, taps_ref, a_ref, r_ref, skip_ref, s_ref, g_ref,
+    q_ref, k_ref, v_ref, c_ref, rim_ref, taps_ref, a_ref, r_ref, skip_ref, s_ref, g_ref, bare_ref,
     mixed_ref, gq_ref, gk_ref, gv_ref, tail_ref, head_ref, grads_ref,
     pad_ref, p_ref, z_ref, y_ref, u_ref, adj_ref, feat_ref,
 ):
@@ -106,7 +98,9 @@
     for lo in range(0, rows, BR):
         fill_rows((q_ref, k_ref, v_ref), pad_ref, lo)
     for s in range(3):
-        feature_stream(pad_ref, taps_ref, s, feat_ref)
+        for lo in range(0, rows, BR):
+            feat_ref[s, lo : lo + BR, :] = bare_ref[s, lo : lo + BR, :]
+        feature_stream(pad_ref, taps_ref, s, feat_ref, tiles=1)
     for lo in range(0, rows, BR):
         fq = feat_ref[0, lo : lo + BR, :]
         fk = feat_ref[1, lo : lo + BR, :]
@@ -202,23 +196,22 @@
         states_kernel,
         grid=(width // lanes,),
         in_specs=[tile(x.shape, lanes) for x in ins],
-        out_specs=[tile((poles, width), lanes), tile((poles, width), lanes)],
-        out_shape=[jax.ShapeDtypeStruct((poles, width), F32)] * 2,
+        out_specs=[tile((poles, width), lanes), tile((poles, width), lanes), tile((3, rows, width), lanes)],
+        out_shape=[jax.ShapeDtypeStruct((poles, width), F32)] * 2 + [jax.ShapeDtypeStruct((3, rows, width), F32)],
         scratch_shapes=[
             pltpu.VMEM((3, rows + RIM, lanes), F32),
             pltpu.VMEM((rows, lanes), F32),
             pltpu.VMEM((rows, lanes), F32),
-            pltpu.VMEM((3, rows, lanes), F32),
         ],
     )(*ins)
 
 
-def run_main(q, k, v, c, rim, taps, a, r, skip, s_in, g_in):
+def run_main(q, k, v, c, rim, taps, a, r, skip, s_in, g_in, bare):
     rows, width = q.shape
     poles = a.shape[0]
     count = taps.shape[1]
     lanes = min(LANES, width)
-    ins = (q, k, v, c, rim, taps, a, r, skip, s_in, g_in)
+    ins = (q, k, v, c, rim, taps, a, r, skip, s_in, g_in, bare)
     out_shapes = [
         jax.ShapeDtypeStruct((rows, width), jnp.bfloat16),
         jax.ShapeDtypeStruct((rows, width), jnp.bfloat16),
@@ -350,7 +343,7 @@
     lead = jnp.stack([q[rows - RIM :], k[rows - RIM :], v[rows - RIM :]], 0)
     rim = passed_along(lead, "seq", 1)
     a = jnp.exp(-decay)
-    f_bare, b_bare = run_states(q, k, v, c, jnp.zeros_like(lead), taps, a)
+    f_bare, b_bare, bare_feats = run_states(q, k, v, c, jnp.zeros_like(lead), taps, a)
     with jax.named_scope("rim_share_of_states"):
         first = jnp.stack([q[:RIM], k[:RIM], v[:RIM]], 0).astype(F32)
 
@@ -370,7 +363,7 @@
     with jax.named_scope("modal_state_scan"):
         s_in, g_in = scan_states(f_local, b_local, decay, rows, "seq")
     mixed, gq, gk, gv, tails, heads, grads = run_main(
-        q, k, v, c, rim, taps, a, residue, skip.reshape(1, width), s_in, g_in
+        q, k, v, c, rim, taps, a, residue, skip.reshape(1, width), s_in, g_in, bare_feats
     )
     after = passed_along(heads, "seq", -1)
     ext = jnp.concatenate(

time: 131 us -> 130 us (level)
  starting transfers between devices: 23.6 us -> 29.6 us
  waiting for transfers between devices: 40.8 us -> 35.6 us
  Pallas kernels: 52.2 us -> 47.5 us
  local copies, waits for them, and re-layouts: 6.55 us -> 8.39 us
    ppermute x11, starting transfers between devices: 15.5 us -> 21.5 us  [exchange(): return lax.ppermute(x, axis, [(i, i ^ size) for i in range(count)])]
    pallas_call x1, Pallas kernels: 38.5 us -> 34.4 us  [run_main(): pl.pallas_call(main_kernel, grid=(width // lanes,), in_specs=[tile(x.shap...]
    ppermute x11, waiting for transfers between devices: 29.8 us -> 26.8 us  [exchange(): return lax.ppermute(x, axis, [(i, i ^ size) for i in range(count)])]
    slice x1, local copies, waits for them, and re-layouts: 0.27 us -> 2.49 us  [head_feats(): taps[:, lag, None, :] * padded[:, RIM - lag:2 * RIM - lag]]
    ppermute x1, waiting for transfers between devices: 9.01 us -> 6.8 us  [scan_four(): across = lax.ppermute(sent, axis, [(1, 3), (2, 0)])]
  transfers between devices with their start and end apart: 15 -> 15, of which waited for: 13 -> 13; matrix products, arithmetic and copies ran while one was open for 3% -> 5% of each run, Pallas kernels for 10% -> 10%
where the time goes in v8:
time: 130 us; the launch traced here: 129 us
  Pallas kernels  47.5 us (37%)
  waiting for transfers between devices  35.6 us (27%)
  starting transfers between devices  29.6 us (23%)
  local copies, waits for them, and re-layouts  8.39 us (6%)
  other arithmetic  7.29 us (6%)
    pallas_call x1, Pallas kernels, run_main(): pl.pallas_call(main_kernel, grid=(width // lanes,), in_specs=[tile(x.shap...  34.4 us
    ppermute x11, waiting for transfers between devices, exchange(): return lax.ppermute(x, axis, [(i, i ^ size) for i in range(count)])  26.8 us
    ppermute x11, starting transfers between devices, exchange(): return lax.ppermute(x, axis, [(i, i ^ size) for i in range(count)])  21.5 us
    pallas_call x1, Pallas kernels, run_states(): pl.pallas_call(states_kernel, grid=(width // lanes,), in_specs=[tile(x.sh...  13.1 us
    ppermute x1, waiting for transfers between devices, scan_four(): across = lax.ppermute(sent, axis, [(1, 3), (2, 0)])  6.8 us
    ppermute x2, starting transfers between devices, passed_along(): return lax.ppermute(x, axis, pairs)  6.16 us
  transfers between devices with their start and end apart: 15, of which 13 were waited for; matrix products, arithmetic and copies ran while one was open for 5% of the time, Pallas kernels for 10%

profile of v8, /device:TPU:0, one launch (start us, length us, event | category | flops | bytes accessed | tf_op | source)
XLA Modules:
  0.0 129.3 jit_solution(12118649373852037667)
XLA Ops:
  2.5 4.9 %collective-permute-start = (bf16[3,8,4096]{2,1,0:T(8,128)(2,1)S(1)}, bf16[3,8,4096]{2,1,0:T(8,128)(2,1)S(1)}, u32[]{:S(2)}, u32[]{:S(2)}) collective-permute-start(bf16[3,8,4096]{2,1,0:T(8,128)(2,1)S(1)} %pad_maximum_fusion.1), channel_id=1, source_target_pairs={{0,8},{8,16},{16,24},{1,9},{9,17},{17,25},{2,10},{10,18},{18,26},{... | collective-permute-start | bytes 589832 | tf_op jit(solution)/shard_map/ppermute | solution.py:20
  7.4 2.5 %fusion.50 = (f32[3,1,4096]{2,1,0:T(1,128)S(1)}, f32[3,1,4096]{2,1,0:T(1,128)S(1)}, f32[3,1,4096]{2,1,0:T(1,128)S(1)}, f32[3,1,4096]{2,1,0:T(1,128)S(1)}, f32[3,...) fusion(f32[3,7,4096]{2,1,0:T(8,128)} %taps_ref.3), kind=kLoop, calls=%fused_computation.115 | loop fusion | bytes 688128 | tf_op jit(solution)/shard_map/rim_share_of_states/slice | solution.py:352
  9.9 1.7 %fusion.51 = (f32[16,4096]{1,0:T(8,128)S(1)}, f32[16,4096]{1,0:T(8,128)}) fusion(f32[16,4096]{1,0:T(8,128)} %param.15), kind=kLoop, calls=%fused_computation.116 | loop fusion | flops 65536 | bytes 786432 | tf_op jit(solution)/shard_map/neg | solution.py:345
  12.6 13.1 %shard_map.135 = (f32[16,4096]{1,0:T(8,128)}, f32[16,4096]{1,0:T(8,128)}, f32[3,128,4096]{2,1,0:T(8,128)}) custom-call(bf16[128,4096]{1,0:T(8,128)(2,1)} %bitcast.33, bf16[128,4096]{1,0:T(8,128)(2,1)} %bitcast.35, bf16[128,4096]{1,0:T(8,128)(2,1)} %bitcast.37, bf16[128,4096]{1,0:T(8,128)(2,1)} %bitcast.39, bf16[3,8,4096]{2,1,0:T(8,128)(2,1)} %broadcast_in_dim.14.rim_ref, ...), custom_call_target="tpu_custom_call" | custom-call | tf_op jit(solution)/shard_map/pallas_call | solution.py:195
  28.4 1.5 %collective-permute-start.1 = (f32[16,4096]{1,0:T(8,128)S(1)}, f32[16,4096]{1,0:T(8,128)S(1)}, u32[]{:S(2)}, u32[]{:S(2)}) collective-permute-start(f32[16,4096]{1,0:T(8,128)S(1)} %get-tuple-element.29), channel_id=1, source_target_pairs={{0,8},{8,0},{16,24},{24,16},{1,9},{9,1},{17,25},{25,17},{2,10},{10... | collective-permute-start | bytes 786440 | tf_op jit(solution)/shard_map/modal_state_scan/ppermute | solution.py:244
  29.9 6.3 %collective-permute-done.1 = f32[16,4096]{1,0:T(8,128)S(1)} collective-permute-done((f32[16,4096]{1,0:T(8,128)S(1)}, f32[16,4096]{1,0:T(8,128)S(1)}, u32[]{:S(2)}, u32[]{:S(2)}) %collective-permute-start.1) | collective-permute-done | bytes 262176 | tf_op jit(solution)/shard_map/modal_state_scan/ppermute | solution.py:244
  38.3 6.8 %collective-permute-done.2 = f32[16,4096]{1,0:T(8,128)S(1)} collective-permute-done((f32[16,4096]{1,0:T(8,128)S(1)}, f32[16,4096]{1,0:T(8,128)S(1)}, u32[]{:S(2)}, u32[]{:S(2)}) %collective-permute-start.2) | collective-permute-done | bytes 262176 | tf_op jit(solution)/shard_map/modal_state_scan/ppermute | solution.py:257
  46.0 34.4 %shard_map.136 = (bf16[128,4096]{1,0:T(8,128)(2,1)}, bf16[128,4096]{1,0:T(8,128)(2,1)}, bf16[128,4096]{1,0:T(8,128)(2,1)}, bf16[128,4096]{1,0:T(8,128)(2,1)}, f3...) custom-call(bf16[128,4096]{1,0:T(8,128)(2,1)} %bitcast.34, bf16[128,4096]{1,0:T(8,128)(2,1)} %bitcast.36, ...), custom_call_target="tpu_custom_call" | custom-call | tf_op jit(solution)/shard_map/pallas_call | solution.py:224
  81.8 1.5 %collective-permute-done.5 = f32[608,128]{1,0:T(8,128)S(1)} collective-permute-done((f32[608,128]{1,0:T(8,128)S(1)}, f32[608,128]{1,0:T(8,128)S(1)}, u32[]{:S(2)}, u32[]{:S(2)}) %collective-permute-start.5) | collective-permute-done | bytes 311328 | tf_op jit(solution)/shard_map/filter_grad_sum/ppermute | solution.py:244
  83.4 4.7 %collective-permute-start.6 = (f32[304,128]{1,0:T(8,128)S(1)}, f32[304,128]{1,0:T(8,128)S(1)}, u32[]{:S(2)}, u32[]{:S(2)}) collective-permute-start(f32[304,128]{1,0:T(8,128)S(1)} %slice_select_fusion.2), channel_id=1, source_target_pairs={{0,8},{8,0},{16,24},{24,16},{1,9},{9,1},{17,25},{25,17},{2,10},{10... | collective-permute-start | bytes 466952 | tf_op jit(solution)/shard_map/filter_grad_sum/ppermute | solution.py:244
  88.1 4.3 %collective-permute-done.6 = f32[304,128]{1,0:T(8,128)S(1)} collective-permute-done((f32[304,128]{1,0:T(8,128)S(1)}, f32[304,128]{1,0:T(8,128)S(1)}, u32[]{:S(2)}, u32[]{:S(2)}) %collective-permute-start.6) | collective-permute-done | bytes 155680 | tf_op jit(solution)/shard_map/filter_grad_sum/ppermute | solution.py:244
  92.5 1.8 %collective-permute-start.7 = (f32[152,128]{1,0:T(8,128)S(1)}, f32[152,128]{1,0:T(8,128)S(1)}, u32[]{:S(2)}, u32[]{:S(2)}) collective-permute-start(f32[152,128]{1,0:T(8,128)S(1)} %slice_select_fusion.3), channel_id=1, source_target_pairs={{0,16},{8,24},{16,0},{24,8},{1,17},{9,25},{17,1},{25,9},{2,18},{10... | collective-permute-start | bytes 233480 | tf_op jit(solution)/shard_map/filter_grad_sum/ppermute | solution.py:244
  94.2 2.7 %collective-permute-done.7 = f32[152,128]{1,0:T(8,128)S(1)} collective-permute-done((f32[152,128]{1,0:T(8,128)S(1)}, f32[152,128]{1,0:T(8,128)S(1)}, u32[]{:S(2)}, u32[]{:S(2)}) %collective-permute-start.7) | collective-permute-done | bytes 77856 | tf_op jit(solution)/shard_map/filter_grad_sum/ppermute | solution.py:244
  97.0 1.6 %collective-permute-start.8 = (f32[76,128]{1,0:T(8,128)S(1)}, f32[76,128]{1,0:T(8,128)S(1)}, u32[]{:S(2)}, u32[]{:S(2)}) collective-permute-start(f32[76,128]{1,0:T(8,128)S(1)} %slice_select_fusion.4), channel_id=1, source_target_pairs={{0,2},{1,3},{2,0},{3,1},{4,6},{5,7},{6,4},{7,5},{8,10},{9,11},{10,... | collective-permute-start | bytes 116744 | tf_op jit(solution)/shard_map/filter_grad_sum/ppermute | solution.py:244
  98.6 2.4 %collective-permute-done.8 = f32[76,128]{1,0:T(8,128)S(1)} collective-permute-done((f32[76,128]{1,0:T(8,128)S(1)}, f32[76,128]{1,0:T(8,128)S(1)}, u32[]{:S(2)}, u32[]{:S(2)}) %collective-permute-start.8) | collective-permute-done | bytes 38944 | tf_op jit(solution)/shard_map/filter_grad_sum/ppermute | solution.py:244
  101.1 2.8 %collective-permute-start.9 = (f32[38,128]{1,0:T(8,128)S(1)}, f32[38,128]{1,0:T(8,128)S(1)}, u32[]{:S(2)}, u32[]{:S(2)}) collective-permute-start(f32[38,128]{1,0:T(8,128)S(1)} %slice_select_fusion.5), channel_id=1, source_target_pairs={{0,4},{1,5},{2,6},{3,7},{4,0},{5,1},{6,2},{7,3},{8,12},{9,13},{10,... | collective-permute-start | bytes 58376 | tf_op jit(solution)/shard_map/filter_grad_sum/ppermute | solution.py:244
  103.9 2.1 %collective-permute-done.9 = f32[38,128]{1,0:T(8,128)S(1)} collective-permute-done((f32[38,128]{1,0:T(8,128)S(1)}, f32[38,128]{1,0:T(8,128)S(1)}, u32[]{:S(2)}, u32[]{:S(2)}) %collective-permute-start.9) | collective-permute-done | bytes 19488 | tf_op jit(solution)/shard_map/filter_grad_sum/ppermute | solution.py:244
  105.9 2.7 %collective-permute-start.10 = (f32[38,128]{1,0:T(8,128)S(1)}, f32[38,128]{1,0:T(8,128)S(1)}, u32[]{:S(2)}, u32[]{:S(2)}) collective-permute-start(f32[38,128]{1,0:T(8,128)S(1)} %select_add_fusion.3), channel_id=1, source_target_pairs={{0,4},{1,5},{2,6},{3,7},{4,0},{5,1},{6,2},{7,3},{8,12},{9,13},{10,... | collective-permute-start | bytes 58376 | tf_op jit(solution)/shard_map/filter_grad_sum/ppermute | solution.py:244
  108.7 2.0 %collective-permute-done.10 = f32[38,128]{1,0:T(8,128)S(1)} collective-permute-done((f32[38,128]{1,0:T(8,128)S(1)}, f32[38,128]{1,0:T(8,128)S(1)}, u32[]{:S(2)}, u32[]{:S(2)}) %collective-permute-start.10) | collective-permute-done | bytes 19488 | tf_op jit(solution)/shard_map/filter_grad_sum/ppermute | solution.py:244
  110.7 1.7 %collective-permute-start.11 = (f32[76,128]{1,0:T(8,128)S(1)}, f32[76,128]{1,0:T(8,128)S(1)}, u32[]{:S(2)}, u32[]{:S(2)}) collective-permute-start(f32[76,128]{1,0:T(8,128)S(1)} %maximum_select_fusion.4), channel_id=1, source_target_pairs={{0,2},{1,3},{2,0},{3,1},{4,6},{5,7},{6,4},{7,5},{8,10},{9,11},{10,... | collective-permute-start | bytes 116744 | tf_op jit(solution)/shard_map/filter_grad_sum/ppermute | solution.py:244
  114.8 2.7 %collective-permute-start.12 = (f32[152,128]{1,0:T(8,128)S(1)}, f32[152,128]{1,0:T(8,128)S(1)}, u32[]{:S(2)}, u32[]{:S(2)}) collective-permute-start(f32[152,128]{1,0:T(8,128)S(1)} %maximum_select_fusion.3), channel_id=1, source_target_pairs={{0,16},{8,24},{16,0},{24,8},{1,17},{9,25},{17,1},{25,9},{2,18},{10... | collective-permute-start | bytes 233480 | tf_op jit(solution)/shard_map/filter_grad_sum/ppermute | solution.py:244
  117.5 2.3 %collective-permute-done.12 = f32[152,128]{1,0:T(8,128)S(1)} collective-permute-done((f32[152,128]{1,0:T(8,128)S(1)}, f32[152,128]{1,0:T(8,128)S(1)}, u32[]{:S(2)}, u32[]{:S(2)}) %collective-permute-start.12) | collective-permute-done | bytes 77856 | tf_op jit(solution)/shard_map/filter_grad_sum/ppermute | solution.py:244
  119.9 1.8 %collective-permute-start.13 = (f32[304,128]{1,0:T(8,128)S(1)}, f32[304,128]{1,0:T(8,128)S(1)}, u32[]{:S(2)}, u32[]{:S(2)}) collective-permute-start(f32[304,128]{1,0:T(8,128)S(1)} %maximum_select_fusion.2), channel_id=1, source_target_pairs={{0,8},{8,0},{16,24},{24,16},{1,9},{9,1},{17,25},{25,17},{2,10},{10... | collective-permute-start | bytes 466952 | tf_op jit(solution)/shard_map/filter_grad_sum/ppermute | solution.py:244
  121.7 2.0 %collective-permute-done.4 = f32[3,8,4096]{2,1,0:T(8,128)S(1)} collective-permute-done((f32[3,8,4096]{2,1,0:T(8,128)S(1)}, f32[3,8,4096]{2,1,0:T(8,128)S(1)}, u32[]{:S(2)}, u32[]{:S(2)}) %collective-permute-start.4) | collective-permute-done | bytes 393248 | tf_op jit(solution)/shard_map/ppermute | solution.py:20
  (64 shorter events, 18.0 us)
Async XLA Ops:
  2.5 23.2 %collective-permute-start = (bf16[3,8,4096]{2,1,0:T(8,128)(2,1)S(1)}, bf16[3,8,4096]{2,1,0:T(8,128)(2,1)S(1)}, u32[]{:S(2)}, u32[]{:S(2)}) collective-permute-start(bf16[3,8,4096]{2,1,0:T(8,128)(2,1)S(1)} %pad_maximum_fusion.1), channel_id=1, source_target_pairs={{0,8},{8,16},{16,24},{1,9},{9,17},{17,25},{2,10},{10,18},{18,26},{... | collective-permute-start | bytes 589832 | tf_op jit(solution)/shard_map/ppermute | solution.py:20
  25.7 2.5 %copy-start.2 = (bf16[3,8,4096]{2,1,0:T(8,128)(2,1)}, bf16[3,8,4096]{2,1,0:T(8,128)(2,1)S(1)}, u32[]{:S(2)}) copy-start(bf16[3,8,4096]{2,1,0:T(8,128)(2,1)S(1)} %collective-permute-done.rim_ref) | copy-start | bytes 589828
  25.8 2.5 %copy-start.3 = (f32[16,4096]{1,0:T(8,128)S(1)}, f32[16,4096]{1,0:T(8,128)}, u32[]{:S(2)}) copy-start(f32[16,4096]{1,0:T(8,128)} %get-tuple-element.18) | copy-start | bytes 786436
  25.8 2.5 %copy-start.4 = (f32[16,4096]{1,0:T(8,128)S(1)}, f32[16,4096]{1,0:T(8,128)}, u32[]{:S(2)}) copy-start(f32[16,4096]{1,0:T(8,128)} %get-tuple-element.17) | copy-start | bytes 786436
  27.6 8.6 %copy-start = (f32[16,4096]{1,0:T(8,128)S(1)}, f32[16,4096]{1,0:T(8,128)}, u32[]{:S(2)}) copy-start(f32[16,4096]{1,0:T(8,128)} %param.15) | copy-start | bytes 786436
  28.4 7.8 %collective-permute-start.1 = (f32[16,4096]{1,0:T(8,128)S(1)}, f32[16,4096]{1,0:T(8,128)S(1)}, u32[]{:S(2)}, u32[]{:S(2)}) collective-permute-start(f32[16,4096]{1,0:T(8,128)S(1)} %get-tuple-element.29), channel_id=1, source_target_pairs={{0,8},{8,0},{16,24},{24,16},{1,9},{9,1},{17,25},{25,17},{2,10},{10... | collective-permute-start | bytes 786440 | tf_op jit(solution)/shard_map/modal_state_scan/ppermute | solution.py:244
  36.3 8.8 %collective-permute-start.2 = (f32[16,4096]{1,0:T(8,128)S(1)}, f32[16,4096]{1,0:T(8,128)S(1)}, u32[]{:S(2)}, u32[]{:S(2)}) collective-permute-start(f32[16,4096]{1,0:T(8,128)S(1)} %add_select_fusion), channel_id=1, source_target_pairs={{8,24},{16,0},{9,25},{17,1},{10,26},{18,2},{11,27},{19,3},{12,28},... | collective-permute-start | bytes 786440 | tf_op jit(solution)/shard_map/modal_state_scan/ppermute | solution.py:257
  37.6 7.5 %collective-permute-start.3 = (f32[16,4096]{1,0:T(8,128)S(1)}, f32[16,4096]{1,0:T(8,128)S(1)}, u32[]{:S(2)}, u32[]{:S(2)}) collective-permute-start(f32[16,4096]{1,0:T(8,128)S(1)} %add_select_fusion), channel_id=1, source_target_pairs={{8,16},{16,8},{9,17},{17,9},{10,18},{18,10},{11,19},{19,11},{12,20... | collective-permute-start | bytes 786440 | tf_op jit(solution)/shard_map/modal_state_scan/ppermute | solution.py:258
  81.7 30.7 %copy-start.5 = (f32[3,8,4096]{2,1,0:T(8,128)S(1)}, f32[3,8,4096]{2,1,0:T(8,128)}, u32[]{:S(2)}) copy-start(f32[3,8,4096]{2,1,0:T(8,128)} %get-tuple-element.23) | copy-start | bytes 1179652
  81.7 1.7 %collective-permute-start.5 = (f32[608,128]{1,0:T(8,128)S(1)}, f32[608,128]{1,0:T(8,128)S(1)}, u32[]{:S(2)}, u32[]{:S(2)}) collective-permute-start(f32[608,128]{1,0:T(8,128)S(1)} %select_n.213), channel_id=1, source_target_pairs={{0,1},{1,0},{2,3},{3,2},{4,5},{5,4},{6,7},{7,6},{8,9},{9,8},{10,11... | collective-permute-start | bytes 933896 | tf_op jit(solution)/shard_map/filter_grad_sum/ppermute | solution.py:244
  81.8 42.0 %copy-start.1 = (f32[3,16,4096]{2,1,0:T(8,128)S(1)}, f32[3,16,4096]{2,1,0:T(8,128)}, u32[]{:S(2)}) copy-start(f32[3,16,4096]{2,1,0:T(8,128)} %get-tuple-element.22) | copy-start | bytes 2359300
  83.4 9.0 %collective-permute-start.6 = (f32[304,128]{1,0:T(8,128)S(1)}, f32[304,128]{1,0:T(8,128)S(1)}, u32[]{:S(2)}, u32[]{:S(2)}) collective-permute-start(f32[304,128]{1,0:T(8,128)S(1)} %slice_select_fusion.2), channel_id=1, source_target_pairs={{0,8},{8,0},{16,24},{24,16},{1,9},{9,1},{17,25},{25,17},{2,10},{10... | collective-permute-start | bytes 466952 | tf_op jit(solution)/shard_map/filter_grad_sum/ppermute | solution.py:244
  92.5 4.5 %collective-permute-start.7 = (f32[152,128]{1,0:T(8,128)S(1)}, f32[152,128]{1,0:T(8,128)S(1)}, u32[]{:S(2)}, u32[]{:S(2)}) collective-permute-start(f32[152,128]{1,0:T(8,128)S(1)} %slice_select_fusion.3), channel_id=1, source_target_pairs={{0,16},{8,24},{16,0},{24,8},{1,17},{9,25},{17,1},{25,9},{2,18},{10... | collective-permute-start | bytes 233480 | tf_op jit(solution)/shard_map/filter_grad_sum/ppermute | solution.py:244
  97.0 4.1 %collective-permute-start.8 = (f32[76,128]{1,0:T(8,128)S(1)}, f32[76,128]{1,0:T(8,128)S(1)}, u32[]{:S(2)}, u32[]{:S(2)}) collective-permute-start(f32[76,128]{1,0:T(8,128)S(1)} %slice_select_fusion.4), channel_id=1, source_target_pairs={{0,2},{1,3},{2,0},{3,1},{4,6},{5,7},{6,4},{7,5},{8,10},{9,11},{10,... | collective-permute-start | bytes 116744 | tf_op jit(solution)/shard_map/filter_grad_sum/ppermute | solution.py:244
  101.1 4.9 %collective-permute-start.9 = (f32[38,128]{1,0:T(8,128)S(1)}, f32[38,128]{1,0:T(8,128)S(1)}, u32[]{:S(2)}, u32[]{:S(2)}) collective-permute-start(f32[38,128]{1,0:T(8,128)S(1)} %slice_select_fusion.5), channel_id=1, source_target_pairs={{0,4},{1,5},{2,6},{3,7},{4,0},{5,1},{6,2},{7,3},{8,12},{9,13},{10,... | collective-permute-start | bytes 58376 | tf_op jit(solution)/shard_map/filter_grad_sum/ppermute | solution.py:244
  105.9 4.7 %collective-permute-start.10 = (f32[38,128]{1,0:T(8,128)S(1)}, f32[38,128]{1,0:T(8,128)S(1)}, u32[]{:S(2)}, u32[]{:S(2)}) collective-permute-start(f32[38,128]{1,0:T(8,128)S(1)} %select_add_fusion.3), channel_id=1, source_target_pairs={{0,4},{1,5},{2,6},{3,7},{4,0},{5,1},{6,2},{7,3},{8,12},{9,13},{10,... | collective-permute-start | bytes 58376 | tf_op jit(solution)/shard_map/filter_grad_sum/ppermute | solution.py:244
  110.7 4.1 %collective-permute-start.11 = (f32[76,128]{1,0:T(8,128)S(1)}, f32[76,128]{1,0:T(8,128)S(1)}, u32[]{:S(2)}, u32[]{:S(2)}) collective-permute-start(f32[76,128]{1,0:T(8,128)S(1)} %maximum_select_fusion.4), channel_id=1, source_target_pairs={{0,2},{1,3},{2,0},{3,1},{4,6},{5,7},{6,4},{7,5},{8,10},{9,11},{10,... | collective-permute-start | bytes 116744 | tf_op jit(solution)/shard_map/filter_grad_sum/ppermute | solution.py:244
  112.4 11.3 %collective-permute-start.4 = (f32[3,8,4096]{2,1,0:T(8,128)S(1)}, f32[3,8,4096]{2,1,0:T(8,128)S(1)}, u32[]{:S(2)}, u32[]{:S(2)}) collective-permute-start(f32[3,8,4096]{2,1,0:T(8,128)S(1)} %copy-done.5), channel_id=1, source_target_pairs={{8,0},{16,8},{24,16},{9,1},{17,9},{25,17},{10,2},{18,10},{26,18},{... | collective-permute-start | bytes 1179656 | tf_op jit(solution)/shard_map/ppermute | solution.py:20
  114.8 5.1 %collective-permute-start.12 = (f32[152,128]{1,0:T(8,128)S(1)}, f32[152,128]{1,0:T(8,128)S(1)}, u32[]{:S(2)}, u32[]{:S(2)}) collective-permute-start(f32[152,128]{1,0:T(8,128)S(1)} %maximum_select_fusion.3), channel_id=1, source_target_pairs={{0,16},{8,24},{16,0},{24,8},{1,17},{9,25},{17,1},{25,9},{2,18},{10... | collective-permute-start | bytes 233480 | tf_op jit(solution)/shard_map/filter_grad_sum/ppermute | solution.py:244
  119.9 5.5 %collective-permute-start.13 = (f32[304,128]{1,0:T(8,128)S(1)}, f32[304,128]{1,0:T(8,128)S(1)}, u32[]{:S(2)}, u32[]{:S(2)}) collective-permute-start(f32[304,128]{1,0:T(8,128)S(1)} %maximum_select_fusion.2), channel_id=1, source_target_pairs={{0,8},{8,0},{16,24},{24,16},{1,9},{9,1},{17,25},{25,17},{2,10},{10... | collective-permute-start | bytes 466952 | tf_op jit(solution)/shard_map/filter_grad_sum/ppermute | solution.py:244
  125.4 1.7 %collective-permute-start.14 = (f32[608,128]{1,0:T(8,128)S(1)}, f32[608,128]{1,0:T(8,128)S(1)}, u32[]{:S(2)}, u32[]{:S(2)}) collective-permute-start(f32[608,128]{1,0:T(8,128)S(1)} %maximum_select_fusion.1), channel_id=1, source_target_pairs={{0,1},{1,0},{2,3},{3,2},{4,5},{5,4},{6,7},{7,6},{8,9},{9,8},{10,11... | collective-permute-start | bytes 933896 | tf_op jit(solution)/shard_map/filter_grad_sum/ppermute | solution.py:244

commit v9 on v8

--- a/solution.py
+++ b/solution.py
@@ -355,11 +355,12 @@
         without = head_feats(jnp.zeros_like(first))
         d_product = with_rim[1] * with_rim[2] - without[1] * without[2]
         d_adjoint = c[:RIM].astype(F32) * (with_rim[0] - without[0])
-        lags = jnp.arange(RIM, dtype=F32)
-        f_local = f_bare + jnp.sum(
-            jnp.exp(-decay[None] * (rows - 1 - lags)[:, None, None]) * d_product[:, None, :], 0
-        )
-        b_local = b_bare + jnp.sum(jnp.exp(-decay[None] * lags[:, None, None]) * d_adjoint[:, None, :], 0)
+        powers = [jnp.ones_like(a)]
+        for _ in range(RIM - 1):
+            powers.append(powers[-1] * a)
+        far = jnp.exp(-decay * float(rows - RIM))
+        f_local = f_bare + sum(far * powers[RIM - 1 - t] * d_product[t] for t in range(RIM))
+        b_local = b_bare + sum(powers[t] * d_adjoint[t] for t in range(RIM))
     with jax.named_scope("modal_state_scan"):
         s_in, g_in = scan_states(f_local, b_local, decay, rows, "seq")
     mixed, gq, gk, gv, tails, heads, grads = run_main(

time: 130 us -> 136 us (1.046)
  starting transfers between devices: 29.6 us -> 33.2 us
  other arithmetic: 7.29 us -> 9.54 us
    ppermute x11, starting transfers between devices: 21.5 us -> 25 us  [exchange(): return lax.ppermute(x, axis, [(i, i ^ size) for i in range(count)])]
    ppermute x2, waiting for transfers between devices: 2.01 us -> 0.01 us  [passed_along(): return lax.ppermute(x, axis, pairs)]
    neg x1 -> x0, other arithmetic: 1.7 us -> none  [per_device(): a = jnp.exp(-decay)]
    exp x0 -> x1, other arithmetic: none -> 1.7 us  [per_device(): a = jnp.exp(-decay)]
    ppermute x11, waiting for transfers between devices: 26.8 us -> 28.3 us  [exchange(): return lax.ppermute(x, axis, [(i, i ^ size) for i in range(count)])]
    select_n x1, other arithmetic: 0.07 us -> 1.52 us  [scan_four(): sent = jnp.where(mine == 1, pair_f, pair_b)]
    select_n x1, other arithmetic: 0.07 us -> 1.48 us  [scan_four(): got = exchange(jnp.where(mine % 2 == 1, final_b, final_f), axis, 1)]
  transfers between devices with their start and end apart: 15 -> 15, of which waited for: 13 -> 12; matrix products, arithmetic and copies ran while one was open for 5% -> 5% of each run, Pallas kernels for 10% -> 10%
where the time goes in v9:
time: 136 us; the launch traced here: 135 us
  Pallas kernels  47.5 us (35%)
  waiting for transfers between devices  35.1 us (26%)
  starting transfers between devices  33.2 us (24%)
  other arithmetic  9.54 us (7%)
  local copies, waits for them, and re-layouts  8.54 us (6%)
    pallas_call x1, Pallas kernels, run_main(): pl.pallas_call(main_kernel, grid=(width // lanes,), in_specs=[tile(x.shap...  34.4 us
    ppermute x11, waiting for transfers between devices, exchange(): return lax.ppermute(x, axis, [(i, i ^ size) for i in range(count)])  28.3 us
    ppermute x11, starting transfers between devices, exchange(): return lax.ppermute(x, axis, [(i, i ^ size) for i in range(count)])  25 us
    pallas_call x1, Pallas kernels, run_states(): pl.pallas_call(states_kernel, grid=(width // lanes,), in_specs=[tile(x.sh...  13.1 us
    ppermute x1, waiting for transfers between devices, scan_four(): across = lax.ppermute(sent, axis, [(1, 3), (2, 0)])  6.8 us
    ppermute x2, starting transfers between devices, passed_along(): return lax.ppermute(x, axis, pairs)  6.29 us
  transfers between devices with their start and end apart: 15, of which 12 were waited for; matrix products, arithmetic and copies ran while one was open for 5% of the time, Pallas kernels for 10%

profile of v9, /device:TPU:0, one launch (start us, length us, event | category | flops | bytes accessed | tf_op | source)
XLA Modules:
  0.0 134.9 jit_solution(14359362289382334525)
XLA Ops:
  2.5 5.0 %collective-permute-start = (bf16[3,8,4096]{2,1,0:T(8,128)(2,1)S(1)}, bf16[3,8,4096]{2,1,0:T(8,128)(2,1)S(1)}, u32[]{:S(2)}, u32[]{:S(2)}) collective-permute-start(bf16[3,8,4096]{2,1,0:T(8,128)(2,1)S(1)} %pad_maximum_fusion.1), channel_id=1, source_target_pairs={{0,8},{8,16},{16,24},{1,9},{9,17},{17,25},{2,10},{10,18},{18,26},{... | collective-permute-start | bytes 589832 | tf_op jit(solution)/shard_map/ppermute | solution.py:20
  7.5 2.5 %fusion.76 = (f32[3,1,4096]{2,1,0:T(1,128)S(1)}, f32[3,1,4096]{2,1,0:T(1,128)S(1)}, f32[3,1,4096]{2,1,0:T(1,128)S(1)}, f32[3,1,4096]{2,1,0:T(1,128)S(1)}, f32[3,...) fusion(f32[3,7,4096]{2,1,0:T(8,128)} %taps_ref.3), kind=kLoop, calls=%fused_computation.141 | loop fusion | bytes 688128 | tf_op jit(solution)/shard_map/rim_share_of_states/slice | solution.py:352
  10.0 1.7 %negate_exponential_fusion.a_ref = f32[16,4096]{1,0:T(8,128)} fusion(f32[16,4096]{1,0:T(8,128)} %param.15), kind=kLoop, calls=%fused_computation.106 | loop fusion | flops 65536 | bytes 524288 | tf_op jit(solution)/shard_map/exp | solution.py:345
  12.8 13.1 %shard_map.135 = (f32[16,4096]{1,0:T(8,128)}, f32[16,4096]{1,0:T(8,128)}, f32[3,128,4096]{2,1,0:T(8,128)}) custom-call(bf16[128,4096]{1,0:T(8,128)(2,1)} %bitcast.45, bf16[128,4096]{1,0:T(8,128)(2,1)} %bitcast.47, bf16[128,4096]{1,0:T(8,128)(2,1)} %bitcast.49, bf16[128,4096]{1,0:T(8,128)(2,1)} %bitcast.51, bf16[3,8,4096]{2,1,0:T(8,128)(2,1)} %broadcast_in_dim.23.rim_ref, ...), custom_call_target="tpu_custom_call" | custom-call | tf_op jit(solution)/shard_map/pallas_call | solution.py:195
  29.4 1.5 %collective-permute-start.1 = (f32[16,4096]{1,0:T(8,128)S(1)}, f32[16,4096]{1,0:T(8,128)S(1)}, u32[]{:S(2)}, u32[]{:S(2)}) collective-permute-start(f32[16,4096]{1,0:T(8,128)S(1)} %broadcast_select_fusion), channel_id=1, source_target_pairs={{0,8},{8,0},{16,24},{24,16},{1,9},{9,1},{17,25},{25,17},{2,10},{10... | collective-permute-start | bytes 786440 | tf_op jit(solution)/shard_map/modal_state_scan/ppermute | solution.py:244
  30.9 6.3 %collective-permute-done.1 = f32[16,4096]{1,0:T(8,128)S(1)} collective-permute-done((f32[16,4096]{1,0:T(8,128)S(1)}, f32[16,4096]{1,0:T(8,128)S(1)}, u32[]{:S(2)}, u32[]{:S(2)}) %collective-permute-start.1) | collective-permute-done | bytes 262176 | tf_op jit(solution)/shard_map/modal_state_scan/ppermute | solution.py:244
  40.7 6.8 %collective-permute-done.2 = f32[16,4096]{1,0:T(8,128)S(1)} collective-permute-done((f32[16,4096]{1,0:T(8,128)S(1)}, f32[16,4096]{1,0:T(8,128)S(1)}, u32[]{:S(2)}, u32[]{:S(2)}) %collective-permute-start.2) | collective-permute-done | bytes 262176 | tf_op jit(solution)/shard_map/modal_state_scan/ppermute | solution.py:257
  48.5 34.4 %shard_map.136 = (bf16[128,4096]{1,0:T(8,128)(2,1)}, bf16[128,4096]{1,0:T(8,128)(2,1)}, bf16[128,4096]{1,0:T(8,128)(2,1)}, bf16[128,4096]{1,0:T(8,128)(2,1)}, f3...) custom-call(bf16[128,4096]{1,0:T(8,128)(2,1)} %bitcast.46, bf16[128,4096]{1,0:T(8,128)(2,1)} %bitcast.48, ...), custom_call_target="tpu_custom_call" | custom-call | tf_op jit(solution)/shard_map/pallas_call | solution.py:224
  84.4 1.5 %collective-permute-done.5 = f32[608,128]{1,0:T(8,128)S(1)} collective-permute-done((f32[608,128]{1,0:T(8,128)S(1)}, f32[608,128]{1,0:T(8,128)S(1)}, u32[]{:S(2)}, u32[]{:S(2)}) %collective-permute-start.5) | collective-permute-done | bytes 311328 | tf_op jit(solution)/shard_map/filter_grad_sum/ppermute | solution.py:244
  86.0 4.7 %collective-permute-start.6 = (f32[304,128]{1,0:T(8,128)S(1)}, f32[304,128]{1,0:T(8,128)S(1)}, u32[]{:S(2)}, u32[]{:S(2)}) collective-permute-start(f32[304,128]{1,0:T(8,128)S(1)} %slice_select_fusion.2), channel_id=1, source_target_pairs={{0,8},{8,0},{16,24},{24,16},{1,9},{9,1},{17,25},{25,17},{2,10},{10... | collective-permute-start | bytes 466952 | tf_op jit(solution)/shard_map/filter_grad_sum/ppermute | solution.py:244
  90.6 4.3 %collective-permute-done.6 = f32[304,128]{1,0:T(8,128)S(1)} collective-permute-done((f32[304,128]{1,0:T(8,128)S(1)}, f32[304,128]{1,0:T(8,128)S(1)}, u32[]{:S(2)}, u32[]{:S(2)}) %collective-permute-start.6) | collective-permute-done | bytes 155680 | tf_op jit(solution)/shard_map/filter_grad_sum/ppermute | solution.py:244
  95.0 1.8 %collective-permute-start.7 = (f32[152,128]{1,0:T(8,128)S(1)}, f32[152,128]{1,0:T(8,128)S(1)}, u32[]{:S(2)}, u32[]{:S(2)}) collective-permute-start(f32[152,128]{1,0:T(8,128)S(1)} %slice_select_fusion.3), channel_id=1, source_target_pairs={{0,16},{8,24},{16,0},{24,8},{1,17},{9,25},{17,1},{25,9},{2,18},{10... | collective-permute-start | bytes 233480 | tf_op jit(solution)/shard_map/filter_grad_sum/ppermute | solution.py:244
  96.8 2.7 %collective-permute-done.7 = f32[152,128]{1,0:T(8,128)S(1)} collective-permute-done((f32[152,128]{1,0:T(8,128)S(1)}, f32[152,128]{1,0:T(8,128)S(1)}, u32[]{:S(2)}, u32[]{:S(2)}) %collective-permute-start.7) | collective-permute-done | bytes 77856 | tf_op jit(solution)/shard_map/filter_grad_sum/ppermute | solution.py:244
  99.5 1.6 %collective-permute-start.8 = (f32[76,128]{1,0:T(8,128)S(1)}, f32[76,128]{1,0:T(8,128)S(1)}, u32[]{:S(2)}, u32[]{:S(2)}) collective-permute-start(f32[76,128]{1,0:T(8,128)S(1)} %slice_select_fusion.4), channel_id=1, source_target_pairs={{0,2},{1,3},{2,0},{3,1},{4,6},{5,7},{6,4},{7,5},{8,10},{9,11},{10,... | collective-permute-start | bytes 116744 | tf_op jit(solution)/shard_map/filter_grad_sum/ppermute | solution.py:244
  101.2 2.4 %collective-permute-done.8 = f32[76,128]{1,0:T(8,128)S(1)} collective-permute-done((f32[76,128]{1,0:T(8,128)S(1)}, f32[76,128]{1,0:T(8,128)S(1)}, u32[]{:S(2)}, u32[]{:S(2)}) %collective-permute-start.8) | collective-permute-done | bytes 38944 | tf_op jit(solution)/shard_map/filter_grad_sum/ppermute | solution.py:244
  103.6 2.8 %collective-permute-start.9 = (f32[38,128]{1,0:T(8,128)S(1)}, f32[38,128]{1,0:T(8,128)S(1)}, u32[]{:S(2)}, u32[]{:S(2)}) collective-permute-start(f32[38,128]{1,0:T(8,128)S(1)} %slice_select_fusion.5), channel_id=1, source_target_pairs={{0,4},{1,5},{2,6},{3,7},{4,0},{5,1},{6,2},{7,3},{8,12},{9,13},{10,... | collective-permute-start | bytes 58376 | tf_op jit(solution)/shard_map/filter_grad_sum/ppermute | solution.py:244
  106.4 2.1 %collective-permute-done.9 = f32[38,128]{1,0:T(8,128)S(1)} collective-permute-done((f32[38,128]{1,0:T(8,128)S(1)}, f32[38,128]{1,0:T(8,128)S(1)}, u32[]{:S(2)}, u32[]{:S(2)}) %collective-permute-start.9) | collective-permute-done | bytes 19488 | tf_op jit(solution)/shard_map/filter_grad_sum/ppermute | solution.py:244
  108.5 2.7 %collective-permute-start.10 = (f32[38,128]{1,0:T(8,128)S(1)}, f32[38,128]{1,0:T(8,128)S(1)}, u32[]{:S(2)}, u32[]{:S(2)}) collective-permute-start(f32[38,128]{1,0:T(8,128)S(1)} %select_add_fusion.3), channel_id=1, source_target_pairs={{0,4},{1,5},{2,6},{3,7},{4,0},{5,1},{6,2},{7,3},{8,12},{9,13},{10,... | collective-permute-start | bytes 58376 | tf_op jit(solution)/shard_map/filter_grad_sum/ppermute | solution.py:244
  111.2 2.0 %collective-permute-done.10 = f32[38,128]{1,0:T(8,128)S(1)} collective-permute-done((f32[38,128]{1,0:T(8,128)S(1)}, f32[38,128]{1,0:T(8,128)S(1)}, u32[]{:S(2)}, u32[]{:S(2)}) %collective-permute-start.10) | collective-permute-done | bytes 19488 | tf_op jit(solution)/shard_map/filter_grad_sum/ppermute | solution.py:244
  113.3 1.7 %collective-permute-start.11 = (f32[76,128]{1,0:T(8,128)S(1)}, f32[76,128]{1,0:T(8,128)S(1)}, u32[]{:S(2)}, u32[]{:S(2)}) collective-permute-start(f32[76,128]{1,0:T(8,128)S(1)} %maximum_select_fusion.4), channel_id=1, source_target_pairs={{0,2},{1,3},{2,0},{3,1},{4,6},{5,7},{6,4},{7,5},{8,10},{9,11},{10,... | collective-permute-start | bytes 116744 | tf_op jit(solution)/shard_map/filter_grad_sum/ppermute | solution.py:244
  117.3 2.7 %collective-permute-start.12 = (f32[152,128]{1,0:T(8,128)S(1)}, f32[152,128]{1,0:T(8,128)S(1)}, u32[]{:S(2)}, u32[]{:S(2)}) collective-permute-start(f32[152,128]{1,0:T(8,128)S(1)} %maximum_select_fusion.3), channel_id=1, source_target_pairs={{0,16},{8,24},{16,0},{24,8},{1,17},{9,25},{17,1},{25,9},{2,18},{10... | collective-permute-start | bytes 233480 | tf_op jit(solution)/shard_map/filter_grad_sum/ppermute | solution.py:244
  120.1 2.3 %collective-permute-done.12 = f32[152,128]{1,0:T(8,128)S(1)} collective-permute-done((f32[152,128]{1,0:T(8,128)S(1)}, f32[152,128]{1,0:T(8,128)S(1)}, u32[]{:S(2)}, u32[]{:S(2)}) %collective-permute-start.12) | collective-permute-done | bytes 77856 | tf_op jit(solution)/shard_map/filter_grad_sum/ppermute | solution.py:244
  122.4 5.3 %collective-permute-start.13 = (f32[304,128]{1,0:T(8,128)S(1)}, f32[304,128]{1,0:T(8,128)S(1)}, u32[]{:S(2)}, u32[]{:S(2)}) collective-permute-start(f32[304,128]{1,0:T(8,128)S(1)} %maximum_select_fusion.2), channel_id=1, source_target_pairs={{0,8},{8,0},{16,24},{24,16},{1,9},{9,1},{17,25},{25,17},{2,10},{10... | collective-permute-start | bytes 466952 | tf_op jit(solution)/shard_map/filter_grad_sum/ppermute | solution.py:244
  128.2 2.7 %collective-permute-done.13 = f32[304,128]{1,0:T(8,128)S(1)} collective-permute-done((f32[304,128]{1,0:T(8,128)S(1)}, f32[304,128]{1,0:T(8,128)S(1)}, u32[]{:S(2)}, u32[]{:S(2)}) %collective-permute-start.13) | collective-permute-done | bytes 155680 | tf_op jit(solution)/shard_map/filter_grad_sum/ppermute | solution.py:244
  (58 shorter events, 19.2 us)
Async XLA Ops:
  2.5 25.4 %copy-start = (f32[16,4096]{1,0:T(8,128)S(1)}, f32[16,4096]{1,0:T(8,128)}, u32[]{:S(2)}) copy-start(f32[16,4096]{1,0:T(8,128)} %param.15) | copy-start | bytes 786436
  2.5 23.3 %collective-permute-start = (bf16[3,8,4096]{2,1,0:T(8,128)(2,1)S(1)}, bf16[3,8,4096]{2,1,0:T(8,128)(2,1)S(1)}, u32[]{:S(2)}, u32[]{:S(2)}) collective-permute-start(bf16[3,8,4096]{2,1,0:T(8,128)(2,1)S(1)} %pad_maximum_fusion.1), channel_id=1, source_target_pairs={{0,8},{8,16},{16,24},{1,9},{9,17},{17,25},{2,10},{10,18},{18,26},{... | collective-permute-start | bytes 589832 | tf_op jit(solution)/shard_map/ppermute | solution.py:20
  25.9 22.6 %copy-start.2 = (bf16[3,8,4096]{2,1,0:T(8,128)(2,1)}, bf16[3,8,4096]{2,1,0:T(8,128)(2,1)S(1)}, u32[]{:S(2)}) copy-start(bf16[3,8,4096]{2,1,0:T(8,128)(2,1)S(1)} %collective-permute-done.rim_ref) | copy-start | bytes 589828
  29.4 7.8 %collective-permute-start.1 = (f32[16,4096]{1,0:T(8,128)S(1)}, f32[16,4096]{1,0:T(8,128)S(1)}, u32[]{:S(2)}, u32[]{:S(2)}) collective-permute-start(f32[16,4096]{1,0:T(8,128)S(1)} %broadcast_select_fusion), channel_id=1, source_target_pairs={{0,8},{8,0},{16,24},{24,16},{1,9},{9,1},{17,25},{25,17},{2,10},{10... | collective-permute-start | bytes 786440 | tf_op jit(solution)/shard_map/modal_state_scan/ppermute | solution.py:244
  38.7 8.8 %collective-permute-start.2 = (f32[16,4096]{1,0:T(8,128)S(1)}, f32[16,4096]{1,0:T(8,128)S(1)}, u32[]{:S(2)}, u32[]{:S(2)}) collective-permute-start(f32[16,4096]{1,0:T(8,128)S(1)} %add_select_fusion), channel_id=1, source_target_pairs={{8,24},{16,0},{9,25},{17,1},{10,26},{18,2},{11,27},{19,3},{12,28},... | collective-permute-start | bytes 786440 | tf_op jit(solution)/shard_map/modal_state_scan/ppermute | solution.py:257
  40.0 7.5 %collective-permute-start.3 = (f32[16,4096]{1,0:T(8,128)S(1)}, f32[16,4096]{1,0:T(8,128)S(1)}, u32[]{:S(2)}, u32[]{:S(2)}) collective-permute-start(f32[16,4096]{1,0:T(8,128)S(1)} %add_select_fusion), channel_id=1, source_target_pairs={{8,16},{16,8},{9,17},{17,9},{10,18},{18,10},{11,19},{19,11},{12,20... | collective-permute-start | bytes 786440 | tf_op jit(solution)/shard_map/modal_state_scan/ppermute | solution.py:258
  82.9 44.8 %copy-start.1 = (f32[3,16,4096]{2,1,0:T(8,128)S(1)}, f32[3,16,4096]{2,1,0:T(8,128)}, u32[]{:S(2)}) copy-start(f32[3,16,4096]{2,1,0:T(8,128)} %get-tuple-element.22) | copy-start | bytes 2359300
  84.2 1.7 %collective-permute-start.5 = (f32[608,128]{1,0:T(8,128)S(1)}, f32[608,128]{1,0:T(8,128)S(1)}, u32[]{:S(2)}, u32[]{:S(2)}) collective-permute-start(f32[608,128]{1,0:T(8,128)S(1)} %select_n.213), channel_id=1, source_target_pairs={{0,1},{1,0},{2,3},{3,2},{4,5},{5,4},{6,7},{7,6},{8,9},{9,8},{10,11... | collective-permute-start | bytes 933896 | tf_op jit(solution)/shard_map/filter_grad_sum/ppermute | solution.py:244
  86.0 9.0 %collective-permute-start.6 = (f32[304,128]{1,0:T(8,128)S(1)}, f32[304,128]{1,0:T(8,128)S(1)}, u32[]{:S(2)}, u32[]{:S(2)}) collective-permute-start(f32[304,128]{1,0:T(8,128)S(1)} %slice_select_fusion.2), channel_id=1, source_target_pairs={{0,8},{8,0},{16,24},{24,16},{1,9},{9,1},{17,25},{25,17},{2,10},{10... | collective-permute-start | bytes 466952 | tf_op jit(solution)/shard_map/filter_grad_sum/ppermute | solution.py:244
  95.0 4.5 %collective-permute-start.7 = (f32[152,128]{1,0:T(8,128)S(1)}, f32[152,128]{1,0:T(8,128)S(1)}, u32[]{:S(2)}, u32[]{:S(2)}) collective-permute-start(f32[152,128]{1,0:T(8,128)S(1)} %slice_select_fusion.3), channel_id=1, source_target_pairs={{0,16},{8,24},{16,0},{24,8},{1,17},{9,25},{17,1},{25,9},{2,18},{10... | collective-permute-start | bytes 233480 | tf_op jit(solution)/shard_map/filter_grad_sum/ppermute | solution.py:244
  99.5 4.1 %collective-permute-start.8 = (f32[76,128]{1,0:T(8,128)S(1)}, f32[76,128]{1,0:T(8,128)S(1)}, u32[]{:S(2)}, u32[]{:S(2)}) collective-permute-start(f32[76,128]{1,0:T(8,128)S(1)} %slice_select_fusion.4), channel_id=1, source_target_pairs={{0,2},{1,3},{2,0},{3,1},{4,6},{5,7},{6,4},{7,5},{8,10},{9,11},{10,... | collective-permute-start | bytes 116744 | tf_op jit(solution)/shard_map/filter_grad_sum/ppermute | solution.py:244
  103.6 4.9 %collective-permute-start.9 = (f32[38,128]{1,0:T(8,128)S(1)}, f32[38,128]{1,0:T(8,128)S(1)}, u32[]{:S(2)}, u32[]{:S(2)}) collective-permute-start(f32[38,128]{1,0:T(8,128)S(1)} %slice_select_fusion.5), channel_id=1, source_target_pairs={{0,4},{1,5},{2,6},{3,7},{4,0},{5,1},{6,2},{7,3},{8,12},{9,13},{10,... | collective-permute-start | bytes 58376 | tf_op jit(solution)/shard_map/filter_grad_sum/ppermute | solution.py:244
  108.5 4.7 %collective-permute-start.10 = (f32[38,128]{1,0:T(8,128)S(1)}, f32[38,128]{1,0:T(8,128)S(1)}, u32[]{:S(2)}, u32[]{:S(2)}) collective-permute-start(f32[38,128]{1,0:T(8,128)S(1)} %select_add_fusion.3), channel_id=1, source_target_pairs={{0,4},{1,5},{2,6},{3,7},{4,0},{5,1},{6,2},{7,3},{8,12},{9,13},{10,... | collective-permute-start | bytes 58376 | tf_op jit(solution)/shard_map/filter_grad_sum/ppermute | solution.py:244
  113.3 4.1 %collective-permute-start.11 = (f32[76,128]{1,0:T(8,128)S(1)}, f32[76,128]{1,0:T(8,128)S(1)}, u32[]{:S(2)}, u32[]{:S(2)}) collective-permute-start(f32[76,128]{1,0:T(8,128)S(1)} %maximum_select_fusion.4), channel_id=1, source_target_pairs={{0,2},{1,3},{2,0},{3,1},{4,6},{5,7},{6,4},{7,5},{8,10},{9,11},{10,... | collective-permute-start | bytes 116744 | tf_op jit(solution)/shard_map/filter_grad_sum/ppermute | solution.py:244
  114.9 12.8 %collective-permute-start.4 = (f32[3,8,4096]{2,1,0:T(8,128)}, f32[3,8,4096]{2,1,0:T(8,128)S(1)}, u32[]{:S(2)}, u32[]{:S(2)}) collective-permute-start(f32[3,8,4096]{2,1,0:T(8,128)} %get-tuple-element.23), channel_id=1, source_target_pairs={{8,0},{16,8},{24,16},{9,1},{17,9},{25,17},{10,2},{18,10},{26,18},{... | collective-permute-start | bytes 1179656 | tf_op jit(solution)/shard_map/ppermute | solution.py:20
  117.3 5.1 %collective-permute-start.12 = (f32[152,128]{1,0:T(8,128)S(1)}, f32[152,128]{1,0:T(8,128)S(1)}, u32[]{:S(2)}, u32[]{:S(2)}) collective-permute-start(f32[152,128]{1,0:T(8,128)S(1)} %maximum_select_fusion.3), channel_id=1, source_target_pairs={{0,16},{8,24},{16,0},{24,8},{1,17},{9,25},{17,1},{25,9},{2,18},{10... | collective-permute-start | bytes 233480 | tf_op jit(solution)/shard_map/filter_grad_sum/ppermute | solution.py:244
  122.4 8.5 %collective-permute-start.13 = (f32[304,128]{1,0:T(8,128)S(1)}, f32[304,128]{1,0:T(8,128)S(1)}, u32[]{:S(2)}, u32[]{:S(2)}) collective-permute-start(f32[304,128]{1,0:T(8,128)S(1)} %maximum_select_fusion.2), channel_id=1, source_target_pairs={{0,8},{8,0},{16,24},{24,16},{1,9},{9,1},{17,25},{25,17},{2,10},{10... | collective-permute-start | bytes 466952 | tf_op jit(solution)/shard_map/filter_grad_sum/ppermute | solution.py:244
  131.0 1.7 %collective-permute-start.14 = (f32[608,128]{1,0:T(8,128)S(1)}, f32[608,128]{1,0:T(8,128)S(1)}, u32[]{:S(2)}, u32[]{:S(2)}) collective-permute-start(f32[608,128]{1,0:T(8,128)S(1)} %maximum_select_fusion.1), channel_id=1, source_target_pairs={{0,1},{1,0},{2,3},{3,2},{4,5},{5,4},{6,7},{7,6},{8,9},{9,8},{10,11... | collective-permute-start | bytes 933896 | tf_op jit(solution)/shard_map/filter_grad_sum/ppermute | solution.py:244

commit v10 on v8

--- a/solution.py
+++ b/solution.py
@@ -210,7 +210,7 @@
     rows, width = q.shape
     poles = a.shape[0]
     count = taps.shape[1]
-    lanes = min(LANES, width)
+    lanes = min(LANES // 2, width)
     ins = (q, k, v, c, rim, taps, a, r, skip, s_in, g_in, bare)
     out_shapes = [
         jax.ShapeDtypeStruct((rows, width), jnp.bfloat16),

time: 130 us -> 131 us (level)
  no operation moved by 1% of the time
where the time goes in v10:
time: 131 us
  Pallas kernels  48.6 us (37%)
  waiting for transfers between devices  35.6 us (27%)
  starting transfers between devices  29.6 us (23%)
  local copies, waits for them, and re-layouts  8.39 us (6%)
  other arithmetic  7.29 us (6%)
    pallas_call x1, Pallas kernels, run_main(): pl.pallas_call(main_kernel, grid=(width // lanes,), in_specs=[tile(x.shap...  35.6 us
    ppermute x11, waiting for transfers between devices, exchange(): return lax.ppermute(x, axis, [(i, i ^ size) for i in range(count)])  26.8 us
    ppermute x11, starting transfers between devices, exchange(): return lax.ppermute(x, axis, [(i, i ^ size) for i in range(count)])  21.5 us
    pallas_call x1, Pallas kernels, run_states(): pl.pallas_call(states_kernel, grid=(width // lanes,), in_specs=[tile(x.sh...  13.1 us
    ppermute x1, waiting for transfers between devices, scan_four(): across = lax.ppermute(sent, axis, [(1, 3), (2, 0)])  6.8 us
    ppermute x2, starting transfers between devices, passed_along(): return lax.ppermute(x, axis, pairs)  6.16 us
  transfers between devices with their start and end apart: 15, of which 13 were waited for; matrix products, arithmetic and copies ran while one was open for 5% of the time, Pallas kernels for 10%

profile of v10, /device:TPU:0, one launch (start us, length us, event | category | flops | bytes accessed | tf_op | source)
XLA Modules:
  0.0 130.5 jit_solution(9598301456211900643)
XLA Ops:
  2.5 4.9 %collective-permute-start = (bf16[3,8,4096]{2,1,0:T(8,128)(2,1)S(1)}, bf16[3,8,4096]{2,1,0:T(8,128)(2,1)S(1)}, u32[]{:S(2)}, u32[]{:S(2)}) collective-permute-start(bf16[3,8,4096]{2,1,0:T(8,128)(2,1)S(1)} %pad_maximum_fusion.1), channel_id=1, source_target_pairs={{0,8},{8,16},{16,24},{1,9},{9,17},{17,25},{2,10},{10,18},{18,26},{... | collective-permute-start | bytes 589832 | tf_op jit(solution)/shard_map/ppermute | solution.py:20
  7.4 2.5 %fusion.50 = (f32[3,1,4096]{2,1,0:T(1,128)S(1)}, f32[3,1,4096]{2,1,0:T(1,128)S(1)}, f32[3,1,4096]{2,1,0:T(1,128)S(1)}, f32[3,1,4096]{2,1,0:T(1,128)S(1)}, f32[3,...) fusion(f32[3,7,4096]{2,1,0:T(8,128)} %taps_ref.3), kind=kLoop, calls=%fused_computation.115 | loop fusion | bytes 688128 | tf_op jit(solution)/shard_map/rim_share_of_states/slice | solution.py:352
  9.9 1.7 %fusion.51 = (f32[16,4096]{1,0:T(8,128)S(1)}, f32[16,4096]{1,0:T(8,128)}) fusion(f32[16,4096]{1,0:T(8,128)} %param.15), kind=kLoop, calls=%fused_computation.116 | loop fusion | flops 65536 | bytes 786432 | tf_op jit(solution)/shard_map/neg | solution.py:345
  12.6 13.1 %shard_map.135 = (f32[16,4096]{1,0:T(8,128)}, f32[16,4096]{1,0:T(8,128)}, f32[3,128,4096]{2,1,0:T(8,128)}) custom-call(bf16[128,4096]{1,0:T(8,128)(2,1)} %bitcast.33, bf16[128,4096]{1,0:T(8,128)(2,1)} %bitcast.35, bf16[128,4096]{1,0:T(8,128)(2,1)} %bitcast.37, bf16[128,4096]{1,0:T(8,128)(2,1)} %bitcast.39, bf16[3,8,4096]{2,1,0:T(8,128)(2,1)} %broadcast_in_dim.14.rim_ref, ...), custom_call_target="tpu_custom_call" | custom-call | tf_op jit(solution)/shard_map/pallas_call | solution.py:195
  28.4 1.5 %collective-permute-start.1 = (f32[16,4096]{1,0:T(8,128)S(1)}, f32[16,4096]{1,0:T(8,128)S(1)}, u32[]{:S(2)}, u32[]{:S(2)}) collective-permute-start(f32[16,4096]{1,0:T(8,128)S(1)} %get-tuple-element.29), channel_id=1, source_target_pairs={{0,8},{8,0},{16,24},{24,16},{1,9},{9,1},{17,25},{25,17},{2,10},{10... | collective-permute-start | bytes 786440 | tf_op jit(solution)/shard_map/modal_state_scan/ppermute | solution.py:244
  29.9 6.3 %collective-permute-done.1 = f32[16,4096]{1,0:T(8,128)S(1)} collective-permute-done((f32[16,4096]{1,0:T(8,128)S(1)}, f32[16,4096]{1,0:T(8,128)S(1)}, u32[]{:S(2)}, u32[]{:S(2)}) %collective-permute-start.1) | collective-permute-done | bytes 262176 | tf_op jit(solution)/shard_map/modal_state_scan/ppermute | solution.py:244
  38.3 6.8 %collective-permute-done.2 = f32[16,4096]{1,0:T(8,128)S(1)} collective-permute-done((f32[16,4096]{1,0:T(8,128)S(1)}, f32[16,4096]{1,0:T(8,128)S(1)}, u32[]{:S(2)}, u32[]{:S(2)}) %collective-permute-start.2) | collective-permute-done | bytes 262176 | tf_op jit(solution)/shard_map/modal_state_scan/ppermute | solution.py:257
  46.0 35.6 %shard_map.136 = (bf16[128,4096]{1,0:T(8,128)(2,1)}, bf16[128,4096]{1,0:T(8,128)(2,1)}, bf16[128,4096]{1,0:T(8,128)(2,1)}, bf16[128,4096]{1,0:T(8,128)(2,1)}, f3...) custom-call(bf16[128,4096]{1,0:T(8,128)(2,1)} %bitcast.34, bf16[128,4096]{1,0:T(8,128)(2,1)} %bitcast.36, ...), custom_call_target="tpu_custom_call" | custom-call | tf_op jit(solution)/shard_map/pallas_call | solution.py:224
  83.0 1.5 %collective-permute-done.5 = f32[608,128]{1,0:T(8,128)S(1)} collective-permute-done((f32[608,128]{1,0:T(8,128)S(1)}, f32[608,128]{1,0:T(8,128)S(1)}, u32[]{:S(2)}, u32[]{:S(2)}) %collective-permute-start.5) | collective-permute-done | bytes 311328 | tf_op jit(solution)/shard_map/filter_grad_sum/ppermute | solution.py:244
  84.6 4.7 %collective-permute-start.6 = (f32[304,128]{1,0:T(8,128)S(1)}, f32[304,128]{1,0:T(8,128)S(1)}, u32[]{:S(2)}, u32[]{:S(2)}) collective-permute-start(f32[304,128]{1,0:T(8,128)S(1)} %slice_select_fusion.2), channel_id=1, source_target_pairs={{0,8},{8,0},{16,24},{24,16},{1,9},{9,1},{17,25},{25,17},{2,10},{10... | collective-permute-start | bytes 466952 | tf_op jit(solution)/shard_map/filter_grad_sum/ppermute | solution.py:244
  89.3 4.3 %collective-permute-done.6 = f32[304,128]{1,0:T(8,128)S(1)} collective-permute-done((f32[304,128]{1,0:T(8,128)S(1)}, f32[304,128]{1,0:T(8,128)S(1)}, u32[]{:S(2)}, u32[]{:S(2)}) %collective-permute-start.6) | collective-permute-done | bytes 155680 | tf_op jit(solution)/shard_map/filter_grad_sum/ppermute | solution.py:244
  93.6 1.8 %collective-permute-start.7 = (f32[152,128]{1,0:T(8,128)S(1)}, f32[152,128]{1,0:T(8,128)S(1)}, u32[]{:S(2)}, u32[]{:S(2)}) collective-permute-start(f32[152,128]{1,0:T(8,128)S(1)} %slice_select_fusion.3), channel_id=1, source_target_pairs={{0,16},{8,24},{16,0},{24,8},{1,17},{9,25},{17,1},{25,9},{2,18},{10... | collective-permute-start | bytes 233480 | tf_op jit(solution)/shard_map/filter_grad_sum/ppermute | solution.py:244
  95.4 2.7 %collective-permute-done.7 = f32[152,128]{1,0:T(8,128)S(1)} collective-permute-done((f32[152,128]{1,0:T(8,128)S(1)}, f32[152,128]{1,0:T(8,128)S(1)}, u32[]{:S(2)}, u32[]{:S(2)}) %collective-permute-start.7) | collective-permute-done | bytes 77856 | tf_op jit(solution)/shard_map/filter_grad_sum/ppermute | solution.py:244
  98.1 1.6 %collective-permute-start.8 = (f32[76,128]{1,0:T(8,128)S(1)}, f32[76,128]{1,0:T(8,128)S(1)}, u32[]{:S(2)}, u32[]{:S(2)}) collective-permute-start(f32[76,128]{1,0:T(8,128)S(1)} %slice_select_fusion.4), channel_id=1, source_target_pairs={{0,2},{1,3},{2,0},{3,1},{4,6},{5,7},{6,4},{7,5},{8,10},{9,11},{10,... | collective-permute-start | bytes 116744 | tf_op jit(solution)/shard_map/filter_grad_sum/ppermute | solution.py:244
  99.8 2.4 %collective-permute-done.8 = f32[76,128]{1,0:T(8,128)S(1)} collective-permute-done((f32[76,128]{1,0:T(8,128)S(1)}, f32[76,128]{1,0:T(8,128)S(1)}, u32[]{:S(2)}, u32[]{:S(2)}) %collective-permute-start.8) | collective-permute-done | bytes 38944 | tf_op jit(solution)/shard_map/filter_grad_sum/ppermute | solution.py:244
  102.2 2.8 %collective-permute-start.9 = (f32[38,128]{1,0:T(8,128)S(1)}, f32[38,128]{1,0:T(8,128)S(1)}, u32[]{:S(2)}, u32[]{:S(2)}) collective-permute-start(f32[38,128]{1,0:T(8,128)S(1)} %slice_select_fusion.5), channel_id=1, source_target_pairs={{0,4},{1,5},{2,6},{3,7},{4,0},{5,1},{6,2},{7,3},{8,12},{9,13},{10,... | collective-permute-start | bytes 58376 | tf_op jit(solution)/shard_map/filter_grad_sum/ppermute | solution.py:244
  105.0 2.1 %collective-permute-done.9 = f32[38,128]{1,0:T(8,128)S(1)} collective-permute-done((f32[38,128]{1,0:T(8,128)S(1)}, f32[38,128]{1,0:T(8,128)S(1)}, u32[]{:S(2)}, u32[]{:S(2)}) %collective-permute-start.9) | collective-permute-done | bytes 19488 | tf_op jit(solution)/shard_map/filter_grad_sum/ppermute | solution.py:244
  107.1 2.7 %collective-permute-start.10 = (f32[38,128]{1,0:T(8,128)S(1)}, f32[38,128]{1,0:T(8,128)S(1)}, u32[]{:S(2)}, u32[]{:S(2)}) collective-permute-start(f32[38,128]{1,0:T(8,128)S(1)} %select_add_fusion.3), channel_id=1, source_target_pairs={{0,4},{1,5},{2,6},{3,7},{4,0},{5,1},{6,2},{7,3},{8,12},{9,13},{10,... | collective-permute-start | bytes 58376 | tf_op jit(solution)/shard_map/filter_grad_sum/ppermute | solution.py:244
  109.8 2.0 %collective-permute-done.10 = f32[38,128]{1,0:T(8,128)S(1)} collective-permute-done((f32[38,128]{1,0:T(8,128)S(1)}, f32[38,128]{1,0:T(8,128)S(1)}, u32[]{:S(2)}, u32[]{:S(2)}) %collective-permute-start.10) | collective-permute-done | bytes 19488 | tf_op jit(solution)/shard_map/filter_grad_sum/ppermute | solution.py:244
  111.9 1.7 %collective-permute-start.11 = (f32[76,128]{1,0:T(8,128)S(1)}, f32[76,128]{1,0:T(8,128)S(1)}, u32[]{:S(2)}, u32[]{:S(2)}) collective-permute-start(f32[76,128]{1,0:T(8,128)S(1)} %maximum_select_fusion.4), channel_id=1, source_target_pairs={{0,2},{1,3},{2,0},{3,1},{4,6},{5,7},{6,4},{7,5},{8,10},{9,11},{10,... | collective-permute-start | bytes 116744 | tf_op jit(solution)/shard_map/filter_grad_sum/ppermute | solution.py:244
  116.0 2.7 %collective-permute-start.12 = (f32[152,128]{1,0:T(8,128)S(1)}, f32[152,128]{1,0:T(8,128)S(1)}, u32[]{:S(2)}, u32[]{:S(2)}) collective-permute-start(f32[152,128]{1,0:T(8,128)S(1)} %maximum_select_fusion.3), channel_id=1, source_target_pairs={{0,16},{8,24},{16,0},{24,8},{1,17},{9,25},{17,1},{25,9},{2,18},{10... | collective-permute-start | bytes 233480 | tf_op jit(solution)/shard_map/filter_grad_sum/ppermute | solution.py:244
  118.7 2.3 %collective-permute-done.12 = f32[152,128]{1,0:T(8,128)S(1)} collective-permute-done((f32[152,128]{1,0:T(8,128)S(1)}, f32[152,128]{1,0:T(8,128)S(1)}, u32[]{:S(2)}, u32[]{:S(2)}) %collective-permute-start.12) | collective-permute-done | bytes 77856 | tf_op jit(solution)/shard_map/filter_grad_sum/ppermute | solution.py:244
  121.1 1.8 %collective-permute-start.13 = (f32[304,128]{1,0:T(8,128)S(1)}, f32[304,128]{1,0:T(8,128)S(1)}, u32[]{:S(2)}, u32[]{:S(2)}) collective-permute-start(f32[304,128]{1,0:T(8,128)S(1)} %maximum_select_fusion.2), channel_id=1, source_target_pairs={{0,8},{8,0},{16,24},{24,16},{1,9},{9,1},{17,25},{25,17},{2,10},{10... | collective-permute-start | bytes 466952 | tf_op jit(solution)/shard_map/filter_grad_sum/ppermute | solution.py:244
  122.9 2.0 %collective-permute-done.4 = f32[3,8,4096]{2,1,0:T(8,128)S(1)} collective-permute-done((f32[3,8,4096]{2,1,0:T(8,128)S(1)}, f32[3,8,4096]{2,1,0:T(8,128)S(1)}, u32[]{:S(2)}, u32[]{:S(2)}) %collective-permute-start.4) | collective-permute-done | bytes 393248 | tf_op jit(solution)/shard_map/ppermute | solution.py:20
  (64 shorter events, 18.0 us)
Async XLA Ops:
  2.5 23.2 %collective-permute-start = (bf16[3,8,4096]{2,1,0:T(8,128)(2,1)S(1)}, bf16[3,8,4096]{2,1,0:T(8,128)(2,1)S(1)}, u32[]{:S(2)}, u32[]{:S(2)}) collective-permute-start(bf16[3,8,4096]{2,1,0:T(8,128)(2,1)S(1)} %pad_maximum_fusion.1), channel_id=1, source_target_pairs={{0,8},{8,16},{16,24},{1,9},{9,17},{17,25},{2,10},{10,18},{18,26},{... | collective-permute-start | bytes 589832 | tf_op jit(solution)/shard_map/ppermute | solution.py:20
  25.7 2.5 %copy-start.2 = (bf16[3,8,4096]{2,1,0:T(8,128)(2,1)}, bf16[3,8,4096]{2,1,0:T(8,128)(2,1)S(1)}, u32[]{:S(2)}) copy-start(bf16[3,8,4096]{2,1,0:T(8,128)(2,1)S(1)} %collective-permute-done.rim_ref) | copy-start | bytes 589828
  25.8 2.5 %copy-start.3 = (f32[16,4096]{1,0:T(8,128)S(1)}, f32[16,4096]{1,0:T(8,128)}, u32[]{:S(2)}) copy-start(f32[16,4096]{1,0:T(8,128)} %get-tuple-element.18) | copy-start | bytes 786436
  25.8 2.5 %copy-start.4 = (f32[16,4096]{1,0:T(8,128)S(1)}, f32[16,4096]{1,0:T(8,128)}, u32[]{:S(2)}) copy-start(f32[16,4096]{1,0:T(8,128)} %get-tuple-element.17) | copy-start | bytes 786436
  27.6 8.6 %copy-start = (f32[16,4096]{1,0:T(8,128)S(1)}, f32[16,4096]{1,0:T(8,128)}, u32[]{:S(2)}) copy-start(f32[16,4096]{1,0:T(8,128)} %param.15) | copy-start | bytes 786436
  28.4 7.8 %collective-permute-start.1 = (f32[16,4096]{1,0:T(8,128)S(1)}, f32[16,4096]{1,0:T(8,128)S(1)}, u32[]{:S(2)}, u32[]{:S(2)}) collective-permute-start(f32[16,4096]{1,0:T(8,128)S(1)} %get-tuple-element.29), channel_id=1, source_target_pairs={{0,8},{8,0},{16,24},{24,16},{1,9},{9,1},{17,25},{25,17},{2,10},{10... | collective-permute-start | bytes 786440 | tf_op jit(solution)/shard_map/modal_state_scan/ppermute | solution.py:244
  36.3 8.8 %collective-permute-start.2 = (f32[16,4096]{1,0:T(8,128)S(1)}, f32[16,4096]{1,0:T(8,128)S(1)}, u32[]{:S(2)}, u32[]{:S(2)}) collective-permute-start(f32[16,4096]{1,0:T(8,128)S(1)} %add_select_fusion), channel_id=1, source_target_pairs={{8,24},{16,0},{9,25},{17,1},{10,26},{18,2},{11,27},{19,3},{12,28},... | collective-permute-start | bytes 786440 | tf_op jit(solution)/shard_map/modal_state_scan/ppermute | solution.py:257
  37.6 7.5 %collective-permute-start.3 = (f32[16,4096]{1,0:T(8,128)S(1)}, f32[16,4096]{1,0:T(8,128)S(1)}, u32[]{:S(2)}, u32[]{:S(2)}) collective-permute-start(f32[16,4096]{1,0:T(8,128)S(1)} %add_select_fusion), channel_id=1, source_target_pairs={{8,16},{16,8},{9,17},{17,9},{10,18},{18,10},{11,19},{19,11},{12,20... | collective-permute-start | bytes 786440 | tf_op jit(solution)/shard_map/modal_state_scan/ppermute | solution.py:258
  82.8 30.7 %copy-start.5 = (f32[3,8,4096]{2,1,0:T(8,128)S(1)}, f32[3,8,4096]{2,1,0:T(8,128)}, u32[]{:S(2)}) copy-start(f32[3,8,4096]{2,1,0:T(8,128)} %get-tuple-element.23) | copy-start | bytes 1179652
  82.8 1.7 %collective-permute-start.5 = (f32[608,128]{1,0:T(8,128)S(1)}, f32[608,128]{1,0:T(8,128)S(1)}, u32[]{:S(2)}, u32[]{:S(2)}) collective-permute-start(f32[608,128]{1,0:T(8,128)S(1)} %select_n.213), channel_id=1, source_target_pairs={{0,1},{1,0},{2,3},{3,2},{4,5},{5,4},{6,7},{7,6},{8,9},{9,8},{10,11... | collective-permute-start | bytes 933896 | tf_op jit(solution)/shard_map/filter_grad_sum/ppermute | solution.py:244
  82.9 42.0 %copy-start.1 = (f32[3,16,4096]{2,1,0:T(8,128)S(1)}, f32[3,16,4096]{2,1,0:T(8,128)}, u32[]{:S(2)}) copy-start(f32[3,16,4096]{2,1,0:T(8,128)} %get-tuple-element.22) | copy-start | bytes 2359300
  84.6 9.0 %collective-permute-start.6 = (f32[304,128]{1,0:T(8,128)S(1)}, f32[304,128]{1,0:T(8,128)S(1)}, u32[]{:S(2)}, u32[]{:S(2)}) collective-permute-start(f32[304,128]{1,0:T(8,128)S(1)} %slice_select_fusion.2), channel_id=1, source_target_pairs={{0,8},{8,0},{16,24},{24,16},{1,9},{9,1},{17,25},{25,17},{2,10},{10... | collective-permute-start | bytes 466952 | tf_op jit(solution)/shard_map/filter_grad_sum/ppermute | solution.py:244
  93.6 4.5 %collective-permute-start.7 = (f32[152,128]{1,0:T(8,128)S(1)}, f32[152,128]{1,0:T(8,128)S(1)}, u32[]{:S(2)}, u32[]{:S(2)}) collective-permute-start(f32[152,128]{1,0:T(8,128)S(1)} %slice_select_fusion.3), channel_id=1, source_target_pairs={{0,16},{8,24},{16,0},{24,8},{1,17},{9,25},{17,1},{25,9},{2,18},{10... | collective-permute-start | bytes 233480 | tf_op jit(solution)/shard_map/filter_grad_sum/ppermute | solution.py:244
  98.1 4.1 %collective-permute-start.8 = (f32[76,128]{1,0:T(8,128)S(1)}, f32[76,128]{1,0:T(8,128)S(1)}, u32[]{:S(2)}, u32[]{:S(2)}) collective-permute-start(f32[76,128]{1,0:T(8,128)S(1)} %slice_select_fusion.4), channel_id=1, source_target_pairs={{0,2},{1,3},{2,0},{3,1},{4,6},{5,7},{6,4},{7,5},{8,10},{9,11},{10,... | collective-permute-start | bytes 116744 | tf_op jit(solution)/shard_map/filter_grad_sum/ppermute | solution.py:244
  102.2 4.9 %collective-permute-start.9 = (f32[38,128]{1,0:T(8,128)S(1)}, f32[38,128]{1,0:T(8,128)S(1)}, u32[]{:S(2)}, u32[]{:S(2)}) collective-permute-start(f32[38,128]{1,0:T(8,128)S(1)} %slice_select_fusion.5), channel_id=1, source_target_pairs={{0,4},{1,5},{2,6},{3,7},{4,0},{5,1},{6,2},{7,3},{8,12},{9,13},{10,... | collective-permute-start | bytes 58376 | tf_op jit(solution)/shard_map/filter_grad_sum/ppermute | solution.py:244
  107.1 4.7 %collective-permute-start.10 = (f32[38,128]{1,0:T(8,128)S(1)}, f32[38,128]{1,0:T(8,128)S(1)}, u32[]{:S(2)}, u32[]{:S(2)}) collective-permute-start(f32[38,128]{1,0:T(8,128)S(1)} %select_add_fusion.3), channel_id=1, source_target_pairs={{0,4},{1,5},{2,6},{3,7},{4,0},{5,1},{6,2},{7,3},{8,12},{9,13},{10,... | collective-permute-start | bytes 58376 | tf_op jit(solution)/shard_map/filter_grad_sum/ppermute | solution.py:244
  111.9 4.1 %collective-permute-start.11 = (f32[76,128]{1,0:T(8,128)S(1)}, f32[76,128]{1,0:T(8,128)S(1)}, u32[]{:S(2)}, u32[]{:S(2)}) collective-permute-start(f32[76,128]{1,0:T(8,128)S(1)} %maximum_select_fusion.4), channel_id=1, source_target_pairs={{0,2},{1,3},{2,0},{3,1},{4,6},{5,7},{6,4},{7,5},{8,10},{9,11},{10,... | collective-permute-start | bytes 116744 | tf_op jit(solution)/shard_map/filter_grad_sum/ppermute | solution.py:244
  113.5 11.3 %collective-permute-start.4 = (f32[3,8,4096]{2,1,0:T(8,128)S(1)}, f32[3,8,4096]{2,1,0:T(8,128)S(1)}, u32[]{:S(2)}, u32[]{:S(2)}) collective-permute-start(f32[3,8,4096]{2,1,0:T(8,128)S(1)} %copy-done.5), channel_id=1, source_target_pairs={{8,0},{16,8},{24,16},{9,1},{17,9},{25,17},{10,2},{18,10},{26,18},{... | collective-permute-start | bytes 1179656 | tf_op jit(solution)/shard_map/ppermute | solution.py:20
  116.0 5.1 %collective-permute-start.12 = (f32[152,128]{1,0:T(8,128)S(1)}, f32[152,128]{1,0:T(8,128)S(1)}, u32[]{:S(2)}, u32[]{:S(2)}) collective-permute-start(f32[152,128]{1,0:T(8,128)S(1)} %maximum_select_fusion.3), channel_id=1, source_target_pairs={{0,16},{8,24},{16,0},{24,8},{1,17},{9,25},{17,1},{25,9},{2,18},{10... | collective-permute-start | bytes 233480 | tf_op jit(solution)/shard_map/filter_grad_sum/ppermute | solution.py:244
  121.1 5.5 %collective-permute-start.13 = (f32[304,128]{1,0:T(8,128)S(1)}, f32[304,128]{1,0:T(8,128)S(1)}, u32[]{:S(2)}, u32[]{:S(2)}) collective-permute-start(f32[304,128]{1,0:T(8,128)S(1)} %maximum_select_fusion.2), channel_id=1, source_target_pairs={{0,8},{8,0},{16,24},{24,16},{1,9},{9,1},{17,25},{25,17},{2,10},{10... | collective-permute-start | bytes 466952 | tf_op jit(solution)/shard_map/filter_grad_sum/ppermute | solution.py:244
  126.6 1.7 %collective-permute-start.14 = (f32[608,128]{1,0:T(8,128)S(1)}, f32[608,128]{1,0:T(8,128)S(1)}, u32[]{:S(2)}, u32[]{:S(2)}) collective-permute-start(f32[608,128]{1,0:T(8,128)S(1)} %maximum_select_fusion.1), channel_id=1, source_target_pairs={{0,1},{1,0},{2,3},{3,2},{4,5},{5,4},{6,7},{7,6},{8,9},{9,8},{10,11... | collective-permute-start | bytes 933896 | tf_op jit(solution)/shard_map/filter_grad_sum/ppermute | solution.py:244

commit v11 on v8

--- a/solution.py
+++ b/solution.py
@@ -124,7 +124,7 @@
         return (h, g, acc)
 
     h, g, acc = lax.fori_loop(
-        0, rows, step, (s_ref[...], g_ref[...], jnp.zeros_like(a)), unroll=8
+        0, rows, step, (s_ref[...], g_ref[...], jnp.zeros_like(a)), unroll=16
     )
     skip = skip_ref[...]
     for lo in range(0, rows, BR):

time: 130 us -> 129 us (level)
  no operation moved by 1% of the time
where the time goes in v11:
time: 129 us; the launch traced here: 128 us
  Pallas kernels  46.6 us (36%)
  waiting for transfers between devices  35.6 us (28%)
  starting transfers between devices  29.6 us (23%)
  local copies, waits for them, and re-layouts  8.39 us (7%)
  other arithmetic  7.29 us (6%)
    pallas_call x1, Pallas kernels, run_main(): pl.pallas_call(main_kernel, grid=(width // lanes,), in_specs=[tile(x.shap...  33.5 us
    ppermute x11, waiting for transfers between devices, exchange(): return lax.ppermute(x, axis, [(i, i ^ size) for i in range(count)])  26.8 us
    ppermute x11, starting transfers between devices, exchange(): return lax.ppermute(x, axis, [(i, i ^ size) for i in range(count)])  21.5 us
    pallas_call x1, Pallas kernels, run_states(): pl.pallas_call(states_kernel, grid=(width // lanes,), in_specs=[tile(x.sh...  13.1 us
    ppermute x1, waiting for transfers between devices, scan_four(): across = lax.ppermute(sent, axis, [(1, 3), (2, 0)])  6.8 us
    ppermute x2, starting transfers between devices, passed_along(): return lax.ppermute(x, axis, pairs)  6.16 us
  transfers between devices with their start and end apart: 15, of which 13 were waited for; matrix products, arithmetic and copies ran while one was open for 5% of the time, Pallas kernels for 10%

profile of v11, /device:TPU:0, one launch (start us, length us, event | category | flops | bytes accessed | tf_op | source)
XLA Modules:
  0.0 128.5 jit_solution(17938783374416115888)
XLA Ops:
  2.5 4.9 %collective-permute-start = (bf16[3,8,4096]{2,1,0:T(8,128)(2,1)S(1)}, bf16[3,8,4096]{2,1,0:T(8,128)(2,1)S(1)}, u32[]{:S(2)}, u32[]{:S(2)}) collective-permute-start(bf16[3,8,4096]{2,1,0:T(8,128)(2,1)S(1)} %pad_maximum_fusion.1), channel_id=1, source_target_pairs={{0,8},{8,16},{16,24},{1,9},{9,17},{17,25},{2,10},{10,18},{18,26},{... | collective-permute-start | bytes 589832 | tf_op jit(solution)/shard_map/ppermute | solution.py:20
  7.4 2.5 %fusion.50 = (f32[3,1,4096]{2,1,0:T(1,128)S(1)}, f32[3,1,4096]{2,1,0:T(1,128)S(1)}, f32[3,1,4096]{2,1,0:T(1,128)S(1)}, f32[3,1,4096]{2,1,0:T(1,128)S(1)}, f32[3,...) fusion(f32[3,7,4096]{2,1,0:T(8,128)} %taps_ref.3), kind=kLoop, calls=%fused_computation.115 | loop fusion | bytes 688128 | tf_op jit(solution)/shard_map/rim_share_of_states/slice | solution.py:352
  9.9 1.7 %fusion.51 = (f32[16,4096]{1,0:T(8,128)S(1)}, f32[16,4096]{1,0:T(8,128)}) fusion(f32[16,4096]{1,0:T(8,128)} %param.15), kind=kLoop, calls=%fused_computation.116 | loop fusion | flops 65536 | bytes 786432 | tf_op jit(solution)/shard_map/neg | solution.py:345
  12.6 13.1 %shard_map.135 = (f32[16,4096]{1,0:T(8,128)}, f32[16,4096]{1,0:T(8,128)}, f32[3,128,4096]{2,1,0:T(8,128)}) custom-call(bf16[128,4096]{1,0:T(8,128)(2,1)} %bitcast.33, bf16[128,4096]{1,0:T(8,128)(2,1)} %bitcast.35, bf16[128,4096]{1,0:T(8,128)(2,1)} %bitcast.37, bf16[128,4096]{1,0:T(8,128)(2,1)} %bitcast.39, bf16[3,8,4096]{2,1,0:T(8,128)(2,1)} %broadcast_in_dim.14.rim_ref, ...), custom_call_target="tpu_custom_call" | custom-call | tf_op jit(solution)/shard_map/pallas_call | solution.py:195
  28.4 1.5 %collective-permute-start.1 = (f32[16,4096]{1,0:T(8,128)S(1)}, f32[16,4096]{1,0:T(8,128)S(1)}, u32[]{:S(2)}, u32[]{:S(2)}) collective-permute-start(f32[16,4096]{1,0:T(8,128)S(1)} %get-tuple-element.29), channel_id=1, source_target_pairs={{0,8},{8,0},{16,24},{24,16},{1,9},{9,1},{17,25},{25,17},{2,10},{10... | collective-permute-start | bytes 786440 | tf_op jit(solution)/shard_map/modal_state_scan/ppermute | solution.py:244
  29.9 6.3 %collective-permute-done.1 = f32[16,4096]{1,0:T(8,128)S(1)} collective-permute-done((f32[16,4096]{1,0:T(8,128)S(1)}, f32[16,4096]{1,0:T(8,128)S(1)}, u32[]{:S(2)}, u32[]{:S(2)}) %collective-permute-start.1) | collective-permute-done | bytes 262176 | tf_op jit(solution)/shard_map/modal_state_scan/ppermute | solution.py:244
  38.3 6.8 %collective-permute-done.2 = f32[16,4096]{1,0:T(8,128)S(1)} collective-permute-done((f32[16,4096]{1,0:T(8,128)S(1)}, f32[16,4096]{1,0:T(8,128)S(1)}, u32[]{:S(2)}, u32[]{:S(2)}) %collective-permute-start.2) | collective-permute-done | bytes 262176 | tf_op jit(solution)/shard_map/modal_state_scan/ppermute | solution.py:257
  46.0 33.5 %shard_map.136 = (bf16[128,4096]{1,0:T(8,128)(2,1)}, bf16[128,4096]{1,0:T(8,128)(2,1)}, bf16[128,4096]{1,0:T(8,128)(2,1)}, bf16[128,4096]{1,0:T(8,128)(2,1)}, f3...) custom-call(bf16[128,4096]{1,0:T(8,128)(2,1)} %bitcast.34, bf16[128,4096]{1,0:T(8,128)(2,1)} %bitcast.36, ...), custom_call_target="tpu_custom_call" | custom-call | tf_op jit(solution)/shard_map/pallas_call | solution.py:224
  80.9 1.5 %collective-permute-done.5 = f32[608,128]{1,0:T(8,128)S(1)} collective-permute-done((f32[608,128]{1,0:T(8,128)S(1)}, f32[608,128]{1,0:T(8,128)S(1)}, u32[]{:S(2)}, u32[]{:S(2)}) %collective-permute-start.5) | collective-permute-done | bytes 311328 | tf_op jit(solution)/shard_map/filter_grad_sum/ppermute | solution.py:244
  82.5 4.7 %collective-permute-start.6 = (f32[304,128]{1,0:T(8,128)S(1)}, f32[304,128]{1,0:T(8,128)S(1)}, u32[]{:S(2)}, u32[]{:S(2)}) collective-permute-start(f32[304,128]{1,0:T(8,128)S(1)} %slice_select_fusion.2), channel_id=1, source_target_pairs={{0,8},{8,0},{16,24},{24,16},{1,9},{9,1},{17,25},{25,17},{2,10},{10... | collective-permute-start | bytes 466952 | tf_op jit(solution)/shard_map/filter_grad_sum/ppermute | solution.py:244
  87.2 4.3 %collective-permute-done.6 = f32[304,128]{1,0:T(8,128)S(1)} collective-permute-done((f32[304,128]{1,0:T(8,128)S(1)}, f32[304,128]{1,0:T(8,128)S(1)}, u32[]{:S(2)}, u32[]{:S(2)}) %collective-permute-start.6) | collective-permute-done | bytes 155680 | tf_op jit(solution)/shard_map/filter_grad_sum/ppermute | solution.py:244
  91.6 1.8 %collective-permute-start.7 = (f32[152,128]{1,0:T(8,128)S(1)}, f32[152,128]{1,0:T(8,128)S(1)}, u32[]{:S(2)}, u32[]{:S(2)}) collective-permute-start(f32[152,128]{1,0:T(8,128)S(1)} %slice_select_fusion.3), channel_id=1, source_target_pairs={{0,16},{8,24},{16,0},{24,8},{1,17},{9,25},{17,1},{25,9},{2,18},{10... | collective-permute-start | bytes 233480 | tf_op jit(solution)/shard_map/filter_grad_sum/ppermute | solution.py:244
  93.3 2.7 %collective-permute-done.7 = f32[152,128]{1,0:T(8,128)S(1)} collective-permute-done((f32[152,128]{1,0:T(8,128)S(1)}, f32[152,128]{1,0:T(8,128)S(1)}, u32[]{:S(2)}, u32[]{:S(2)}) %collective-permute-start.7) | collective-permute-done | bytes 77856 | tf_op jit(solution)/shard_map/filter_grad_sum/ppermute | solution.py:244
  96.1 1.6 %collective-permute-start.8 = (f32[76,128]{1,0:T(8,128)S(1)}, f32[76,128]{1,0:T(8,128)S(1)}, u32[]{:S(2)}, u32[]{:S(2)}) collective-permute-start(f32[76,128]{1,0:T(8,128)S(1)} %slice_select_fusion.4), channel_id=1, source_target_pairs={{0,2},{1,3},{2,0},{3,1},{4,6},{5,7},{6,4},{7,5},{8,10},{9,11},{10,... | collective-permute-start | bytes 116744 | tf_op jit(solution)/shard_map/filter_grad_sum/ppermute | solution.py:244
  97.7 2.4 %collective-permute-done.8 = f32[76,128]{1,0:T(8,128)S(1)} collective-permute-done((f32[76,128]{1,0:T(8,128)S(1)}, f32[76,128]{1,0:T(8,128)S(1)}, u32[]{:S(2)}, u32[]{:S(2)}) %collective-permute-start.8) | collective-permute-done | bytes 38944 | tf_op jit(solution)/shard_map/filter_grad_sum/ppermute | solution.py:244
  100.2 2.8 %collective-permute-start.9 = (f32[38,128]{1,0:T(8,128)S(1)}, f32[38,128]{1,0:T(8,128)S(1)}, u32[]{:S(2)}, u32[]{:S(2)}) collective-permute-start(f32[38,128]{1,0:T(8,128)S(1)} %slice_select_fusion.5), channel_id=1, source_target_pairs={{0,4},{1,5},{2,6},{3,7},{4,0},{5,1},{6,2},{7,3},{8,12},{9,13},{10,... | collective-permute-start | bytes 58376 | tf_op jit(solution)/shard_map/filter_grad_sum/ppermute | solution.py:244
  103.0 2.1 %collective-permute-done.9 = f32[38,128]{1,0:T(8,128)S(1)} collective-permute-done((f32[38,128]{1,0:T(8,128)S(1)}, f32[38,128]{1,0:T(8,128)S(1)}, u32[]{:S(2)}, u32[]{:S(2)}) %collective-permute-start.9) | collective-permute-done | bytes 19488 | tf_op jit(solution)/shard_map/filter_grad_sum/ppermute | solution.py:244
  105.0 2.7 %collective-permute-start.10 = (f32[38,128]{1,0:T(8,128)S(1)}, f32[38,128]{1,0:T(8,128)S(1)}, u32[]{:S(2)}, u32[]{:S(2)}) collective-permute-start(f32[38,128]{1,0:T(8,128)S(1)} %select_add_fusion.3), channel_id=1, source_target_pairs={{0,4},{1,5},{2,6},{3,7},{4,0},{5,1},{6,2},{7,3},{8,12},{9,13},{10,... | collective-permute-start | bytes 58376 | tf_op jit(solution)/shard_map/filter_grad_sum/ppermute | solution.py:244
  107.8 2.0 %collective-permute-done.10 = f32[38,128]{1,0:T(8,128)S(1)} collective-permute-done((f32[38,128]{1,0:T(8,128)S(1)}, f32[38,128]{1,0:T(8,128)S(1)}, u32[]{:S(2)}, u32[]{:S(2)}) %collective-permute-start.10) | collective-permute-done | bytes 19488 | tf_op jit(solution)/shard_map/filter_grad_sum/ppermute | solution.py:244
  109.8 1.7 %collective-permute-start.11 = (f32[76,128]{1,0:T(8,128)S(1)}, f32[76,128]{1,0:T(8,128)S(1)}, u32[]{:S(2)}, u32[]{:S(2)}) collective-permute-start(f32[76,128]{1,0:T(8,128)S(1)} %maximum_select_fusion.4), channel_id=1, source_target_pairs={{0,2},{1,3},{2,0},{3,1},{4,6},{5,7},{6,4},{7,5},{8,10},{9,11},{10,... | collective-permute-start | bytes 116744 | tf_op jit(solution)/shard_map/filter_grad_sum/ppermute | solution.py:244
  113.9 2.7 %collective-permute-start.12 = (f32[152,128]{1,0:T(8,128)S(1)}, f32[152,128]{1,0:T(8,128)S(1)}, u32[]{:S(2)}, u32[]{:S(2)}) collective-permute-start(f32[152,128]{1,0:T(8,128)S(1)} %maximum_select_fusion.3), channel_id=1, source_target_pairs={{0,16},{8,24},{16,0},{24,8},{1,17},{9,25},{17,1},{25,9},{2,18},{10... | collective-permute-start | bytes 233480 | tf_op jit(solution)/shard_map/filter_grad_sum/ppermute | solution.py:244
  116.6 2.3 %collective-permute-done.12 = f32[152,128]{1,0:T(8,128)S(1)} collective-permute-done((f32[152,128]{1,0:T(8,128)S(1)}, f32[152,128]{1,0:T(8,128)S(1)}, u32[]{:S(2)}, u32[]{:S(2)}) %collective-permute-start.12) | collective-permute-done | bytes 77856 | tf_op jit(solution)/shard_map/filter_grad_sum/ppermute | solution.py:244
  119.0 1.8 %collective-permute-start.13 = (f32[304,128]{1,0:T(8,128)S(1)}, f32[304,128]{1,0:T(8,128)S(1)}, u32[]{:S(2)}, u32[]{:S(2)}) collective-permute-start(f32[304,128]{1,0:T(8,128)S(1)} %maximum_select_fusion.2), channel_id=1, source_target_pairs={{0,8},{8,0},{16,24},{24,16},{1,9},{9,1},{17,25},{25,17},{2,10},{10... | collective-permute-start | bytes 466952 | tf_op jit(solution)/shard_map/filter_grad_sum/ppermute | solution.py:244
  120.8 2.0 %collective-permute-done.4 = f32[3,8,4096]{2,1,0:T(8,128)S(1)} collective-permute-done((f32[3,8,4096]{2,1,0:T(8,128)S(1)}, f32[3,8,4096]{2,1,0:T(8,128)S(1)}, u32[]{:S(2)}, u32[]{:S(2)}) %collective-permute-start.4) | collective-permute-done | bytes 393248 | tf_op jit(solution)/shard_map/ppermute | solution.py:20
  (64 shorter events, 18.0 us)
Async XLA Ops:
  2.5 23.2 %collective-permute-start = (bf16[3,8,4096]{2,1,0:T(8,128)(2,1)S(1)}, bf16[3,8,4096]{2,1,0:T(8,128)(2,1)S(1)}, u32[]{:S(2)}, u32[]{:S(2)}) collective-permute-start(bf16[3,8,4096]{2,1,0:T(8,128)(2,1)S(1)} %pad_maximum_fusion.1), channel_id=1, source_target_pairs={{0,8},{8,16},{16,24},{1,9},{9,17},{17,25},{2,10},{10,18},{18,26},{... | collective-permute-start | bytes 589832 | tf_op jit(solution)/shard_map/ppermute | solution.py:20
  25.7 2.5 %copy-start.2 = (bf16[3,8,4096]{2,1,0:T(8,128)(2,1)}, bf16[3,8,4096]{2,1,0:T(8,128)(2,1)S(1)}, u32[]{:S(2)}) copy-start(bf16[3,8,4096]{2,1,0:T(8,128)(2,1)S(1)} %collective-permute-done.rim_ref) | copy-start | bytes 589828
  25.8 2.5 %copy-start.3 = (f32[16,4096]{1,0:T(8,128)S(1)}, f32[16,4096]{1,0:T(8,128)}, u32[]{:S(2)}) copy-start(f32[16,4096]{1,0:T(8,128)} %get-tuple-element.18) | copy-start | bytes 786436
  25.8 2.5 %copy-start.4 = (f32[16,4096]{1,0:T(8,128)S(1)}, f32[16,4096]{1,0:T(8,128)}, u32[]{:S(2)}) copy-start(f32[16,4096]{1,0:T(8,128)} %get-tuple-element.17) | copy-start | bytes 786436
  27.6 8.6 %copy-start = (f32[16,4096]{1,0:T(8,128)S(1)}, f32[16,4096]{1,0:T(8,128)}, u32[]{:S(2)}) copy-start(f32[16,4096]{1,0:T(8,128)} %param.15) | copy-start | bytes 786436
  28.4 7.8 %collective-permute-start.1 = (f32[16,4096]{1,0:T(8,128)S(1)}, f32[16,4096]{1,0:T(8,128)S(1)}, u32[]{:S(2)}, u32[]{:S(2)}) collective-permute-start(f32[16,4096]{1,0:T(8,128)S(1)} %get-tuple-element.29), channel_id=1, source_target_pairs={{0,8},{8,0},{16,24},{24,16},{1,9},{9,1},{17,25},{25,17},{2,10},{10... | collective-permute-start | bytes 786440 | tf_op jit(solution)/shard_map/modal_state_scan/ppermute | solution.py:244
  36.3 8.8 %collective-permute-start.2 = (f32[16,4096]{1,0:T(8,128)S(1)}, f32[16,4096]{1,0:T(8,128)S(1)}, u32[]{:S(2)}, u32[]{:S(2)}) collective-permute-start(f32[16,4096]{1,0:T(8,128)S(1)} %add_select_fusion), channel_id=1, source_target_pairs={{8,24},{16,0},{9,25},{17,1},{10,26},{18,2},{11,27},{19,3},{12,28},... | collective-permute-start | bytes 786440 | tf_op jit(solution)/shard_map/modal_state_scan/ppermute | solution.py:257
  37.6 7.5 %collective-permute-start.3 = (f32[16,4096]{1,0:T(8,128)S(1)}, f32[16,4096]{1,0:T(8,128)S(1)}, u32[]{:S(2)}, u32[]{:S(2)}) collective-permute-start(f32[16,4096]{1,0:T(8,128)S(1)} %add_select_fusion), channel_id=1, source_target_pairs={{8,16},{16,8},{9,17},{17,9},{10,18},{18,10},{11,19},{19,11},{12,20... | collective-permute-start | bytes 786440 | tf_op jit(solution)/shard_map/modal_state_scan/ppermute | solution.py:258
  80.8 30.7 %copy-start.5 = (f32[3,8,4096]{2,1,0:T(8,128)S(1)}, f32[3,8,4096]{2,1,0:T(8,128)}, u32[]{:S(2)}) copy-start(f32[3,8,4096]{2,1,0:T(8,128)} %get-tuple-element.23) | copy-start | bytes 1179652
  80.8 1.7 %collective-permute-start.5 = (f32[608,128]{1,0:T(8,128)S(1)}, f32[608,128]{1,0:T(8,128)S(1)}, u32[]{:S(2)}, u32[]{:S(2)}) collective-permute-start(f32[608,128]{1,0:T(8,128)S(1)} %select_n.213), channel_id=1, source_target_pairs={{0,1},{1,0},{2,3},{3,2},{4,5},{5,4},{6,7},{7,6},{8,9},{9,8},{10,11... | collective-permute-start | bytes 933896 | tf_op jit(solution)/shard_map/filter_grad_sum/ppermute | solution.py:244
  80.9 42.0 %copy-start.1 = (f32[3,16,4096]{2,1,0:T(8,128)S(1)}, f32[3,16,4096]{2,1,0:T(8,128)}, u32[]{:S(2)}) copy-start(f32[3,16,4096]{2,1,0:T(8,128)} %get-tuple-element.22) | copy-start | bytes 2359300
  82.5 9.0 %collective-permute-start.6 = (f32[304,128]{1,0:T(8,128)S(1)}, f32[304,128]{1,0:T(8,128)S(1)}, u32[]{:S(2)}, u32[]{:S(2)}) collective-permute-start(f32[304,128]{1,0:T(8,128)S(1)} %slice_select_fusion.2), channel_id=1, source_target_pairs={{0,8},{8,0},{16,24},{24,16},{1,9},{9,1},{17,25},{25,17},{2,10},{10... | collective-permute-start | bytes 466952 | tf_op jit(solution)/shard_map/filter_grad_sum/ppermute | solution.py:244
  91.6 4.5 %collective-permute-start.7 = (f32[152,128]{1,0:T(8,128)S(1)}, f32[152,128]{1,0:T(8,128)S(1)}, u32[]{:S(2)}, u32[]{:S(2)}) collective-permute-start(f32[152,128]{1,0:T(8,128)S(1)} %slice_select_fusion.3), channel_id=1, source_target_pairs={{0,16},{8,24},{16,0},{24,8},{1,17},{9,25},{17,1},{25,9},{2,18},{10... | collective-permute-start | bytes 233480 | tf_op jit(solution)/shard_map/filter_grad_sum/ppermute | solution.py:244
  96.1 4.1 %collective-permute-start.8 = (f32[76,128]{1,0:T(8,128)S(1)}, f32[76,128]{1,0:T(8,128)S(1)}, u32[]{:S(2)}, u32[]{:S(2)}) collective-permute-start(f32[76,128]{1,0:T(8,128)S(1)} %slice_select_fusion.4), channel_id=1, source_target_pairs={{0,2},{1,3},{2,0},{3,1},{4,6},{5,7},{6,4},{7,5},{8,10},{9,11},{10,... | collective-permute-start | bytes 116744 | tf_op jit(solution)/shard_map/filter_grad_sum/ppermute | solution.py:244
  100.2 4.9 %collective-permute-start.9 = (f32[38,128]{1,0:T(8,128)S(1)}, f32[38,128]{1,0:T(8,128)S(1)}, u32[]{:S(2)}, u32[]{:S(2)}) collective-permute-start(f32[38,128]{1,0:T(8,128)S(1)} %slice_select_fusion.5), channel_id=1, source_target_pairs={{0,4},{1,5},{2,6},{3,7},{4,0},{5,1},{6,2},{7,3},{8,12},{9,13},{10,... | collective-permute-start | bytes 58376 | tf_op jit(solution)/shard_map/filter_grad_sum/ppermute | solution.py:244
  105.0 4.7 %collective-permute-start.10 = (f32[38,128]{1,0:T(8,128)S(1)}, f32[38,128]{1,0:T(8,128)S(1)}, u32[]{:S(2)}, u32[]{:S(2)}) collective-permute-start(f32[38,128]{1,0:T(8,128)S(1)} %select_add_fusion.3), channel_id=1, source_target_pairs={{0,4},{1,5},{2,6},{3,7},{4,0},{5,1},{6,2},{7,3},{8,12},{9,13},{10,... | collective-permute-start | bytes 58376 | tf_op jit(solution)/shard_map/filter_grad_sum/ppermute | solution.py:244
  109.8 4.1 %collective-permute-start.11 = (f32[76,128]{1,0:T(8,128)S(1)}, f32[76,128]{1,0:T(8,128)S(1)}, u32[]{:S(2)}, u32[]{:S(2)}) collective-permute-start(f32[76,128]{1,0:T(8,128)S(1)} %maximum_select_fusion.4), channel_id=1, source_target_pairs={{0,2},{1,3},{2,0},{3,1},{4,6},{5,7},{6,4},{7,5},{8,10},{9,11},{10,... | collective-permute-start | bytes 116744 | tf_op jit(solution)/shard_map/filter_grad_sum/ppermute | solution.py:244
  111.5 11.3 %collective-permute-start.4 = (f32[3,8,4096]{2,1,0:T(8,128)S(1)}, f32[3,8,4096]{2,1,0:T(8,128)S(1)}, u32[]{:S(2)}, u32[]{:S(2)}) collective-permute-start(f32[3,8,4096]{2,1,0:T(8,128)S(1)} %copy-done.5), channel_id=1, source_target_pairs={{8,0},{16,8},{24,16},{9,1},{17,9},{25,17},{10,2},{18,10},{26,18},{... | collective-permute-start | bytes 1179656 | tf_op jit(solution)/shard_map/ppermute | solution.py:20
  113.9 5.1 %collective-permute-start.12 = (f32[152,128]{1,0:T(8,128)S(1)}, f32[152,128]{1,0:T(8,128)S(1)}, u32[]{:S(2)}, u32[]{:S(2)}) collective-permute-start(f32[152,128]{1,0:T(8,128)S(1)} %maximum_select_fusion.3), channel_id=1, source_target_pairs={{0,16},{8,24},{16,0},{24,8},{1,17},{9,25},{17,1},{25,9},{2,18},{10... | collective-permute-start | bytes 233480 | tf_op jit(solution)/shard_map/filter_grad_sum/ppermute | solution.py:244
  119.0 5.5 %collective-permute-start.13 = (f32[304,128]{1,0:T(8,128)S(1)}, f32[304,128]{1,0:T(8,128)S(1)}, u32[]{:S(2)}, u32[]{:S(2)}) collective-permute-start(f32[304,128]{1,0:T(8,128)S(1)} %maximum_select_fusion.2), channel_id=1, source_target_pairs={{0,8},{8,0},{16,24},{24,16},{1,9},{9,1},{17,25},{25,17},{2,10},{10... | collective-permute-start | bytes 466952 | tf_op jit(solution)/shard_map/filter_grad_sum/ppermute | solution.py:244
  124.5 1.7 %collective-permute-start.14 = (f32[608,128]{1,0:T(8,128)S(1)}, f32[608,128]{1,0:T(8,128)S(1)}, u32[]{:S(2)}, u32[]{:S(2)}) collective-permute-start(f32[608,128]{1,0:T(8,128)S(1)} %maximum_select_fusion.1), channel_id=1, source_target_pairs={{0,1},{1,0},{2,3},{3,2},{4,5},{5,4},{6,7},{7,6},{8,9},{9,8},{10,11... | collective-permute-start | bytes 933896 | tf_op jit(solution)/shard_map/filter_grad_sum/ppermute | solution.py:244
